TPU v7x, 32 devices: a whole 2x2x4 slice. The times are simulated.
32 devices in a mesh: grp: 2 (over y), vec: 8 (over z, x), orb: 2 (over core).
Axes of the slice: x: 2, y: 2, z: 4, core: 2. Of those that a mesh axis runs over, the one named last changes fastest.
Arguments:
- vectors: bfloat16 [32, 1024, 1024], P(('grp', 'vec'), None, 'orb'), parts along dimension 0, may hold values from -6 to 6
- rotation: bfloat16 [2048, 1024], P(('grp', 'vec', 'orb')), parts along dimension 0, may hold values from -0.1875 to 0.1875
- active: int32 [32, 2], P(('grp', 'vec')), parts along dimension 0, may hold values from 0 to 7, all different within a row
- factors: bfloat16 [32, 256, 1024], P(('grp', 'vec'), None, 'orb'), parts along dimension 0, may hold values from -0.09375 to 0.09375
- owner: int32 [16], P('grp'), parts along dimension 0, may hold values from 0 to 7, each once
Outputs:
- fock_owned: float32 [2048, 1024], P(('grp', 'vec'), 'orb'), parts along dimension 0
There are 2 independent parts, one for each index of `grp`. A program takes and returns all parts, laid end to end along the dimension named above; each array names one. Nothing has to cross between parts.
Inputs may be any that keep to these rules, and one draw needn't show every extreme that they name: `active`: each row names 2 different orbital blocks. Each row group has exactly one owner.
All inputs are finite; a program needn't handle non-finite values.
Results may differ from a plain program's by a relative error of at most 0.004.
Values may be sent and summed in bfloat16 or wider, within the bound.
No kernel may reach another device: no remote copies, remote signals or barrier semaphores. Data moves between devices by JAX's collectives and lax.ppermute only.
A program may use at most 64 MiB of HBM per device.

v0:
```python
import jax
import jax.numpy as jnp
from jax import lax
from jax.sharding import PartitionSpec as P

B = 128


def per_device(vectors, rotation, active, factors, owner):
    whole = lax.all_gather(rotation, ("vec", "orb"), axis=0, tiled=True)
    count = vectors.shape[0]
    orbitals = whole.shape[0]
    blocks = orbitals // B
    half_rotated = jnp.einsum(
        "sp,gsr->gpr", whole, vectors, preferred_element_type=jnp.float32
    ).astype(jnp.bfloat16)
    table = whole.reshape(orbitals, blocks, B)
    picked = jnp.take(table, active, axis=1)
    picked = jnp.moveaxis(picked, 1, 0).reshape(count, orbitals, -1)
    summed = jnp.einsum(
        "gpr,grj->gpj",
        lax.all_gather(half_rotated, "orb", axis=2, tiled=True),
        picked,
        preferred_element_type=jnp.float32,
    )
    active_rotated = summed.astype(jnp.bfloat16)
    groups = owner.shape[0]
    group_rows = orbitals // groups
    partial_fock = jnp.einsum(
        "gpj,gjq->pq", active_rotated, factors, preferred_element_type=jnp.float32
    )
    ordered = partial_fock.reshape(groups, group_rows, -1)[owner].reshape(orbitals, -1)
    fock_owned = lax.psum_scatter(ordered, "vec", scatter_dimension=0, tiled=True)
    return fock_owned


def solution(mesh):
    placed = (
        P(("grp", "vec"), None, "orb"),
        P(("grp", "vec", "orb"), None),
        P(("grp", "vec"), None),
        P(("grp", "vec"), None, "orb"),
        P("grp"),
    )
    return jax.shard_map(
        per_device, mesh=mesh, in_specs=placed, out_specs=P(("grp", "vec"), "orb"), check_vma=False
    )
```

profile of v0, /device:TPU:0, one launch (start us, length us, event | category | flops | bytes accessed | tf_op | source)
XLA Modules:
  0.0 158.3 jit_solution(18372694688198548694)
XLA Ops:
  6.5 0.0 copy-start
  6.5 0.0 all-gather.3.cloned.1.call-start
  6.5 0.7 all-gather.3.cloned.1.call-update
  7.3 0.0 all-gather.5.cloned.1.call-start
  7.3 46.4 %all-gather.3.cloned.1.call-done = bf16[1024,1024]{1,0:T(8,128)(2,1)} async-done(((bf16[64,1024]{1,0:T(8,128)(2,1)}), bf16[1024,1024]{1,0:T(8,128)(2,1)}) %all-gather.3.cloned.1.call-update) | async-done | bytes 2097168 | tf_op jit(solution)/shard_map/all_gather | solution.py:10
  53.7 0.0 copy-done
  53.7 5.3 %convert_bitcast_fusion = bf16[2,1024,512]{1,2,0:T(8,128)(2,1)} fusion(bf16[2,1024,512]{2,1,0:T(8,128)(2,1)S(1)} %copy-done, bf16[1024,1024]{1,0:T(8,128)(2,1)} %all-gather.3.cloned.1.call-done), kind=kOutput, calls=%fused_computation.4 | convolution fusion | flops 2148532224 | bytes 6291456 | tf_op jit(solution)/shard_map/sp,gsr->gpr/dot_general | solution.py:14
  59.0 0.0 copy-start.1
  59.0 0.0 copy-start.2
  59.0 0.0 all-gather.5.cloned.1.call-update
  59.0 0.0 reduce-scatter.2.cloned.1.call-start
  59.1 0.6 copy-done.1
  59.7 0.1 reshape.23
  59.8 0.0 copy-done.2
  59.8 3.9 %copy.7 = bf16[1024,1024]{0,1:T(8,128)(2,1)} copy(bf16[1024,1024]{1,0:T(8,128)(2,1)} %all-gather.3.cloned.1.call-done) | data formatting | bytes 4194304 | tf_op jit(solution)/shard_map/all_gather | solution.py:10
  63.7 4.2 %copy.8 = bf16[1024,8,128]{2,0,1:T(8,128)(2,1)} copy(bf16[1024,8,128]{0,2,1:T(8,128)(2,1)} %bitcast.21) | data formatting | bytes 4194304 | tf_op jit(solution)/shard_map/reshape | solution.py:17
  67.9 3.9 %gather_fusion = bf16[4,1024,128]{2,1,0:T(8,128)(2,1)} fusion(bf16[1024,8,128]{2,0,1:T(8,128)(2,1)} %copy.8, s32[1024]{0:T(1024)S(1)} %pad_clamp_fusion.1), kind=kCustom, calls=%fused_computation | custom fusion | bytes 2097168 | tf_op jit(solution)/shard_map/jit(_take)/gather | solution.py:18
  71.8 1.5 copy.9
  73.3 1.2 broadcast_select_fusion
  74.4 0.0 all-gather.5.cloned.1.call-done
  74.4 5.9 %fusion.4 = f32[1024,512,1]{1,0,2:T(8,128)} fusion(bf16[2,256,512]{2,1,0:T(8,128)(2,1)} %param.8, bf16[2,1024,1024]{1,2,0:T(8,128)(2,1)} %all-gather.5.cloned.1.call-done, bf16[2,1024,256]{1,2,0:T(8,128)(2,1)} %bitcast.24), kind=kOutput, calls=%fused_computation.6 | convolution fusion | flops 1611137024 | bytes 7864320 | tf_op jit(solution)/shard_map/gpj,gjq->pq/dot_general | solution.py:29
  80.3 3.6 %gather_fusion.1 = f32[8,128,512]{2,1,0:T(8,128)} fusion(f32[8,128,512]{2,1,0:T(8,128)} %bitcast.23, s32[1024]{0:T(1024)S(1)} %pad_clamp_fusion), kind=kCustom, calls=%fused_computation.1 | custom fusion | bytes 4194336 | tf_op jit(solution)/shard_map/gather | solution.py:32
  84.0 0.0 reduce-scatter.2.cloned.1.call-update
  84.0 67.8 %reduce-scatter.2.cloned.1.call-done = f32[128,512]{1,0:T(8,128)} async-done(((f32[1024,512]{1,0:T(8,128)}), f32[128,512]{1,0:T(8,128)}) %reduce-scatter.2.cloned.1.call-update) | async-done | bytes 262160 | tf_op jit(solution)/shard_map/reduce_scatter | solution.py:33
  (5 shorter events, 0.0 us)
Async XLA Ops:
  6.5 47.2 %copy-start = (bf16[2,1024,512]{2,1,0:T(8,128)(2,1)S(1)}, bf16[2,1024,512]{2,1,0:T(8,128)(2,1)}, u32[]{:S(2)}) copy-start(bf16[2,1024,512]{2,1,0:T(8,128)(2,1)} %param.5) | copy-start | bytes 6291460
  6.5 47.2 %all-gather.3.cloned.1.call-start = ((), (), s32[]{:S(2)}) async-start(), calls=%async_computation.1 | async-start | bytes 2228224 | tf_op jit(solution)/shard_map/all_gather | solution.py:10
  7.3 67.2 %all-gather.5.cloned.1.call-start = ((), (), s32[]{:S(2)}) async-start(), calls=%async_computation.2 | async-start | bytes 6291456 | tf_op jit(solution)/shard_map/all_gather | solution.py:22
  59.0 0.7 copy-start.1
  59.0 0.8 copy-start.2
  59.0 92.7 %reduce-scatter.2.cloned.1.call-start = ((), (), s32[]{:S(2)}) async-start(), calls=%async_computation.3 | async-start | bytes 2359296 | tf_op jit(solution)/shard_map/reduce_scatter | solution.py:33
Sparse Core Ops, SparseCore 0:
  9.5 44.1 all-gather.2
  59.1 12.3 all-gather.4
  84.1 67.6 reduce-scatter.1
where the time goes:
time: 159 us; the launch traced here: 158 us
  waiting for transfers between devices  115 us (72%)
  local copies, waits for them, and re-layouts  17.7 us (11%)
  between operations  13.1 us (8%)
  matrix products  11.2 us (7%)
    reduce_scatter x1, waiting for transfers between devices, per_device(): lax.psum_scatter(ordered, 'vec', scatter_dimension=0, tiled=True)  67.8 us
    all_gather x1, waiting for transfers between devices, per_device(): whole = lax.all_gather(rotation, ('vec', 'orb'), axis=0, tiled=True)  46.4 us
    dot_general x1, matrix products, per_device(): jnp.einsum('gpj,gjq->pq', active_rotated, factors, preferred_element_type...  5.94 us
    gather x2, local copies, waits for them, and re-layouts, per_device(): picked = jnp.take(table, active, axis=1)  5.35 us
    dot_general x1, matrix products, per_device(): jnp.einsum('sp,gsr->gpr', whole, vectors, preferred_element_type=jnp.floa...  5.28 us
    reshape x1, local copies, waits for them, and re-layouts, per_device(): table = whole.reshape(orbitals, blocks, B)  4.16 us
    all_gather x1, local copies, waits for them, and re-layouts, per_device(): whole = lax.all_gather(rotation, ('vec', 'orb'), axis=0, tiled=True)  3.93 us
    gather x1, local copies, waits for them, and re-layouts, per_device(): partial_fock.reshape(groups, group_rows, -1)[owner].reshape(orbitals, -1)  3.61 us
  transfers between devices with their start and end apart: 3, of which 2 were waited for; matrix products, arithmetic and copies ran while one was open for 9% of the time, Pallas kernels for 0%

commit v1 on v0

v1 whole, which is shorter than its diff:
```python
import jax
import jax.numpy as jnp
import numpy as np
from jax import lax
from jax.sharding import PartitionSpec as P

B = 128
RING_MAX = 16


def ring_of(mesh):
    devs = mesh.devices
    n = devs.shape[1]
    coords = [getattr(devs[0, v, 0], "coords", None) for v in range(n)]
    if any(c is None for c in coords):
        return list(range(n))
    zs = sorted({c[2] for c in coords})
    xs = sorted({c[0] for c in coords})
    at = {(c[2], c[0]): v for v, c in enumerate(coords)}
    if len(at) != n or len(zs) * len(xs) != n or len(zs) % 2 or len(xs) < 2:
        return list(range(n))
    cycle = [(z, xs[0]) for z in zs]
    for i, z in enumerate(reversed(zs)):
        row = xs[1:] if i % 2 == 0 else xs[1:][::-1]
        cycle += [(z, x) for x in row]
    return [at[c] for c in cycle]


def swap_orb(x, axis):
    other = lax.ppermute(x, "orb", [(0, 1), (1, 0)])
    first = lax.axis_index("orb") == 0
    lo = jnp.where(first, x, other)
    hi = jnp.where(first, other, x)
    return jnp.concatenate([lo, hi], axis=axis)


def ring_all_gather(x, ring):
    n = len(ring)
    right = [(ring[i], ring[(i + 1) % n]) for i in range(n)]
    left = [(ring[i], ring[(i - 1) % n]) for i in range(n)]
    nr = n // 2
    nl = n - 1 - nr
    rb, lb = [], []
    cur = x
    for _ in range(nr):
        cur = lax.ppermute(cur, "vec", right)
        rb.append(cur)
    cur = x
    for _ in range(nl):
        cur = lax.ppermute(cur, "vec", left)
        lb.append(cur)
    stacked = jnp.stack([x] + lb + rb[::-1])
    pos_of = jnp.asarray(np.argsort(np.array(ring)).astype(np.int32))
    pos = pos_of[lax.axis_index("vec")]
    return jnp.take(stacked, (pos_of - pos) % n, axis=0)


def make(mesh):
    ring = ring_of(mesh)
    n = len(ring)
    use_ring = n <= RING_MAX

    def per_device(vectors, rotation, active, factors, owner):
        if use_ring:
            part = ring_all_gather(rotation, ring)
            whole = swap_orb(part, 1).reshape(-1, rotation.shape[1])
        else:
            whole = lax.all_gather(rotation, ("vec", "orb"), axis=0, tiled=True)
        orbitals = whole.shape[0]
        half_rotated = jnp.einsum(
            "sp,gsr->gpr", whole, vectors, preferred_element_type=jnp.float32
        ).astype(jnp.bfloat16)
        full_half = swap_orb(half_rotated, 2)

        columns = (active[:, :, None] * B + jnp.arange(B, dtype=jnp.int32)).reshape(
            active.shape[0], -1
        )
        onehot = (
            jnp.arange(orbitals, dtype=jnp.int32)[None, :, None] == columns[:, None, :]
        ).astype(jnp.bfloat16)
        picked = jnp.einsum(
            "rc,gcj->grj", whole, onehot, preferred_element_type=jnp.float32
        ).astype(jnp.bfloat16)

        active_rotated = jnp.einsum(
            "gpr,grj->gpj", full_half, picked, preferred_element_type=jnp.float32
        ).astype(jnp.bfloat16)

        groups = owner.shape[0]
        group_rows = orbitals // groups
        rows = (owner[:, None] * group_rows + jnp.arange(group_rows, dtype=jnp.int32)).reshape(-1)
        if not use_ring:
            ordered_ar = jnp.take(active_rotated, rows, axis=1)
            ordered = jnp.einsum(
                "gpj,gjq->pq", ordered_ar, factors, preferred_element_type=jnp.float32
            )
            return lax.psum_scatter(ordered, "vec", scatter_dimension=0, tiled=True)

        per = orbitals // n
        blocks = rows.reshape(n, per)
        ring_arr = jnp.asarray(np.array(ring, np.int32))
        pos_of = jnp.asarray(np.argsort(np.array(ring)).astype(np.int32))
        pos = pos_of[lax.axis_index("vec")]
        steps = jnp.arange(n, dtype=jnp.int32)
        rows_r = blocks[ring_arr[(pos - 1 - steps) % n]].reshape(-1)
        rows_l = blocks[ring_arr[(pos + 1 + steps) % n]].reshape(-1)
        cols = factors.shape[2] // 2
        part_r = jnp.einsum(
            "gpj,gjq->pq",
            jnp.take(active_rotated, rows_r, axis=1),
            factors[:, :, :cols],
            preferred_element_type=jnp.float32,
        ).reshape(n, per, cols)
        part_l = jnp.einsum(
            "gpj,gjq->pq",
            jnp.take(active_rotated, rows_l, axis=1),
            factors[:, :, cols:],
            preferred_element_type=jnp.float32,
        ).reshape(n, per, -1)
        right = [(ring[i], ring[(i + 1) % n]) for i in range(n)]
        left = [(ring[i], ring[(i - 1) % n]) for i in range(n)]
        acc_r = part_r[0]
        acc_l = part_l[0]
        for k in range(1, n):
            acc_r = lax.ppermute(acc_r, "vec", right) + part_r[k]
            acc_l = lax.ppermute(acc_l, "vec", left) + part_l[k]
        return jnp.concatenate([acc_r, acc_l], axis=1)

    return per_device


def solution(mesh):
    placed = (
        P(("grp", "vec"), None, "orb"),
        P(("grp", "vec", "orb"), None),
        P(("grp", "vec"), None),
        P(("grp", "vec"), None, "orb"),
        P("grp"),
    )
    return jax.shard_map(
        make(mesh), mesh=mesh, in_specs=placed, out_specs=P(("grp", "vec"), "orb"), check_vma=False
    )
```

time: 159 us -> 127 us (0.80)
  waiting for transfers between devices: 115 us -> 36.9 us
  starting transfers between devices: 0.08 us -> 23.2 us
  other arithmetic: 1.18 us -> 20 us
  local copies, waits for them, and re-layouts: 17.7 us -> 32.8 us
  between operations: 13.1 us -> 1.64 us
    reduce_scatter x1 -> x0, waiting for transfers between devices: 67.8 us -> none  [per_device(): lax.psum_scatter(ordered, 'vec', scatter_dimension=0, tiled=True)]
    all_gather x2 -> x0, waiting for transfers between devices: 46.4 us -> none  [the longest x1 46.4 us: per_device(): whole = lax.all_gather(rotation, ('vec', 'orb'), axis=0, tiled=True)]
    ppermute x0 -> x23, waiting for transfers between devices: none -> 36.9 us  [the longest x7 23 us: per_device(): acc_l = lax.ppermute(acc_l, 'vec', left) + part_l[k]]
    ppermute x0 -> x23, starting transfers between devices: none -> 23.2 us  [the longest x7 9.92 us: per_device(): acc_l = lax.ppermute(acc_l, 'vec', left) + part_l[k]]
    select_n x3 -> x9, other arithmetic: 1.16 us -> 18 us  [the longest x2 5.99 us: swap_orb(): lo = jnp.where(first, x, other)]
    gather x3 -> x7, local copies, waits for them, and re-layouts: 8.96 us -> 21.1 us  [the longest x1 8.46 us: per_device(): jnp.take(active_rotated, rows_l, axis=1)]
    unnamed x6 -> x26, local copies, waits for them, and re-layouts: 0.61 us -> 6.6 us
    reshape x1 -> x0, local copies, waits for them, and re-layouts: 4.16 us -> none  [per_device(): table = whole.reshape(orbitals, blocks, B)]
  transfers between devices with their start and end apart: 3 -> 23, of which waited for: 2 -> 12; matrix products, arithmetic and copies ran while one was open for 9% -> 19% of each run, Pallas kernels for 0% -> 0%
where the time goes in v1:
time: 127 us; the launch traced here: 126 us
  waiting for transfers between devices  36.9 us (29%)
  local copies, waits for them, and re-layouts  32.8 us (26%)
  starting transfers between devices  23.2 us (18%)
  other arithmetic  20 us (16%)
  matrix products  11.5 us (9%)
  between operations  1.64 us (1%)
    ppermute x7, waiting for transfers between devices, per_device(): acc_l = lax.ppermute(acc_l, 'vec', left) + part_l[k]  23 us
    ppermute x7, starting transfers between devices, per_device(): acc_l = lax.ppermute(acc_l, 'vec', left) + part_l[k]  9.92 us
    gather x1, local copies, waits for them, and re-layouts, per_device(): jnp.take(active_rotated, rows_l, axis=1)  8.46 us
    gather x1, local copies, waits for them, and re-layouts, per_device(): jnp.take(active_rotated, rows_r, axis=1)  8.44 us
    ppermute x4, waiting for transfers between devices, ring_all_gather(): cur = lax.ppermute(cur, 'vec', right)  8.37 us
    ppermute x3, starting transfers between devices, ring_all_gather(): cur = lax.ppermute(cur, 'vec', left)  6.79 us
    dot_general x1, matrix products, per_device(): jnp.einsum('gpr,grj->gpj', full_half, picked, preferred_element_type=jnp....  6.74 us
    unnamed x26, local copies, waits for them, and re-layouts  6.6 us
  transfers between devices with their start and end apart: 23, of which 12 were waited for; matrix products, arithmetic and copies ran while one was open for 19% of the time, Pallas kernels for 0%

profile of v1, /device:TPU:0, one launch (start us, length us, event | category | flops | bytes accessed | tf_op | source)
XLA Modules:
  0.0 126.1 jit_solution(5360117609471465368)
XLA Ops:
  0.0 3.0 %collective-permute-start = (bf16[64,1024]{1,0:T(8,128)(2,1)}, bf16[64,1024]{1,0:T(8,128)(2,1)S(1)}, u32[]{:S(2)}, u32[]{:S(2)}) collective-permute-start(bf16[64,1024]{1,0:T(8,128)(2,1)} %param.11), channel_id=1, source_target_pairs={{0,2},{4,0},{8,4},{12,8},{14,12},{10,14},{6,10},{2,6},{1,3},{5,1},... | collective-permute-start | bytes 393224 | tf_op jit(solution)/shard_map/ppermute | solution.py:50
  3.0 0.1 collective-permute-start.3
  3.1 1.6 %bitcast_dynamic-update-slice_fusion.7 = bf16[8,64,1024]{2,1,0:T(8,128)(2,1)} fusion(bf16[64,1024]{1,0:T(8,128)(2,1)} %param.11), kind=kLoop, calls=%fused_computation.55 | loop fusion | bytes 262144
  4.7 1.2 dynamic_slice.6
  5.9 1.3 %compare_and_fusion.2 = (pred[8]{0:T(512)(128)(4,1)S(1)}, s32[8]{0:T(128)S(1)}) fusion(s32[8]{0:T(128)} %constant.72.clone, s32[]{:T(128)} %bitcast.5), kind=kLoop, calls=%fused_computation.82 | loop fusion | flops 144 | bytes 76 | tf_op jit(solution)/shard_map/jit(_take)/and | solution.py:55
  7.3 1.9 %collective-permute-start.1 = (bf16[64,1024]{1,0:T(8,128)(2,1)S(1)}, bf16[64,1024]{1,0:T(8,128)(2,1)S(1)}, u32[]{:S(2)}, u32[]{:S(2)}) collective-permute-start(bf16[64,1024]{1,0:T(8,128)(2,1)S(1)} %collective-permute-done), channel_id=1, source_target_pairs={{0,2},{4,0},{8,4},{12,8},{14,12},{10,14},{6,10},{2,6},{1,3},{5,1},... | collective-permute-start | bytes 393224 | tf_op jit(solution)/shard_map/ppermute | solution.py:50
  9.2 0.2 collective-permute-start.4
  9.4 0.7 bitcast_dynamic-update-slice_fusion.6
  10.0 2.3 %collective-permute-done.1 = bf16[64,1024]{1,0:T(8,128)(2,1)S(1)} collective-permute-done((bf16[64,1024]{1,0:T(8,128)(2,1)S(1)}, bf16[64,1024]{1,0:T(8,128)(2,1)S(1)}, u32[]{:S(2)}, u32[]{:S(2)}) %collective-permute-start.1) | collective-permute-done | bytes 131104 | tf_op jit(solution)/shard_map/ppermute | solution.py:50
  12.3 1.9 %collective-permute-start.2 = (bf16[64,1024]{1,0:T(8,128)(2,1)S(1)}, bf16[64,1024]{1,0:T(8,128)(2,1)S(1)}, u32[]{:S(2)}, u32[]{:S(2)}) collective-permute-start(bf16[64,1024]{1,0:T(8,128)(2,1)S(1)} %collective-permute-done.1), channel_id=1, source_target_pairs={{0,2},{4,0},{8,4},{12,8},{14,12},{10,14},{6,10},{2,6},{1,3},{5,1},... | collective-permute-start | bytes 393224 | tf_op jit(solution)/shard_map/ppermute | solution.py:50
  14.2 0.2 collective-permute-start.5
  14.3 0.7 bitcast_dynamic-update-slice_fusion.5
  15.0 4.3 %collective-permute-done.5 = bf16[64,1024]{1,0:T(8,128)(2,1)S(1)} collective-permute-done((bf16[64,1024]{1,0:T(8,128)(2,1)S(1)}, bf16[64,1024]{1,0:T(8,128)(2,1)S(1)}, u32[]{:S(2)}, u32[]{:S(2)}) %collective-permute-start.5) | collective-permute-done | bytes 131104 | tf_op jit(solution)/shard_map/ppermute | solution.py:46
  19.3 0.2 collective-permute-start.6
  19.5 0.7 bitcast_dynamic-update-slice_fusion.4
  20.2 4.1 %collective-permute-done.6 = bf16[64,1024]{1,0:T(8,128)(2,1)S(1)} collective-permute-done((bf16[64,1024]{1,0:T(8,128)(2,1)S(1)}, bf16[64,1024]{1,0:T(8,128)(2,1)S(1)}, u32[]{:S(2)}, u32[]{:S(2)}) %collective-permute-start.6) | collective-permute-done | bytes 131104 | tf_op jit(solution)/shard_map/ppermute | solution.py:46
  24.2 0.7 bitcast_dynamic-update-slice_fusion.3
  24.9 0.6 bitcast_dynamic-update-slice_fusion.2
  25.5 0.7 bitcast_dynamic-update-slice_fusion.1
  26.2 0.7 bitcast_dynamic-update-slice_fusion
  26.9 1.9 %gather_fusion = bf16[8,64,1024]{2,1,0:T(8,128)(2,1)S(1)} fusion(bf16[8,64,1024]{2,1,0:T(8,128)(2,1)} %bitcast_dynamic-update-slice_fusion, s32[1024]{0:T(1024)S(1)} %pad_clamp_fusion.2), kind=kCustom, calls=%fused_computation.2 | custom fusion | bytes 2097184 | tf_op jit(solution)/shard_map/jit(_take)/gather | solution.py:55
  28.7 1.1 broadcast_select_fusion.4
  31.2 0.6 gather_fusion.1
  31.9 0.6 gather_fusion.3
  32.6 0.3 collective-permute-done.7
  32.9 1.4 %broadcast_select_fusion.6 = (bf16[8,64,1024]{2,1,0:T(8,128)(2,1)S(1)}, bf16[8,64,1024]{2,1,0:T(8,128)(2,1)S(1)}) fusion(bf16[8,64,1024]{2,1,0:T(8,128)(2,1)} %collective-permute-done.7, pred[]{:T(512)S(6)} %eq.21, bf16[8,64,1024]{2,1,0:T(8,128)(2,1)S(1)} %gather_fusion, pred[8]{0:T(512)(128)(4,1)S(1)} %get-tuple-element.6), kind=kLoop, calls=%fused_computation.30 | loop fusion | flops 1572864 | bytes 4194313 | tf_op jit(solution)/shard_map/jit(_where)/select_n | solution.py:32
  34.3 0.2 pad_maximum_fusion
  34.5 3.8 %convert_bitcast_fusion = bf16[2,1024,512]{1,2,0:T(8,128)(2,1)} fusion(bf16[1024,1024,1]{1,0,2:T(8,128)(2,1)S(1)} %bitcast.65, bf16[2,1024,512]{2,1,0:T(8,128)(2,1)S(1)} %copy-done), kind=kOutput, calls=%fused_computation.13 | convolution fusion | flops 2148532224 | bytes 6291456 | tf_op jit(solution)/shard_map/sp,gsr->gpr/dot_general | solution.py:70
  38.4 0.2 collective-permute-start.8
  38.6 0.6 gather_fusion.2
  39.2 0.6 gather_fusion.4
  39.9 2.9 %collective-permute-done.8 = bf16[2,1024,512]{1,2,0:T(8,128)(2,1)} collective-permute-done((bf16[2,1024,512]{1,2,0:T(8,128)(2,1)}, bf16[2,1024,512]{1,2,0:T(8,128)(2,1)}, u32[]{:S(2)}, u32[]{:S(2)}) %collective-permute-start.8) | collective-permute-done | bytes 2097184 | tf_op jit(solution)/shard_map/ppermute | solution.py:30
  42.9 4.6 %broadcast_select_fusion.3 = (bf16[2,1024,512]{1,2,0:T(8,128)(2,1)}, bf16[2,1024,512]{1,2,0:T(8,128)(2,1)}) fusion(bf16[2,1024,512]{1,2,0:T(8,128)(2,1)} %convert_bitcast_fusion, bf16[2,1024,512]{1,2,0:T(8,128)(2,1)} %collective-permute-done.8, pred[]{:T(512)S(6)} %eq.21), kind=kLoop, calls=%fused_computation.18 | loop fusion | flops 2097152 | bytes 8388609 | tf_op jit(solution)/shard_map/jit(_where)/select_n | solution.py:32
  47.4 6.7 %fusion.5 = bf16[2,1024,256]{2,1,0:T(8,128)(2,1)} fusion(bf16[2,1024,512]{1,2,0:T(8,128)(2,1)} %get-tuple-element.9, bf16[2,1024,512]{1,2,0:T(8,128)(2,1)} %get-tuple-element.8, bf16[1024,1024,1]{1,0,2:T(8,128)(2,1)} %bitcast.66, s32[2,256]{1,0:T(2,128)S(1)} %bitcast_add_fusion), kind=kOutput, calls=%fused_computation.19 | convolution fusion | flops 2157969408 | bytes 7342080 | tf_op jit(solution)/shard_map/gpr,grj->gpj/dot_general | solution.py:85
  54.2 2.3 %copy.16 = bf16[2,1024,256]{2,0,1:T(2,128)(2,1)S(1)} copy(bf16[2,1024,256]{2,1,0:T(8,128)(2,1)} %fusion.5) | data formatting | bytes 2097152 | tf_op jit(solution)/shard_map/convert_element_type | solution.py:87
  56.5 8.4 %gather_fusion.5 = bf16[1024,2,256]{2,1,0:T(2,128)(2,1)} fusion(bf16[2,1024,256]{2,0,1:T(2,128)(2,1)S(1)} %copy.16, s32[1024]{0:T(1024)S(1)} %fusion.18), kind=kCustom, calls=%fused_computation.clone | custom fusion | bytes 2101248 | tf_op jit(solution)/shard_map/jit(_take)/gather | solution.py:110
  64.9 5.4 %fusion.14 = bf16[2,1024,256]{2,0,1:T(2,128)(2,1)S(1)} fusion(bf16[1024,2,256]{2,1,0:T(2,128)(2,1)} %gather_fusion.5, pred[1024]{0:T(1024)(128)(4,1)S(1)} %compare_and_fusion.1), kind=kLoop, calls=%fused_computation.26 | loop fusion | flops 524288 | bytes 2098176 | tf_op jit(solution)/shard_map/jit(_take)/select_n | solution.py:110
  70.3 0.5 convolution_bitcast_fusion.1
  70.8 1.0 copy-done.2
  71.8 0.3 collective-permute-start.9
  72.1 8.5 %gather_fusion.6 = bf16[1024,2,256]{2,1,0:T(2,128)(2,1)} fusion(bf16[2,1024,256]{2,0,1:T(2,128)(2,1)S(1)} %copy.16, s32[1024]{0:T(1024)S(1)} %fusion.19), kind=kCustom, calls=%fused_computation.1.clone | custom fusion | bytes 2101248 | tf_op jit(solution)/shard_map/jit(_take)/gather | solution.py:116
  80.6 5.5 %fusion.15 = bf16[2,1024,256]{2,0,1:T(2,128)(2,1)S(1)} fusion(bf16[1024,2,256]{2,1,0:T(2,128)(2,1)} %gather_fusion.6, pred[1024]{0:T(1024)(128)(4,1)S(1)} %compare_and_fusion), kind=kLoop, calls=%fused_computation.27 | loop fusion | flops 524288 | bytes 2098176 | tf_op jit(solution)/shard_map/jit(_take)/select_n | solution.py:116
  86.1 0.5 convolution_bitcast_fusion
  86.6 1.8 %collective-permute-start.16 = (f32[128,256]{0,1:T(8,128)S(1)}, f32[128,256]{0,1:T(8,128)S(1)}, u32[]{:S(2)}, u32[]{:S(2)}) collective-permute-start(f32[128,256]{0,1:T(8,128)S(1)} %slice.110), channel_id=1, source_target_pairs={{0,2},{4,0},{8,4},{12,8},{14,12},{10,14},{6,10},{2,6},{1,3},{5,1},... | collective-permute-start | bytes 393224 | tf_op jit(solution)/shard_map/ppermute | solution.py:126
  88.4 0.8 collective-permute-start.10
  89.2 3.5 %collective-permute-done.16 = f32[128,256]{0,1:T(8,128)S(1)} collective-permute-done((f32[128,256]{0,1:T(8,128)S(1)}, f32[128,256]{0,1:T(8,128)S(1)}, u32[]{:S(2)}, u32[]{:S(2)}) %collective-permute-start.16) | collective-permute-done | bytes 131104 | tf_op jit(solution)/shard_map/ppermute | solution.py:126
  92.7 1.1 collective-permute-start.17
  93.9 1.0 collective-permute-start.11
  94.9 2.9 %collective-permute-done.17 = f32[128,256]{0,1:T(8,128)S(1)} collective-permute-done((f32[128,256]{0,1:T(8,128)S(1)}, f32[128,256]{0,1:T(8,128)S(1)}, u32[]{:S(2)}, u32[]{:S(2)}) %collective-permute-start.17) | collective-permute-done | bytes 131104 | tf_op jit(solution)/shard_map/ppermute | solution.py:126
  97.8 1.1 collective-permute-start.18
  98.9 1.0 collective-permute-start.12
  99.9 3.1 %collective-permute-done.18 = f32[128,256]{0,1:T(8,128)S(1)} collective-permute-done((f32[128,256]{0,1:T(8,128)S(1)}, f32[128,256]{0,1:T(8,128)S(1)}, u32[]{:S(2)}, u32[]{:S(2)}) %collective-permute-start.18) | collective-permute-done | bytes 131104 | tf_op jit(solution)/shard_map/ppermute | solution.py:126
  103.1 1.4 %collective-permute-start.19 = (f32[128,256]{0,1:T(8,128)S(1)}, f32[128,256]{0,1:T(8,128)S(1)}, u32[]{:S(2)}, u32[]{:S(2)}) collective-permute-start(f32[128,256]{0,1:T(8,128)S(1)} %slice_add_fusion.4), channel_id=1, source_target_pairs={{0,2},{4,0},{8,4},{12,8},{14,12},{10,14},{6,10},{2,6},{1,3},{5,1},... | collective-permute-start | bytes 393224 | tf_op jit(solution)/shard_map/ppermute | solution.py:126
  104.5 1.0 collective-permute-start.13
  105.5 3.7 %collective-permute-done.19 = f32[128,256]{0,1:T(8,128)S(1)} collective-permute-done((f32[128,256]{0,1:T(8,128)S(1)}, f32[128,256]{0,1:T(8,128)S(1)}, u32[]{:S(2)}, u32[]{:S(2)}) %collective-permute-start.19) | collective-permute-done | bytes 131104 | tf_op jit(solution)/shard_map/ppermute | solution.py:126
  109.2 1.7 %collective-permute-start.20 = (f32[128,256]{0,1:T(8,128)S(1)}, f32[128,256]{0,1:T(8,128)S(1)}, u32[]{:S(2)}, u32[]{:S(2)}) collective-permute-start(f32[128,256]{0,1:T(8,128)S(1)} %slice_add_fusion.3), channel_id=1, source_target_pairs={{0,2},{4,0},{8,4},{12,8},{14,12},{10,14},{6,10},{2,6},{1,3},{5,1},... | collective-permute-start | bytes 393224 | tf_op jit(solution)/shard_map/ppermute | solution.py:126
  111.0 0.7 collective-permute-start.14
  111.7 3.4 %collective-permute-done.20 = f32[128,256]{0,1:T(8,128)S(1)} collective-permute-done((f32[128,256]{0,1:T(8,128)S(1)}, f32[128,256]{0,1:T(8,128)S(1)}, u32[]{:S(2)}, u32[]{:S(2)}) %collective-permute-start.20) | collective-permute-done | bytes 131104 | tf_op jit(solution)/shard_map/ppermute | solution.py:126
  115.1 1.4 %collective-permute-start.21 = (f32[128,256]{0,1:T(8,128)S(1)}, f32[128,256]{0,1:T(8,128)S(1)}, u32[]{:S(2)}, u32[]{:S(2)}) collective-permute-start(f32[128,256]{0,1:T(8,128)S(1)} %slice_add_fusion.2), channel_id=1, source_target_pairs={{0,2},{4,0},{8,4},{12,8},{14,12},{10,14},{6,10},{2,6},{1,3},{5,1},... | collective-permute-start | bytes 393224 | tf_op jit(solution)/shard_map/ppermute | solution.py:126
  116.6 0.7 collective-permute-start.15
  117.3 2.9 %collective-permute-done.21 = f32[128,256]{0,1:T(8,128)S(1)} collective-permute-done((f32[128,256]{0,1:T(8,128)S(1)}, f32[128,256]{0,1:T(8,128)S(1)}, u32[]{:S(2)}, u32[]{:S(2)}) %collective-permute-start.21) | collective-permute-done | bytes 131104 | tf_op jit(solution)/shard_map/ppermute | solution.py:126
  120.2 1.4 %collective-permute-start.22 = (f32[128,256]{0,1:T(8,128)S(1)}, f32[128,256]{0,1:T(8,128)S(1)}, u32[]{:S(2)}, u32[]{:S(2)}) collective-permute-start(f32[128,256]{0,1:T(8,128)S(1)} %slice_add_fusion.1), channel_id=1, source_target_pairs={{0,2},{4,0},{8,4},{12,8},{14,12},{10,14},{6,10},{2,6},{1,3},{5,1},... | collective-permute-start | bytes 393224 | tf_op jit(solution)/shard_map/ppermute | solution.py:126
  121.6 3.6 %collective-permute-done.22 = f32[128,256]{0,1:T(8,128)S(1)} collective-permute-done((f32[128,256]{0,1:T(8,128)S(1)}, f32[128,256]{0,1:T(8,128)S(1)}, u32[]{:S(2)}, u32[]{:S(2)}) %collective-permute-start.22) | collective-permute-done | bytes 131104 | tf_op jit(solution)/shard_map/ppermute | solution.py:126
  125.3 0.8 copy.22
  (64 shorter events, 0.7 us)
Async XLA Ops:
  0.0 34.5 %copy-start = (bf16[2,1024,512]{2,1,0:T(8,128)(2,1)S(1)}, bf16[2,1024,512]{2,1,0:T(8,128)(2,1)}, u32[]{:S(2)}) copy-start(bf16[2,1024,512]{2,1,0:T(8,128)(2,1)} %param.10) | copy-start | bytes 6291460
  0.0 7.3 %collective-permute-start = (bf16[64,1024]{1,0:T(8,128)(2,1)}, bf16[64,1024]{1,0:T(8,128)(2,1)S(1)}, u32[]{:S(2)}, u32[]{:S(2)}) collective-permute-start(bf16[64,1024]{1,0:T(8,128)(2,1)} %param.11), channel_id=1, source_target_pairs={{0,2},{4,0},{8,4},{12,8},{14,12},{10,14},{6,10},{2,6},{1,3},{5,1},... | collective-permute-start | bytes 393224 | tf_op jit(solution)/shard_map/ppermute | solution.py:50
  3.0 6.2 %collective-permute-start.3 = (bf16[64,1024]{1,0:T(8,128)(2,1)}, bf16[64,1024]{1,0:T(8,128)(2,1)S(1)}, u32[]{:S(2)}, u32[]{:S(2)}) collective-permute-start(bf16[64,1024]{1,0:T(8,128)(2,1)} %param.11), channel_id=1, source_target_pairs={{0,4},{4,8},{8,12},{12,14},{14,10},{10,6},{6,2},{2,0},{1,5},{5,9},... | collective-permute-start | bytes 393224 | tf_op jit(solution)/shard_map/ppermute | solution.py:46
  7.3 5.0 %collective-permute-start.1 = (bf16[64,1024]{1,0:T(8,128)(2,1)S(1)}, bf16[64,1024]{1,0:T(8,128)(2,1)S(1)}, u32[]{:S(2)}, u32[]{:S(2)}) collective-permute-start(bf16[64,1024]{1,0:T(8,128)(2,1)S(1)} %collective-permute-done), channel_id=1, source_target_pairs={{0,2},{4,0},{8,4},{12,8},{14,12},{10,14},{6,10},{2,6},{1,3},{5,1},... | collective-permute-start | bytes 393224 | tf_op jit(solution)/shard_map/ppermute | solution.py:50
  9.2 5.0 %collective-permute-start.4 = (bf16[64,1024]{1,0:T(8,128)(2,1)S(1)}, bf16[64,1024]{1,0:T(8,128)(2,1)S(1)}, u32[]{:S(2)}, u32[]{:S(2)}) collective-permute-start(bf16[64,1024]{1,0:T(8,128)(2,1)S(1)} %collective-permute-done.3), channel_id=1, source_target_pairs={{0,4},{4,8},{8,12},{12,14},{14,10},{10,6},{6,2},{2,0},{1,5},{5,9},... | collective-permute-start | bytes 393224 | tf_op jit(solution)/shard_map/ppermute | solution.py:46
  12.3 7.2 %collective-permute-start.2 = (bf16[64,1024]{1,0:T(8,128)(2,1)S(1)}, bf16[64,1024]{1,0:T(8,128)(2,1)S(1)}, u32[]{:S(2)}, u32[]{:S(2)}) collective-permute-start(bf16[64,1024]{1,0:T(8,128)(2,1)S(1)} %collective-permute-done.1), channel_id=1, source_target_pairs={{0,2},{4,0},{8,4},{12,8},{14,12},{10,14},{6,10},{2,6},{1,3},{5,1},... | collective-permute-start | bytes 393224 | tf_op jit(solution)/shard_map/ppermute | solution.py:50
  14.2 5.1 %collective-permute-start.5 = (bf16[64,1024]{1,0:T(8,128)(2,1)S(1)}, bf16[64,1024]{1,0:T(8,128)(2,1)S(1)}, u32[]{:S(2)}, u32[]{:S(2)}) collective-permute-start(bf16[64,1024]{1,0:T(8,128)(2,1)S(1)} %collective-permute-done.4), channel_id=1, source_target_pairs={{0,4},{4,8},{8,12},{12,14},{14,10},{10,6},{6,2},{2,0},{1,5},{5,9},... | collective-permute-start | bytes 393224 | tf_op jit(solution)/shard_map/ppermute | solution.py:46
  19.3 5.0 %collective-permute-start.6 = (bf16[64,1024]{1,0:T(8,128)(2,1)S(1)}, bf16[64,1024]{1,0:T(8,128)(2,1)S(1)}, u32[]{:S(2)}, u32[]{:S(2)}) collective-permute-start(bf16[64,1024]{1,0:T(8,128)(2,1)S(1)} %collective-permute-done.5), channel_id=1, source_target_pairs={{0,4},{4,8},{8,12},{12,14},{14,10},{10,6},{6,2},{2,0},{1,5},{5,9},... | collective-permute-start | bytes 393224 | tf_op jit(solution)/shard_map/ppermute | solution.py:46
  26.9 4.3 %copy-start.1 = (s32[8]{0:T(128)S(1)}, s32[8]{0:T(128)}, u32[]{:S(2)}) copy-start(s32[8]{0:T(128)} %constant.73.clone) | copy-start | bytes 100
  29.9 3.0 %collective-permute-start.7 = (bf16[8,64,1024]{2,1,0:T(8,128)(2,1)}, bf16[8,64,1024]{2,1,0:T(8,128)(2,1)}, u32[]{:S(2)}, u32[]{:S(2)}) collective-permute-start(bf16[8,64,1024]{2,1,0:T(8,128)(2,1)} %broadcast_select_fusion.4), channel_id=1, source_target_pairs={{0,1},{1,0},{2,3},{3,2},{4,5},{5,4},{6,7},{7,6},{8,9},{9,8},{10,11... | collective-permute-start | bytes 3145736 | tf_op jit(solution)/shard_map/ppermute | solution.py:30
  34.5 3.9 %copy-start.4 = (bf16[8,128,1024]{2,1,0:T(8,128)(2,1)}, bf16[8,128,1024]{2,1,0:T(8,128)(2,1)S(1)}, u32[]{:S(2)}) copy-start(bf16[8,128,1024]{2,1,0:T(8,128)(2,1)S(1)} %pad_maximum_fusion) | copy-start | bytes 6291460
  34.5 4.1 %copy-start.8 = (s32[8]{0:T(128)S(1)}, s32[8]{0:T(128)}, u32[]{:S(2)}) copy-start(s32[8]{0:T(128)} %param.14) | copy-start | bytes 100
  34.5 5.3 %copy-start.7 = (s32[2,2]{1,0:T(2,128)S(1)}, s32[2,2]{1,0:T(2,128)}, u32[]{:S(2)}) copy-start(s32[2,2]{1,0:T(2,128)} %param.12) | copy-start | bytes 52
  38.4 4.5 %collective-permute-start.8 = (bf16[2,1024,512]{1,2,0:T(8,128)(2,1)}, bf16[2,1024,512]{1,2,0:T(8,128)(2,1)}, u32[]{:S(2)}, u32[]{:S(2)}) collective-permute-start(bf16[2,1024,512]{1,2,0:T(8,128)(2,1)} %convert_bitcast_fusion), channel_id=1, source_target_pairs={{0,1},{1,0},{2,3},{3,2},{4,5},{5,4},{6,7},{7,6},{8,9},{9,8},{10,11... | collective-permute-start | bytes 6291464 | tf_op jit(solution)/shard_map/ppermute | solution.py:30
  64.9 5.4 %copy-start.5 = (bf16[2,256,512]{2,1,0:T(8,128)(2,1)S(1)}, bf16[2,256,512]{2,1,0:T(8,128)(2,1)}, u32[]{:S(2)}) copy-start(bf16[2,256,512]{2,1,0:T(8,128)(2,1)} %param.13) | copy-start | bytes 1572868
  70.8 1.0 copy-start.2
  71.8 16.6 %collective-permute-start.9 = (f32[128,256]{0,1:T(8,128)S(1)}, f32[128,256]{0,1:T(8,128)S(1)}, u32[]{:S(2)}, u32[]{:S(2)}) collective-permute-start(f32[128,256]{0,1:T(8,128)S(1)} %slice.102), channel_id=1, source_target_pairs={{0,4},{4,8},{8,12},{12,14},{14,10},{10,6},{6,2},{2,0},{1,5},{5,9},... | collective-permute-start | bytes 393224 | tf_op jit(solution)/shard_map/ppermute | solution.py:125
  80.6 5.5 %copy-start.6 = (bf16[2,256,512]{2,1,0:T(8,128)(2,1)S(1)}, bf16[2,256,512]{2,1,0:T(8,128)(2,1)}, u32[]{:S(2)}) copy-start(bf16[2,256,512]{2,1,0:T(8,128)(2,1)} %param.13) | copy-start | bytes 1572868
  80.6 7.8 %copy-start.3 = (f32[1024,256]{0,1:T(8,128)S(1)}, f32[1024,256]{0,1:T(8,128)}, u32[]{:S(2)}) copy-start(f32[1024,256]{0,1:T(8,128)} %copy-done.2) | copy-start | bytes 3145732
  86.6 6.1 %collective-permute-start.16 = (f32[128,256]{0,1:T(8,128)S(1)}, f32[128,256]{0,1:T(8,128)S(1)}, u32[]{:S(2)}, u32[]{:S(2)}) collective-permute-start(f32[128,256]{0,1:T(8,128)S(1)} %slice.110), channel_id=1, source_target_pairs={{0,2},{4,0},{8,4},{12,8},{14,12},{10,14},{6,10},{2,6},{1,3},{5,1},... | collective-permute-start | bytes 393224 | tf_op jit(solution)/shard_map/ppermute | solution.py:126
  88.4 5.4 %collective-permute-start.10 = (f32[128,256]{0,1:T(8,128)S(1)}, f32[128,256]{0,1:T(8,128)S(1)}, u32[]{:S(2)}, u32[]{:S(2)}) collective-permute-start(f32[128,256]{0,1:T(8,128)S(1)} %slice_add_fusion.13), channel_id=1, source_target_pairs={{0,4},{4,8},{8,12},{12,14},{14,10},{10,6},{6,2},{2,0},{1,5},{5,9},... | collective-permute-start | bytes 393224 | tf_op jit(solution)/shard_map/ppermute | solution.py:125
  92.7 5.0 %collective-permute-start.17 = (f32[128,256]{0,1:T(8,128)S(1)}, f32[128,256]{0,1:T(8,128)S(1)}, u32[]{:S(2)}, u32[]{:S(2)}) collective-permute-start(f32[128,256]{0,1:T(8,128)S(1)} %slice_add_fusion.6), channel_id=1, source_target_pairs={{0,2},{4,0},{8,4},{12,8},{14,12},{10,14},{6,10},{2,6},{1,3},{5,1},... | collective-permute-start | bytes 393224 | tf_op jit(solution)/shard_map/ppermute | solution.py:126
  93.9 5.0 %collective-permute-start.11 = (f32[128,256]{0,1:T(8,128)S(1)}, f32[128,256]{0,1:T(8,128)S(1)}, u32[]{:S(2)}, u32[]{:S(2)}) collective-permute-start(f32[128,256]{0,1:T(8,128)S(1)} %slice_add_fusion.12), channel_id=1, source_target_pairs={{0,4},{4,8},{8,12},{12,14},{14,10},{10,6},{6,2},{2,0},{1,5},{5,9},... | collective-permute-start | bytes 393224 | tf_op jit(solution)/shard_map/ppermute | solution.py:125
  97.8 5.3 %collective-permute-start.18 = (f32[128,256]{0,1:T(8,128)S(1)}, f32[128,256]{0,1:T(8,128)S(1)}, u32[]{:S(2)}, u32[]{:S(2)}) collective-permute-start(f32[128,256]{0,1:T(8,128)S(1)} %slice_add_fusion.5), channel_id=1, source_target_pairs={{0,2},{4,0},{8,4},{12,8},{14,12},{10,14},{6,10},{2,6},{1,3},{5,1},... | collective-permute-start | bytes 393224 | tf_op jit(solution)/shard_map/ppermute | solution.py:126
  98.9 5.6 %collective-permute-start.12 = (f32[128,256]{0,1:T(8,128)S(1)}, f32[128,256]{0,1:T(8,128)S(1)}, u32[]{:S(2)}, u32[]{:S(2)}) collective-permute-start(f32[128,256]{0,1:T(8,128)S(1)} %slice_add_fusion.11), channel_id=1, source_target_pairs={{0,4},{4,8},{8,12},{12,14},{14,10},{10,6},{6,2},{2,0},{1,5},{5,9},... | collective-permute-start | bytes 393224 | tf_op jit(solution)/shard_map/ppermute | solution.py:125
  103.1 6.1 %collective-permute-start.19 = (f32[128,256]{0,1:T(8,128)S(1)}, f32[128,256]{0,1:T(8,128)S(1)}, u32[]{:S(2)}, u32[]{:S(2)}) collective-permute-start(f32[128,256]{0,1:T(8,128)S(1)} %slice_add_fusion.4), channel_id=1, source_target_pairs={{0,2},{4,0},{8,4},{12,8},{14,12},{10,14},{6,10},{2,6},{1,3},{5,1},... | collective-permute-start | bytes 393224 | tf_op jit(solution)/shard_map/ppermute | solution.py:126
  104.5 6.4 %collective-permute-start.13 = (f32[128,256]{0,1:T(8,128)S(1)}, f32[128,256]{0,1:T(8,128)S(1)}, u32[]{:S(2)}, u32[]{:S(2)}) collective-permute-start(f32[128,256]{0,1:T(8,128)S(1)} %slice_add_fusion.10), channel_id=1, source_target_pairs={{0,4},{4,8},{8,12},{12,14},{14,10},{10,6},{6,2},{2,0},{1,5},{5,9},... | collective-permute-start | bytes 393224 | tf_op jit(solution)/shard_map/ppermute | solution.py:125
  109.2 5.9 %collective-permute-start.20 = (f32[128,256]{0,1:T(8,128)S(1)}, f32[128,256]{0,1:T(8,128)S(1)}, u32[]{:S(2)}, u32[]{:S(2)}) collective-permute-start(f32[128,256]{0,1:T(8,128)S(1)} %slice_add_fusion.3), channel_id=1, source_target_pairs={{0,2},{4,0},{8,4},{12,8},{14,12},{10,14},{6,10},{2,6},{1,3},{5,1},... | collective-permute-start | bytes 393224 | tf_op jit(solution)/shard_map/ppermute | solution.py:126
  111.0 5.6 %collective-permute-start.14 = (f32[128,256]{0,1:T(8,128)S(1)}, f32[128,256]{0,1:T(8,128)S(1)}, u32[]{:S(2)}, u32[]{:S(2)}) collective-permute-start(f32[128,256]{0,1:T(8,128)S(1)} %slice_add_fusion.9), channel_id=1, source_target_pairs={{0,4},{4,8},{8,12},{12,14},{14,10},{10,6},{6,2},{2,0},{1,5},{5,9},... | collective-permute-start | bytes 393224 | tf_op jit(solution)/shard_map/ppermute | solution.py:125
  115.1 5.0 %collective-permute-start.21 = (f32[128,256]{0,1:T(8,128)S(1)}, f32[128,256]{0,1:T(8,128)S(1)}, u32[]{:S(2)}, u32[]{:S(2)}) collective-permute-start(f32[128,256]{0,1:T(8,128)S(1)} %slice_add_fusion.2), channel_id=1, source_target_pairs={{0,2},{4,0},{8,4},{12,8},{14,12},{10,14},{6,10},{2,6},{1,3},{5,1},... | collective-permute-start | bytes 393224 | tf_op jit(solution)/shard_map/ppermute | solution.py:126
  116.6 5.0 %collective-permute-start.15 = (f32[128,256]{0,1:T(8,128)S(1)}, f32[128,256]{0,1:T(8,128)S(1)}, u32[]{:S(2)}, u32[]{:S(2)}) collective-permute-start(f32[128,256]{0,1:T(8,128)S(1)} %slice_add_fusion.8), channel_id=1, source_target_pairs={{0,4},{4,8},{8,12},{12,14},{14,10},{10,6},{6,2},{2,0},{1,5},{5,9},... | collective-permute-start | bytes 393224 | tf_op jit(solution)/shard_map/ppermute | solution.py:125
  120.2 5.0 %collective-permute-start.22 = (f32[128,256]{0,1:T(8,128)S(1)}, f32[128,256]{0,1:T(8,128)S(1)}, u32[]{:S(2)}, u32[]{:S(2)}) collective-permute-start(f32[128,256]{0,1:T(8,128)S(1)} %slice_add_fusion.1), channel_id=1, source_target_pairs={{0,2},{4,0},{8,4},{12,8},{14,12},{10,14},{6,10},{2,6},{1,3},{5,1},... | collective-permute-start | bytes 393224 | tf_op jit(solution)/shard_map/ppermute | solution.py:126

commit v2 on v1

--- a/solution.py
+++ b/solution.py
@@ -52,7 +52,7 @@
     stacked = jnp.stack([x] + lb + rb[::-1])
     pos_of = jnp.asarray(np.argsort(np.array(ring)).astype(np.int32))
     pos = pos_of[lax.axis_index("vec")]
-    return jnp.take(stacked, (pos_of - pos) % n, axis=0)
+    return jnp.take(stacked, (pos_of - pos) % n, axis=0, mode="clip")
 
 
 def make(mesh):
@@ -70,7 +70,7 @@
         half_rotated = jnp.einsum(
             "sp,gsr->gpr", whole, vectors, preferred_element_type=jnp.float32
         ).astype(jnp.bfloat16)
-        full_half = swap_orb(half_rotated, 2)
+        other_half = lax.ppermute(half_rotated, "orb", [(0, 1), (1, 0)])
 
         columns = (active[:, :, None] * B + jnp.arange(B, dtype=jnp.int32)).reshape(
             active.shape[0], -1
@@ -81,9 +81,14 @@
         picked = jnp.einsum(
             "rc,gcj->grj", whole, onehot, preferred_element_type=jnp.float32
         ).astype(jnp.bfloat16)
-
-        active_rotated = jnp.einsum(
-            "gpr,grj->gpj", full_half, picked, preferred_element_type=jnp.float32
+        width = vectors.shape[2]
+        first = lax.axis_index("orb") == 0
+        lo, hi = picked[:, :width], picked[:, width:]
+        mine = jnp.where(first, lo, hi)
+        theirs = jnp.where(first, hi, lo)
+        active_rotated = (
+            jnp.einsum("gpr,grj->gpj", half_rotated, mine, preferred_element_type=jnp.float32)
+            + jnp.einsum("gpr,grj->gpj", other_half, theirs, preferred_element_type=jnp.float32)
         ).astype(jnp.bfloat16)
 
         groups = owner.shape[0]
@@ -97,23 +102,28 @@
             return lax.psum_scatter(ordered, "vec", scatter_dimension=0, tiled=True)
 
         per = orbitals // n
-        blocks = rows.reshape(n, per)
+        held = owner.reshape(n, -1)
         ring_arr = jnp.asarray(np.array(ring, np.int32))
         pos_of = jnp.asarray(np.argsort(np.array(ring)).astype(np.int32))
         pos = pos_of[lax.axis_index("vec")]
         steps = jnp.arange(n, dtype=jnp.int32)
-        rows_r = blocks[ring_arr[(pos - 1 - steps) % n]].reshape(-1)
-        rows_l = blocks[ring_arr[(pos + 1 + steps) % n]].reshape(-1)
+        by_group = active_rotated.reshape(active_rotated.shape[0], groups, group_rows, -1)
+
+        def in_step_order(order):
+            picked_groups = held[ring_arr[order % n]].reshape(-1)
+            taken = jnp.take(by_group, picked_groups, axis=1, mode="clip")
+            return taken.reshape(active_rotated.shape)
+
         cols = factors.shape[2] // 2
         part_r = jnp.einsum(
             "gpj,gjq->pq",
-            jnp.take(active_rotated, rows_r, axis=1),
+            in_step_order(pos - 1 - steps),
             factors[:, :, :cols],
             preferred_element_type=jnp.float32,
         ).reshape(n, per, cols)
         part_l = jnp.einsum(
             "gpj,gjq->pq",
-            jnp.take(active_rotated, rows_l, axis=1),
+            in_step_order(pos + 1 + steps),
             factors[:, :, cols:],
             preferred_element_type=jnp.float32,
         ).reshape(n, per, -1)

time: 127 us -> 95 us (0.75)
  other arithmetic: 20 us -> 3.32 us
  local copies, waits for them, and re-layouts: 32.8 us -> 19.7 us
  waiting for transfers between devices: 36.9 us -> 34.6 us
    gather x7 -> x9, local copies, waits for them, and re-layouts: 21.1 us -> 10.3 us  [the longest x4 5.93 us: in_step_order(): taken = jnp.take(by_group, picked_groups, axis=1, mode='clip')]
    select_n x7 -> x5, other arithmetic: 12 us -> 1.34 us  [the longest x1 1.31 us: ring_all_gather(): return jnp.take(stacked, (pos_of - pos) % n, axis=0, mode='clip')]
    select_n x2 -> x1, other arithmetic: 5.99 us -> 1.36 us  [swap_orb(): lo = jnp.where(first, x, other)]
    ppermute x2 -> x1, waiting for transfers between devices: 3.25 us -> 0.76 us  [swap_orb(): other = lax.ppermute(x, 'orb', [(0, 1), (1, 0)])]
    convert_element_type x1 -> x0, local copies, waits for them, and re-layouts: 2.3 us -> none  [per_device(): active_rotated = jnp.einsum('gpr,grj->gpj', full_half, picked, preferred_...]
    and x3 -> x0, other arithmetic: 1.33 us -> none  [the longest x1 1.31 us: ring_all_gather(): return jnp.take(stacked, (pos_of - pos) % n, axis=0)]
    dot_general x3 -> x5, matrix products: 7.7 us -> 8.51 us  [the longest x1 2.88 us: per_device(): jnp.einsum('rc,gcj->grj', whole, onehot, preferred_element_type=jnp.float32)]
  transfers between devices with their start and end apart: 23 -> 23, of which waited for: 12 -> 13; matrix products, arithmetic and copies ran while one was open for 19% -> 19% of each run, Pallas kernels for 0% -> 0%
where the time goes in v2:
time: 95 us; the launch traced here: 94.6 us
  waiting for transfers between devices  34.6 us (36%)
  starting transfers between devices  23 us (24%)
  local copies, waits for them, and re-layouts  19.7 us (21%)
  matrix products  12.3 us (13%)
  other arithmetic  3.32 us (3%)
  between operations  1.62 us (2%)
    ppermute x7, waiting for transfers between devices, per_device(): acc_l = lax.ppermute(acc_l, 'vec', left) + part_l[k]  22.8 us
    ppermute x7, starting transfers between devices, per_device(): acc_l = lax.ppermute(acc_l, 'vec', left) + part_l[k]  9.75 us
    ppermute x4, waiting for transfers between devices, ring_all_gather(): cur = lax.ppermute(cur, 'vec', right)  8.36 us
    ppermute x3, starting transfers between devices, ring_all_gather(): cur = lax.ppermute(cur, 'vec', left)  6.78 us
    unnamed x26, local copies, waits for them, and re-layouts  6.62 us
    gather x4, local copies, waits for them, and re-layouts, in_step_order(): taken = jnp.take(by_group, picked_groups, axis=1, mode='clip')  5.93 us
    ppermute x7, starting transfers between devices, per_device(): acc_r = lax.ppermute(acc_r, 'vec', right) + part_r[k]  5.62 us
    dot_general x1, matrix products, per_device(): jnp.einsum('sp,gsr->gpr', whole, vectors, preferred_element_type=jnp.floa...  3.8 us
  transfers between devices with their start and end apart: 23, of which 13 were waited for; matrix products, arithmetic and copies ran while one was open for 19% of the time, Pallas kernels for 0%

profile of v2, /device:TPU:0, one launch (start us, length us, event | category | flops | bytes accessed | tf_op | source)
XLA Modules:
  0.0 94.6 jit_solution(7086915316380791154)
XLA Ops:
  0.0 3.0 %collective-permute-start = (bf16[64,1024]{1,0:T(8,128)(2,1)}, bf16[64,1024]{1,0:T(8,128)(2,1)S(1)}, u32[]{:S(2)}, u32[]{:S(2)}) collective-permute-start(bf16[64,1024]{1,0:T(8,128)(2,1)} %param.9), channel_id=1, source_target_pairs={{0,2},{4,0},{8,4},{12,8},{14,12},{10,14},{6,10},{2,6},{1,3},{5,1},... | collective-permute-start | bytes 393224 | tf_op jit(solution)/shard_map/ppermute | solution.py:50
  3.0 0.1 collective-permute-start.3
  3.1 1.6 %bitcast_dynamic-update-slice_fusion.7 = bf16[8,64,1024]{2,1,0:T(8,128)(2,1)} fusion(bf16[64,1024]{1,0:T(8,128)(2,1)} %param.9), kind=kLoop, calls=%fused_computation.52 | loop fusion | bytes 262144
  4.7 1.2 %dynamic_slice.6 = s32[1]{0:T(128)} dynamic-slice(s32[8]{0:T(128)} %constant.48.clone, s32[]{:T(128)S(6)} %select_n.98), dynamic_slice_sizes={1} | dynamic-slice | bytes 12 | tf_op jit(solution)/shard_map/dynamic_slice | solution.py:54
  6.0 1.3 %and_select_fusion.2 = s32[8]{0:T(128)S(1)} fusion(s32[8]{0:T(128)} %constant.48.clone, s32[]{:T(128)} %bitcast.8), kind=kLoop, calls=%fused_computation.73 | loop fusion | flops 96 | bytes 68 | tf_op jit(solution)/shard_map/jit(remainder)/select_n | solution.py:55
  7.3 1.9 %collective-permute-start.1 = (bf16[64,1024]{1,0:T(8,128)(2,1)S(1)}, bf16[64,1024]{1,0:T(8,128)(2,1)S(1)}, u32[]{:S(2)}, u32[]{:S(2)}) collective-permute-start(bf16[64,1024]{1,0:T(8,128)(2,1)S(1)} %collective-permute-done), channel_id=1, source_target_pairs={{0,2},{4,0},{8,4},{12,8},{14,12},{10,14},{6,10},{2,6},{1,3},{5,1},... | collective-permute-start | bytes 393224 | tf_op jit(solution)/shard_map/ppermute | solution.py:50
  9.2 0.2 collective-permute-start.4
  9.4 0.7 bitcast_dynamic-update-slice_fusion.6
  10.0 2.3 %collective-permute-done.1 = bf16[64,1024]{1,0:T(8,128)(2,1)S(1)} collective-permute-done((bf16[64,1024]{1,0:T(8,128)(2,1)S(1)}, bf16[64,1024]{1,0:T(8,128)(2,1)S(1)}, u32[]{:S(2)}, u32[]{:S(2)}) %collective-permute-start.1) | collective-permute-done | bytes 131104 | tf_op jit(solution)/shard_map/ppermute | solution.py:50
  12.3 1.9 %collective-permute-start.2 = (bf16[64,1024]{1,0:T(8,128)(2,1)S(1)}, bf16[64,1024]{1,0:T(8,128)(2,1)S(1)}, u32[]{:S(2)}, u32[]{:S(2)}) collective-permute-start(bf16[64,1024]{1,0:T(8,128)(2,1)S(1)} %collective-permute-done.1), channel_id=1, source_target_pairs={{0,2},{4,0},{8,4},{12,8},{14,12},{10,14},{6,10},{2,6},{1,3},{5,1},... | collective-permute-start | bytes 393224 | tf_op jit(solution)/shard_map/ppermute | solution.py:50
  14.2 0.2 collective-permute-start.5
  14.3 0.7 bitcast_dynamic-update-slice_fusion.5
  15.0 4.3 %collective-permute-done.5 = bf16[64,1024]{1,0:T(8,128)(2,1)S(1)} collective-permute-done((bf16[64,1024]{1,0:T(8,128)(2,1)S(1)}, bf16[64,1024]{1,0:T(8,128)(2,1)S(1)}, u32[]{:S(2)}, u32[]{:S(2)}) %collective-permute-start.5) | collective-permute-done | bytes 131104 | tf_op jit(solution)/shard_map/ppermute | solution.py:46
  19.3 0.2 collective-permute-start.6
  19.5 0.7 bitcast_dynamic-update-slice_fusion.4
  20.2 4.1 %collective-permute-done.6 = bf16[64,1024]{1,0:T(8,128)(2,1)S(1)} collective-permute-done((bf16[64,1024]{1,0:T(8,128)(2,1)S(1)}, bf16[64,1024]{1,0:T(8,128)(2,1)S(1)}, u32[]{:S(2)}, u32[]{:S(2)}) %collective-permute-start.6) | collective-permute-done | bytes 131104 | tf_op jit(solution)/shard_map/ppermute | solution.py:46
  24.2 0.7 bitcast_dynamic-update-slice_fusion.3
  24.9 0.7 bitcast_dynamic-update-slice_fusion.2
  25.6 0.7 bitcast_dynamic-update-slice_fusion.1
  26.2 0.7 bitcast_dynamic-update-slice_fusion
  26.9 1.8 %gather_fusion = bf16[8,64,1024]{2,1,0:T(8,128)(2,1)S(1)} fusion(bf16[8,64,1024]{2,1,0:T(8,128)(2,1)} %bitcast_dynamic-update-slice_fusion, s32[1024]{0:T(1024)S(1)} %pad_clamp_fusion.6), kind=kCustom, calls=%fused_computation | custom fusion | bytes 2097184 | tf_op jit(solution)/shard_map/jit(_take)/gather | solution.py:55
  30.1 0.6 gather_fusion.1
  30.8 0.8 collective-permute-done.7
  31.6 1.4 %broadcast_select_fusion.1 = (bf16[8,64,1024]{2,1,0:T(8,128)(2,1)S(1)}, bf16[8,64,1024]{2,1,0:T(8,128)(2,1)S(1)}) fusion(bf16[8,64,1024]{2,1,0:T(8,128)(2,1)S(1)} %gather_fusion, bf16[8,64,1024]{2,1,0:T(8,128)(2,1)} %collective-permute-done.7, pred[]{:T(512)S(6)} %eq.21), kind=kLoop, calls=%fused_computation.18 | loop fusion | flops 1048576 | bytes 4194305 | tf_op jit(solution)/shard_map/jit(_where)/select_n | solution.py:32
  33.0 0.2 pad_maximum_fusion
  33.2 3.8 %convert_bitcast_fusion = bf16[2,1024,512]{2,1,0:T(8,128)(2,1)} fusion(bf16[1024,1024,1]{1,0,2:T(8,128)(2,1)S(1)} %bitcast.69, bf16[2,1024,512]{2,1,0:T(8,128)(2,1)S(1)} %copy-done), kind=kOutput, calls=%fused_computation.10 | convolution fusion | flops 2148532224 | bytes 6291456 | tf_op jit(solution)/shard_map/sp,gsr->gpr/dot_general | solution.py:70
  37.0 0.1 collective-permute-start.8
  37.1 0.6 gather_fusion.4
  37.8 0.6 gather_fusion.2
  38.4 0.6 gather_fusion.5
  39.2 2.9 %fusion.2 = bf16[2,1024,256]{1,2,0:T(8,128)(2,1)S(1)} fusion(bf16[1024,1024,1]{1,0,2:T(8,128)(2,1)} %bitcast.70, s32[2,256]{1,0:T(2,128)S(1)} %bitcast_add_fusion), kind=kOutput, calls=%fused_computation.13 | convolution fusion | flops 1074790400 | bytes 3147776 | tf_op jit(solution)/shard_map/rc,gcj->grj/dot_general | solution.py:81
  42.1 2.3 %fusion.5 = f32[2,1024,256]{2,1,0:T(8,128)S(1)} fusion(bf16[2,1024,512]{2,1,0:T(8,128)(2,1)} %convert_bitcast_fusion, pred[]{:T(512)S(6)} %eq.21, bf16[2,1024,256]{1,2,0:T(8,128)(2,1)S(1)} %fusion.2), kind=kOutput, calls=%fused_computation.20 | convolution fusion | flops 537133056 | bytes 5242881 | tf_op jit(solution)/shard_map/gpr,grj->gpj/dot_general | solution.py:90
  44.5 2.3 %add_convert_fusion = bf16[2,1024,256]{2,1,0:T(8,128)(2,1)S(1)} fusion(f32[2,1024,256]{2,1,0:T(8,128)S(1)} %fusion.5, bf16[2,1024,512]{2,1,0:T(8,128)(2,1)} %collective-permute-done.8, pred[]{:T(512)S(6)} %eq.21, bf16[2,1024,256]{1,2,0:T(8,128)(2,1)S(1)} %fusion.2), kind=kOutput, calls=%fused_computation.8 | convolution fusion | flops 538181632 | bytes 6291457 | tf_op jit(solution)/shard_map/gpr,grj->gpj/dot_general | solution.py:91
  46.8 1.6 %gather_fusion.3 = bf16[8,2,128,256]{3,2,1,0:T(8,128)(2,1)} fusion(bf16[2,8,128,256]{3,2,1,0:T(8,128)(2,1)S(1)} %bitcast.63, s32[1024]{0:T(1024)S(1)} %get-tuple-element.8), kind=kCustom, calls=%fused_computation.3 | custom fusion | bytes 2097184 | tf_op jit(solution)/shard_map/jit(_take)/gather | solution.py:114
  48.4 1.4 %copy.22 = bf16[2,8,128,256]{3,2,1,0:T(8,128)(2,1)S(1)} copy(bf16[2,8,128,256]{3,2,0,1:T(8,128)(2,1)} %bitcast.66) | data formatting | bytes 2097152 | tf_op jit(solution)/shard_map/jit(_take)/gather | solution.py:114
  49.7 0.5 convolution_bitcast_fusion.1
  50.2 1.0 %copy-done.3 = f32[1024,256]{0,1:T(8,128)} copy-done((f32[1024,256]{0,1:T(8,128)}, f32[1024,256]{0,1:T(8,128)S(1)}, u32[]{:S(2)}) %copy-start.3) | copy-done | bytes 1048600
  51.2 0.3 collective-permute-start.9
  51.5 1.6 %gather_fusion.6 = bf16[8,2,128,256]{3,2,1,0:T(8,128)(2,1)} fusion(bf16[2,8,128,256]{3,2,1,0:T(8,128)(2,1)S(1)} %bitcast.64, s32[1024]{0:T(1024)S(1)} %get-tuple-element.7), kind=kCustom, calls=%fused_computation.6 | custom fusion | bytes 2097184 | tf_op jit(solution)/shard_map/jit(_take)/gather | solution.py:114
  53.1 1.4 %copy.24 = bf16[2,8,128,256]{3,2,1,0:T(8,128)(2,1)S(1)} copy(bf16[2,8,128,256]{3,2,0,1:T(8,128)(2,1)} %bitcast.65) | data formatting | bytes 2097152 | tf_op jit(solution)/shard_map/jit(_take)/gather | solution.py:114
  54.5 0.5 convolution_bitcast_fusion
  55.1 1.8 %collective-permute-start.16 = (f32[128,256]{0,1:T(8,128)S(1)}, f32[128,256]{0,1:T(8,128)S(1)}, u32[]{:S(2)}, u32[]{:S(2)}) collective-permute-start(f32[128,256]{0,1:T(8,128)S(1)} %slice.120), channel_id=1, source_target_pairs={{0,2},{4,0},{8,4},{12,8},{14,12},{10,14},{6,10},{2,6},{1,3},{5,1},... | collective-permute-start | bytes 393224 | tf_op jit(solution)/shard_map/ppermute | solution.py:136
  56.9 0.2 collective-permute-done.9
  57.1 0.6 collective-permute-start.10
  57.7 3.6 %collective-permute-done.16 = f32[128,256]{0,1:T(8,128)S(1)} collective-permute-done((f32[128,256]{0,1:T(8,128)S(1)}, f32[128,256]{0,1:T(8,128)S(1)}, u32[]{:S(2)}, u32[]{:S(2)}) %collective-permute-start.16) | collective-permute-done | bytes 131104 | tf_op jit(solution)/shard_map/ppermute | solution.py:136
  61.4 1.2 %collective-permute-start.17 = (f32[128,256]{0,1:T(8,128)S(1)}, f32[128,256]{0,1:T(8,128)S(1)}, u32[]{:S(2)}, u32[]{:S(2)}) collective-permute-start(f32[128,256]{0,1:T(8,128)S(1)} %slice_add_fusion.6), channel_id=1, source_target_pairs={{0,2},{4,0},{8,4},{12,8},{14,12},{10,14},{6,10},{2,6},{1,3},{5,1},... | collective-permute-start | bytes 393224 | tf_op jit(solution)/shard_map/ppermute | solution.py:136
  62.6 1.0 %collective-permute-start.11 = (f32[128,256]{0,1:T(8,128)S(1)}, f32[128,256]{0,1:T(8,128)S(1)}, u32[]{:S(2)}, u32[]{:S(2)}) collective-permute-start(f32[128,256]{0,1:T(8,128)S(1)} %slice_add_fusion.12), channel_id=1, source_target_pairs={{0,4},{4,8},{8,12},{12,14},{14,10},{10,6},{6,2},{2,0},{1,5},{5,9},... | collective-permute-start | bytes 393224 | tf_op jit(solution)/shard_map/ppermute | solution.py:135
  63.5 2.9 %collective-permute-done.17 = f32[128,256]{0,1:T(8,128)S(1)} collective-permute-done((f32[128,256]{0,1:T(8,128)S(1)}, f32[128,256]{0,1:T(8,128)S(1)}, u32[]{:S(2)}, u32[]{:S(2)}) %collective-permute-start.17) | collective-permute-done | bytes 131104 | tf_op jit(solution)/shard_map/ppermute | solution.py:136
  66.4 1.2 %collective-permute-start.18 = (f32[128,256]{0,1:T(8,128)S(1)}, f32[128,256]{0,1:T(8,128)S(1)}, u32[]{:S(2)}, u32[]{:S(2)}) collective-permute-start(f32[128,256]{0,1:T(8,128)S(1)} %slice_add_fusion.5), channel_id=1, source_target_pairs={{0,2},{4,0},{8,4},{12,8},{14,12},{10,14},{6,10},{2,6},{1,3},{5,1},... | collective-permute-start | bytes 393224 | tf_op jit(solution)/shard_map/ppermute | solution.py:136
  67.6 1.0 %collective-permute-start.12 = (f32[128,256]{0,1:T(8,128)S(1)}, f32[128,256]{0,1:T(8,128)S(1)}, u32[]{:S(2)}, u32[]{:S(2)}) collective-permute-start(f32[128,256]{0,1:T(8,128)S(1)} %slice_add_fusion.11), channel_id=1, source_target_pairs={{0,4},{4,8},{8,12},{12,14},{14,10},{10,6},{6,2},{2,0},{1,5},{5,9},... | collective-permute-start | bytes 393224 | tf_op jit(solution)/shard_map/ppermute | solution.py:135
  68.6 3.0 %collective-permute-done.18 = f32[128,256]{0,1:T(8,128)S(1)} collective-permute-done((f32[128,256]{0,1:T(8,128)S(1)}, f32[128,256]{0,1:T(8,128)S(1)}, u32[]{:S(2)}, u32[]{:S(2)}) %collective-permute-start.18) | collective-permute-done | bytes 131104 | tf_op jit(solution)/shard_map/ppermute | solution.py:136
  71.6 1.4 %collective-permute-start.19 = (f32[128,256]{0,1:T(8,128)S(1)}, f32[128,256]{0,1:T(8,128)S(1)}, u32[]{:S(2)}, u32[]{:S(2)}) collective-permute-start(f32[128,256]{0,1:T(8,128)S(1)} %slice_add_fusion.4), channel_id=1, source_target_pairs={{0,2},{4,0},{8,4},{12,8},{14,12},{10,14},{6,10},{2,6},{1,3},{5,1},... | collective-permute-start | bytes 393224 | tf_op jit(solution)/shard_map/ppermute | solution.py:136
  73.0 1.1 %collective-permute-start.13 = (f32[128,256]{0,1:T(8,128)S(1)}, f32[128,256]{0,1:T(8,128)S(1)}, u32[]{:S(2)}, u32[]{:S(2)}) collective-permute-start(f32[128,256]{0,1:T(8,128)S(1)} %slice_add_fusion.10), channel_id=1, source_target_pairs={{0,4},{4,8},{8,12},{12,14},{14,10},{10,6},{6,2},{2,0},{1,5},{5,9},... | collective-permute-start | bytes 393224 | tf_op jit(solution)/shard_map/ppermute | solution.py:135
  74.0 3.6 %collective-permute-done.19 = f32[128,256]{0,1:T(8,128)S(1)} collective-permute-done((f32[128,256]{0,1:T(8,128)S(1)}, f32[128,256]{0,1:T(8,128)S(1)}, u32[]{:S(2)}, u32[]{:S(2)}) %collective-permute-start.19) | collective-permute-done | bytes 131104 | tf_op jit(solution)/shard_map/ppermute | solution.py:136
  77.7 1.5 %collective-permute-start.20 = (f32[128,256]{0,1:T(8,128)S(1)}, f32[128,256]{0,1:T(8,128)S(1)}, u32[]{:S(2)}, u32[]{:S(2)}) collective-permute-start(f32[128,256]{0,1:T(8,128)S(1)} %slice_add_fusion.3), channel_id=1, source_target_pairs={{0,2},{4,0},{8,4},{12,8},{14,12},{10,14},{6,10},{2,6},{1,3},{5,1},... | collective-permute-start | bytes 393224 | tf_op jit(solution)/shard_map/ppermute | solution.py:136
  79.2 0.2 collective-permute-done.13
  79.4 1.0 %collective-permute-start.14 = (f32[128,256]{0,1:T(8,128)S(1)}, f32[128,256]{0,1:T(8,128)S(1)}, u32[]{:S(2)}, u32[]{:S(2)}) collective-permute-start(f32[128,256]{0,1:T(8,128)S(1)} %slice_add_fusion.9), channel_id=1, source_target_pairs={{0,4},{4,8},{8,12},{12,14},{14,10},{10,6},{6,2},{2,0},{1,5},{5,9},... | collective-permute-start | bytes 393224 | tf_op jit(solution)/shard_map/ppermute | solution.py:135
  80.3 3.3 %collective-permute-done.20 = f32[128,256]{0,1:T(8,128)S(1)} collective-permute-done((f32[128,256]{0,1:T(8,128)S(1)}, f32[128,256]{0,1:T(8,128)S(1)}, u32[]{:S(2)}, u32[]{:S(2)}) %collective-permute-start.20) | collective-permute-done | bytes 131104 | tf_op jit(solution)/shard_map/ppermute | solution.py:136
  83.7 1.4 %collective-permute-start.21 = (f32[128,256]{0,1:T(8,128)S(1)}, f32[128,256]{0,1:T(8,128)S(1)}, u32[]{:S(2)}, u32[]{:S(2)}) collective-permute-start(f32[128,256]{0,1:T(8,128)S(1)} %slice_add_fusion.2), channel_id=1, source_target_pairs={{0,2},{4,0},{8,4},{12,8},{14,12},{10,14},{6,10},{2,6},{1,3},{5,1},... | collective-permute-start | bytes 393224 | tf_op jit(solution)/shard_map/ppermute | solution.py:136
  85.0 0.8 collective-permute-start.15
  85.8 2.9 %collective-permute-done.21 = f32[128,256]{0,1:T(8,128)S(1)} collective-permute-done((f32[128,256]{0,1:T(8,128)S(1)}, f32[128,256]{0,1:T(8,128)S(1)}, u32[]{:S(2)}, u32[]{:S(2)}) %collective-permute-start.21) | collective-permute-done | bytes 131104 | tf_op jit(solution)/shard_map/ppermute | solution.py:136
  88.7 1.4 %collective-permute-start.22 = (f32[128,256]{0,1:T(8,128)S(1)}, f32[128,256]{0,1:T(8,128)S(1)}, u32[]{:S(2)}, u32[]{:S(2)}) collective-permute-start(f32[128,256]{0,1:T(8,128)S(1)} %slice_add_fusion.1), channel_id=1, source_target_pairs={{0,2},{4,0},{8,4},{12,8},{14,12},{10,14},{6,10},{2,6},{1,3},{5,1},... | collective-permute-start | bytes 393224 | tf_op jit(solution)/shard_map/ppermute | solution.py:136
  90.1 3.6 %collective-permute-done.22 = f32[128,256]{0,1:T(8,128)S(1)} collective-permute-done((f32[128,256]{0,1:T(8,128)S(1)}, f32[128,256]{0,1:T(8,128)S(1)}, u32[]{:S(2)}, u32[]{:S(2)}) %collective-permute-start.22) | collective-permute-done | bytes 131104 | tf_op jit(solution)/shard_map/ppermute | solution.py:136
  93.8 0.8 copy.26
  (59 shorter events, 0.7 us)
Async XLA Ops:
  0.0 33.1 %copy-start = (bf16[2,1024,512]{2,1,0:T(8,128)(2,1)S(1)}, bf16[2,1024,512]{2,1,0:T(8,128)(2,1)}, u32[]{:S(2)}) copy-start(bf16[2,1024,512]{2,1,0:T(8,128)(2,1)} %param.8) | copy-start | bytes 6291460
  0.0 30.1 %copy-start.2 = (s32[8]{0:T(128)S(1)}, s32[8]{0:T(128)}, u32[]{:S(2)}) copy-start(s32[8]{0:T(128)} %constant.49.clone) | copy-start | bytes 100
  0.0 7.3 %collective-permute-start = (bf16[64,1024]{1,0:T(8,128)(2,1)}, bf16[64,1024]{1,0:T(8,128)(2,1)S(1)}, u32[]{:S(2)}, u32[]{:S(2)}) collective-permute-start(bf16[64,1024]{1,0:T(8,128)(2,1)} %param.9), channel_id=1, source_target_pairs={{0,2},{4,0},{8,4},{12,8},{14,12},{10,14},{6,10},{2,6},{1,3},{5,1},... | collective-permute-start | bytes 393224 | tf_op jit(solution)/shard_map/ppermute | solution.py:50
  3.0 6.2 %collective-permute-start.3 = (bf16[64,1024]{1,0:T(8,128)(2,1)}, bf16[64,1024]{1,0:T(8,128)(2,1)S(1)}, u32[]{:S(2)}, u32[]{:S(2)}) collective-permute-start(bf16[64,1024]{1,0:T(8,128)(2,1)} %param.9), channel_id=1, source_target_pairs={{0,4},{4,8},{8,12},{12,14},{14,10},{10,6},{6,2},{2,0},{1,5},{5,9},... | collective-permute-start | bytes 393224 | tf_op jit(solution)/shard_map/ppermute | solution.py:46
  7.3 5.0 %collective-permute-start.1 = (bf16[64,1024]{1,0:T(8,128)(2,1)S(1)}, bf16[64,1024]{1,0:T(8,128)(2,1)S(1)}, u32[]{:S(2)}, u32[]{:S(2)}) collective-permute-start(bf16[64,1024]{1,0:T(8,128)(2,1)S(1)} %collective-permute-done), channel_id=1, source_target_pairs={{0,2},{4,0},{8,4},{12,8},{14,12},{10,14},{6,10},{2,6},{1,3},{5,1},... | collective-permute-start | bytes 393224 | tf_op jit(solution)/shard_map/ppermute | solution.py:50
  9.2 5.0 %collective-permute-start.4 = (bf16[64,1024]{1,0:T(8,128)(2,1)S(1)}, bf16[64,1024]{1,0:T(8,128)(2,1)S(1)}, u32[]{:S(2)}, u32[]{:S(2)}) collective-permute-start(bf16[64,1024]{1,0:T(8,128)(2,1)S(1)} %collective-permute-done.3), channel_id=1, source_target_pairs={{0,4},{4,8},{8,12},{12,14},{14,10},{10,6},{6,2},{2,0},{1,5},{5,9},... | collective-permute-start | bytes 393224 | tf_op jit(solution)/shard_map/ppermute | solution.py:46
  12.3 7.2 %collective-permute-start.2 = (bf16[64,1024]{1,0:T(8,128)(2,1)S(1)}, bf16[64,1024]{1,0:T(8,128)(2,1)S(1)}, u32[]{:S(2)}, u32[]{:S(2)}) collective-permute-start(bf16[64,1024]{1,0:T(8,128)(2,1)S(1)} %collective-permute-done.1), channel_id=1, source_target_pairs={{0,2},{4,0},{8,4},{12,8},{14,12},{10,14},{6,10},{2,6},{1,3},{5,1},... | collective-permute-start | bytes 393224 | tf_op jit(solution)/shard_map/ppermute | solution.py:50
  14.2 5.1 %collective-permute-start.5 = (bf16[64,1024]{1,0:T(8,128)(2,1)S(1)}, bf16[64,1024]{1,0:T(8,128)(2,1)S(1)}, u32[]{:S(2)}, u32[]{:S(2)}) collective-permute-start(bf16[64,1024]{1,0:T(8,128)(2,1)S(1)} %collective-permute-done.4), channel_id=1, source_target_pairs={{0,4},{4,8},{8,12},{12,14},{14,10},{10,6},{6,2},{2,0},{1,5},{5,9},... | collective-permute-start | bytes 393224 | tf_op jit(solution)/shard_map/ppermute | solution.py:46
  19.3 5.0 %collective-permute-start.6 = (bf16[64,1024]{1,0:T(8,128)(2,1)S(1)}, bf16[64,1024]{1,0:T(8,128)(2,1)S(1)}, u32[]{:S(2)}, u32[]{:S(2)}) collective-permute-start(bf16[64,1024]{1,0:T(8,128)(2,1)S(1)} %collective-permute-done.5), channel_id=1, source_target_pairs={{0,4},{4,8},{8,12},{12,14},{14,10},{10,6},{6,2},{2,0},{1,5},{5,9},... | collective-permute-start | bytes 393224 | tf_op jit(solution)/shard_map/ppermute | solution.py:46
  28.7 2.9 %collective-permute-start.7 = (bf16[8,64,1024]{2,1,0:T(8,128)(2,1)S(1)}, bf16[8,64,1024]{2,1,0:T(8,128)(2,1)}, u32[]{:S(2)}, u32[]{:S(2)}) collective-permute-start(bf16[8,64,1024]{2,1,0:T(8,128)(2,1)S(1)} %gather_fusion), channel_id=1, source_target_pairs={{0,1},{1,0},{2,3},{3,2},{4,5},{5,4},{6,7},{7,6},{8,9},{9,8},{10,11... | collective-permute-start | bytes 3145736 | tf_op jit(solution)/shard_map/ppermute | solution.py:30
  33.1 3.9 %copy-start.5 = (bf16[8,128,1024]{2,1,0:T(8,128)(2,1)}, bf16[8,128,1024]{2,1,0:T(8,128)(2,1)S(1)}, u32[]{:S(2)}) copy-start(bf16[8,128,1024]{2,1,0:T(8,128)(2,1)S(1)} %pad_maximum_fusion) | copy-start | bytes 6291460
  33.2 4.6 %copy-start.1 = (s32[8]{0:T(128)S(1)}, s32[8]{0:T(128)}, u32[]{:S(2)}) copy-start(s32[8]{0:T(128)} %param.12) | copy-start | bytes 100
  33.2 5.9 %copy-start.8 = (s32[2,2]{1,0:T(2,128)S(1)}, s32[2,2]{1,0:T(2,128)}, u32[]{:S(2)}) copy-start(s32[2,2]{1,0:T(2,128)} %param.10) | copy-start | bytes 52
  37.0 7.5 %collective-permute-start.8 = (bf16[2,1024,512]{2,1,0:T(8,128)(2,1)}, bf16[2,1024,512]{2,1,0:T(8,128)(2,1)}, u32[]{:S(2)}, u32[]{:S(2)}) collective-permute-start(bf16[2,1024,512]{2,1,0:T(8,128)(2,1)} %convert_bitcast_fusion), channel_id=1, source_target_pairs={{0,1},{1,0},{2,3},{3,2},{4,5},{5,4},{6,7},{7,6},{8,9},{9,8},{10,11... | collective-permute-start | bytes 6291464 | tf_op jit(solution)/shard_map/ppermute | solution.py:73
  48.4 1.4 %copy-start.6 = (bf16[2,256,512]{2,1,0:T(8,128)(2,1)S(1)}, bf16[2,256,512]{2,1,0:T(8,128)(2,1)}, u32[]{:S(2)}) copy-start(bf16[2,256,512]{2,1,0:T(8,128)(2,1)} %param.11) | copy-start | bytes 1572868
  50.2 1.0 %copy-start.3 = (f32[1024,256]{0,1:T(8,128)}, f32[1024,256]{0,1:T(8,128)S(1)}, u32[]{:S(2)}) copy-start(f32[1024,256]{0,1:T(8,128)S(1)} %convolution_bitcast_fusion.1) | copy-start | bytes 3145732
  51.2 5.9 %collective-permute-start.9 = (f32[128,256]{0,1:T(8,128)S(1)}, f32[128,256]{0,1:T(8,128)S(1)}, u32[]{:S(2)}, u32[]{:S(2)}) collective-permute-start(f32[128,256]{0,1:T(8,128)S(1)} %slice.112), channel_id=1, source_target_pairs={{0,4},{4,8},{8,12},{12,14},{14,10},{10,6},{6,2},{2,0},{1,5},{5,9},... | collective-permute-start | bytes 393224 | tf_op jit(solution)/shard_map/ppermute | solution.py:135
  53.1 1.4 %copy-start.7 = (bf16[2,256,512]{2,1,0:T(8,128)(2,1)S(1)}, bf16[2,256,512]{2,1,0:T(8,128)(2,1)}, u32[]{:S(2)}) copy-start(bf16[2,256,512]{2,1,0:T(8,128)(2,1)} %param.11) | copy-start | bytes 1572868
  53.1 4.0 %copy-start.4 = (f32[1024,256]{0,1:T(8,128)S(1)}, f32[1024,256]{0,1:T(8,128)}, u32[]{:S(2)}) copy-start(f32[1024,256]{0,1:T(8,128)} %copy-done.3) | copy-start | bytes 3145732
  55.1 6.3 %collective-permute-start.16 = (f32[128,256]{0,1:T(8,128)S(1)}, f32[128,256]{0,1:T(8,128)S(1)}, u32[]{:S(2)}, u32[]{:S(2)}) collective-permute-start(f32[128,256]{0,1:T(8,128)S(1)} %slice.120), channel_id=1, source_target_pairs={{0,2},{4,0},{8,4},{12,8},{14,12},{10,14},{6,10},{2,6},{1,3},{5,1},... | collective-permute-start | bytes 393224 | tf_op jit(solution)/shard_map/ppermute | solution.py:136
  57.1 5.4 %collective-permute-start.10 = (f32[128,256]{0,1:T(8,128)S(1)}, f32[128,256]{0,1:T(8,128)S(1)}, u32[]{:S(2)}, u32[]{:S(2)}) collective-permute-start(f32[128,256]{0,1:T(8,128)S(1)} %slice_add_fusion.13), channel_id=1, source_target_pairs={{0,4},{4,8},{8,12},{12,14},{14,10},{10,6},{6,2},{2,0},{1,5},{5,9},... | collective-permute-start | bytes 393224 | tf_op jit(solution)/shard_map/ppermute | solution.py:135
  61.4 5.0 %collective-permute-start.17 = (f32[128,256]{0,1:T(8,128)S(1)}, f32[128,256]{0,1:T(8,128)S(1)}, u32[]{:S(2)}, u32[]{:S(2)}) collective-permute-start(f32[128,256]{0,1:T(8,128)S(1)} %slice_add_fusion.6), channel_id=1, source_target_pairs={{0,2},{4,0},{8,4},{12,8},{14,12},{10,14},{6,10},{2,6},{1,3},{5,1},... | collective-permute-start | bytes 393224 | tf_op jit(solution)/shard_map/ppermute | solution.py:136
  62.6 5.0 %collective-permute-start.11 = (f32[128,256]{0,1:T(8,128)S(1)}, f32[128,256]{0,1:T(8,128)S(1)}, u32[]{:S(2)}, u32[]{:S(2)}) collective-permute-start(f32[128,256]{0,1:T(8,128)S(1)} %slice_add_fusion.12), channel_id=1, source_target_pairs={{0,4},{4,8},{8,12},{12,14},{14,10},{10,6},{6,2},{2,0},{1,5},{5,9},... | collective-permute-start | bytes 393224 | tf_op jit(solution)/shard_map/ppermute | solution.py:135
  66.4 5.2 %collective-permute-start.18 = (f32[128,256]{0,1:T(8,128)S(1)}, f32[128,256]{0,1:T(8,128)S(1)}, u32[]{:S(2)}, u32[]{:S(2)}) collective-permute-start(f32[128,256]{0,1:T(8,128)S(1)} %slice_add_fusion.5), channel_id=1, source_target_pairs={{0,2},{4,0},{8,4},{12,8},{14,12},{10,14},{6,10},{2,6},{1,3},{5,1},... | collective-permute-start | bytes 393224 | tf_op jit(solution)/shard_map/ppermute | solution.py:136
  67.6 5.4 %collective-permute-start.12 = (f32[128,256]{0,1:T(8,128)S(1)}, f32[128,256]{0,1:T(8,128)S(1)}, u32[]{:S(2)}, u32[]{:S(2)}) collective-permute-start(f32[128,256]{0,1:T(8,128)S(1)} %slice_add_fusion.11), channel_id=1, source_target_pairs={{0,4},{4,8},{8,12},{12,14},{14,10},{10,6},{6,2},{2,0},{1,5},{5,9},... | collective-permute-start | bytes 393224 | tf_op jit(solution)/shard_map/ppermute | solution.py:135
  71.6 6.0 %collective-permute-start.19 = (f32[128,256]{0,1:T(8,128)S(1)}, f32[128,256]{0,1:T(8,128)S(1)}, u32[]{:S(2)}, u32[]{:S(2)}) collective-permute-start(f32[128,256]{0,1:T(8,128)S(1)} %slice_add_fusion.4), channel_id=1, source_target_pairs={{0,2},{4,0},{8,4},{12,8},{14,12},{10,14},{6,10},{2,6},{1,3},{5,1},... | collective-permute-start | bytes 393224 | tf_op jit(solution)/shard_map/ppermute | solution.py:136
  73.0 6.4 %collective-permute-start.13 = (f32[128,256]{0,1:T(8,128)S(1)}, f32[128,256]{0,1:T(8,128)S(1)}, u32[]{:S(2)}, u32[]{:S(2)}) collective-permute-start(f32[128,256]{0,1:T(8,128)S(1)} %slice_add_fusion.10), channel_id=1, source_target_pairs={{0,4},{4,8},{8,12},{12,14},{14,10},{10,6},{6,2},{2,0},{1,5},{5,9},... | collective-permute-start | bytes 393224 | tf_op jit(solution)/shard_map/ppermute | solution.py:135
  77.7 6.0 %collective-permute-start.20 = (f32[128,256]{0,1:T(8,128)S(1)}, f32[128,256]{0,1:T(8,128)S(1)}, u32[]{:S(2)}, u32[]{:S(2)}) collective-permute-start(f32[128,256]{0,1:T(8,128)S(1)} %slice_add_fusion.3), channel_id=1, source_target_pairs={{0,2},{4,0},{8,4},{12,8},{14,12},{10,14},{6,10},{2,6},{1,3},{5,1},... | collective-permute-start | bytes 393224 | tf_op jit(solution)/shard_map/ppermute | solution.py:136
  79.4 5.6 %collective-permute-start.14 = (f32[128,256]{0,1:T(8,128)S(1)}, f32[128,256]{0,1:T(8,128)S(1)}, u32[]{:S(2)}, u32[]{:S(2)}) collective-permute-start(f32[128,256]{0,1:T(8,128)S(1)} %slice_add_fusion.9), channel_id=1, source_target_pairs={{0,4},{4,8},{8,12},{12,14},{14,10},{10,6},{6,2},{2,0},{1,5},{5,9},... | collective-permute-start | bytes 393224 | tf_op jit(solution)/shard_map/ppermute | solution.py:135
  83.7 5.0 %collective-permute-start.21 = (f32[128,256]{0,1:T(8,128)S(1)}, f32[128,256]{0,1:T(8,128)S(1)}, u32[]{:S(2)}, u32[]{:S(2)}) collective-permute-start(f32[128,256]{0,1:T(8,128)S(1)} %slice_add_fusion.2), channel_id=1, source_target_pairs={{0,2},{4,0},{8,4},{12,8},{14,12},{10,14},{6,10},{2,6},{1,3},{5,1},... | collective-permute-start | bytes 393224 | tf_op jit(solution)/shard_map/ppermute | solution.py:136
  85.0 5.0 %collective-permute-start.15 = (f32[128,256]{0,1:T(8,128)S(1)}, f32[128,256]{0,1:T(8,128)S(1)}, u32[]{:S(2)}, u32[]{:S(2)}) collective-permute-start(f32[128,256]{0,1:T(8,128)S(1)} %slice_add_fusion.8), channel_id=1, source_target_pairs={{0,4},{4,8},{8,12},{12,14},{14,10},{10,6},{6,2},{2,0},{1,5},{5,9},... | collective-permute-start | bytes 393224 | tf_op jit(solution)/shard_map/ppermute | solution.py:135
  88.7 5.0 %collective-permute-start.22 = (f32[128,256]{0,1:T(8,128)S(1)}, f32[128,256]{0,1:T(8,128)S(1)}, u32[]{:S(2)}, u32[]{:S(2)}) collective-permute-start(f32[128,256]{0,1:T(8,128)S(1)} %slice_add_fusion.1), channel_id=1, source_target_pairs={{0,2},{4,0},{8,4},{12,8},{14,12},{10,14},{6,10},{2,6},{1,3},{5,1},... | collective-permute-start | bytes 393224 | tf_op jit(solution)/shard_map/ppermute | solution.py:136

commit v3 on v2

--- a/solution.py
+++ b/solution.py
@@ -114,26 +114,21 @@
             taken = jnp.take(by_group, picked_groups, axis=1, mode="clip")
             return taken.reshape(active_rotated.shape)
 
+        ordered = in_step_order(pos - 1 - steps)
         cols = factors.shape[2] // 2
         part_r = jnp.einsum(
-            "gpj,gjq->pq",
-            in_step_order(pos - 1 - steps),
-            factors[:, :, :cols],
-            preferred_element_type=jnp.float32,
+            "gpj,gjq->pq", ordered, factors[:, :, :cols], preferred_element_type=jnp.float32
         ).reshape(n, per, cols)
         part_l = jnp.einsum(
-            "gpj,gjq->pq",
-            in_step_order(pos + 1 + steps),
-            factors[:, :, cols:],
-            preferred_element_type=jnp.float32,
+            "gpj,gjq->pq", ordered, factors[:, :, cols:], preferred_element_type=jnp.float32
         ).reshape(n, per, -1)
         right = [(ring[i], ring[(i + 1) % n]) for i in range(n)]
         left = [(ring[i], ring[(i - 1) % n]) for i in range(n)]
         acc_r = part_r[0]
-        acc_l = part_l[0]
+        acc_l = part_l[n - 2]
         for k in range(1, n):
             acc_r = lax.ppermute(acc_r, "vec", right) + part_r[k]
-            acc_l = lax.ppermute(acc_l, "vec", left) + part_l[k]
+            acc_l = lax.ppermute(acc_l, "vec", left) + part_l[n - 2 - k if k < n - 1 else n - 1]
         return jnp.concatenate([acc_r, acc_l], axis=1)
 
     return per_device

time: 95 us -> 91.1 us (0.959)
  local copies, waits for them, and re-layouts: 19.7 us -> 14.4 us
  waiting for transfers between devices: 34.6 us -> 39.4 us
  starting transfers between devices: 23 us -> 19.4 us
  matrix products: 12.3 us -> 13.3 us
    ppermute x7, waiting for transfers between devices: 0.39 us -> 21.4 us  [per_device(): acc_r = lax.ppermute(acc_r, 'vec', right) + part_r[k]]
    ppermute x7, waiting for transfers between devices: 22.8 us -> 5.28 us  [per_device(): lax.ppermute(acc_l, 'vec', left) + part_l[n - 2 - k if k < n - 1 else n - 1]]
    gather x4 -> x2, local copies, waits for them, and re-layouts: 5.93 us -> 1.93 us  [in_step_order(): taken = jnp.take(by_group, picked_groups, axis=1, mode='clip')]
    ppermute x7, starting transfers between devices: 5.62 us -> 2.22 us  [per_device(): acc_r = lax.ppermute(acc_r, 'vec', right) + part_r[k]]
    ppermute x1, waiting for transfers between devices: 0.76 us -> 2.12 us  [swap_orb(): other = lax.ppermute(x, 'orb', [(0, 1), (1, 0)])]
    gather x4 -> x2, local copies, waits for them, and re-layouts: 2.57 us -> 1.29 us  [in_step_order(): picked_groups = held[ring_arr[order % n]].reshape(-1)]
    dot_general x1, matrix products: 2.34 us -> 3.34 us  [per_device(): jnp.einsum('gpr,grj->gpj', other_half, theirs, preferred_element_type=jnp...]
    unnamed x26 -> x20, local copies, waits for them, and re-layouts: 6.62 us -> 6.57 us
  transfers between devices with their start and end apart: 23 -> 23, of which waited for: 13 -> 18; matrix products, arithmetic and copies ran while one was open for 19% -> 15% of each run, Pallas kernels for 0% -> 0%
where the time goes in v3:
time: 91.1 us; the launch traced here: 90.7 us
  waiting for transfers between devices  39.4 us (43%)
  starting transfers between devices  19.4 us (21%)
  local copies, waits for them, and re-layouts  14.4 us (16%)
  matrix products  13.3 us (15%)
  other arithmetic  3.3 us (4%)
  between operations  0.94 us (1%)
    ppermute x7, waiting for transfers between devices, per_device(): acc_r = lax.ppermute(acc_r, 'vec', right) + part_r[k]  21.4 us
    ppermute x7, starting transfers between devices, per_device(): lax.ppermute(acc_l, 'vec', left) + part_l[n - 2 - k if k < n - 1 else n - 1]  9.47 us
    ppermute x4, waiting for transfers between devices, ring_all_gather(): cur = lax.ppermute(cur, 'vec', right)  8.37 us
    ppermute x3, starting transfers between devices, ring_all_gather(): cur = lax.ppermute(cur, 'vec', left)  6.79 us
    unnamed x20, local copies, waits for them, and re-layouts  6.57 us
    ppermute x7, waiting for transfers between devices, per_device(): lax.ppermute(acc_l, 'vec', left) + part_l[n - 2 - k if k < n - 1 else n - 1]  5.28 us
    dot_general x1, matrix products, per_device(): jnp.einsum('sp,gsr->gpr', whole, vectors, preferred_element_type=jnp.floa...  3.75 us
    dot_general x1, matrix products, per_device(): jnp.einsum('gpr,grj->gpj', other_half, theirs, preferred_element_type=jnp...  3.34 us
  transfers between devices with their start and end apart: 23, of which 18 were waited for; matrix products, arithmetic and copies ran while one was open for 15% of the time, Pallas kernels for 0%

profile of v3, /device:TPU:0, one launch (start us, length us, event | category | flops | bytes accessed | tf_op | source)
XLA Modules:
  0.0 90.7 jit_solution(11793061164957003849)
XLA Ops:
  0.0 3.0 %collective-permute-start = (bf16[64,1024]{1,0:T(8,128)(2,1)}, bf16[64,1024]{1,0:T(8,128)(2,1)S(1)}, u32[]{:S(2)}, u32[]{:S(2)}) collective-permute-start(bf16[64,1024]{1,0:T(8,128)(2,1)} %param.9), channel_id=1, source_target_pairs={{0,2},{4,0},{8,4},{12,8},{14,12},{10,14},{6,10},{2,6},{1,3},{5,1},... | collective-permute-start | bytes 393224 | tf_op jit(solution)/shard_map/ppermute | solution.py:50
  3.0 0.1 collective-permute-start.3
  3.1 1.6 %bitcast_dynamic-update-slice_fusion.7 = bf16[8,64,1024]{2,1,0:T(8,128)(2,1)} fusion(bf16[64,1024]{1,0:T(8,128)(2,1)} %param.9), kind=kLoop, calls=%fused_computation.49 | loop fusion | bytes 262144
  4.7 1.2 %dynamic_slice.6 = s32[1]{0:T(128)} dynamic-slice(s32[8]{0:T(128)} %constant.41.clone, s32[]{:T(128)S(6)} %select_n.67), dynamic_slice_sizes={1} | dynamic-slice | bytes 12 | tf_op jit(solution)/shard_map/dynamic_slice | solution.py:54
  5.9 1.3 %and_select_fusion.1 = s32[8]{0:T(128)S(1)} fusion(s32[8]{0:T(128)} %constant.41.clone, s32[]{:T(128)} %bitcast.8), kind=kLoop, calls=%fused_computation.62 | loop fusion | flops 96 | bytes 68 | tf_op jit(solution)/shard_map/jit(remainder)/select_n | solution.py:55
  7.3 1.9 %collective-permute-start.1 = (bf16[64,1024]{1,0:T(8,128)(2,1)S(1)}, bf16[64,1024]{1,0:T(8,128)(2,1)S(1)}, u32[]{:S(2)}, u32[]{:S(2)}) collective-permute-start(bf16[64,1024]{1,0:T(8,128)(2,1)S(1)} %collective-permute-done), channel_id=1, source_target_pairs={{0,2},{4,0},{8,4},{12,8},{14,12},{10,14},{6,10},{2,6},{1,3},{5,1},... | collective-permute-start | bytes 393224 | tf_op jit(solution)/shard_map/ppermute | solution.py:50
  9.2 0.2 collective-permute-start.4
  9.4 0.7 bitcast_dynamic-update-slice_fusion.6
  10.0 2.3 %collective-permute-done.1 = bf16[64,1024]{1,0:T(8,128)(2,1)S(1)} collective-permute-done((bf16[64,1024]{1,0:T(8,128)(2,1)S(1)}, bf16[64,1024]{1,0:T(8,128)(2,1)S(1)}, u32[]{:S(2)}, u32[]{:S(2)}) %collective-permute-start.1) | collective-permute-done | bytes 131104 | tf_op jit(solution)/shard_map/ppermute | solution.py:50
  12.3 1.9 %collective-permute-start.2 = (bf16[64,1024]{1,0:T(8,128)(2,1)S(1)}, bf16[64,1024]{1,0:T(8,128)(2,1)S(1)}, u32[]{:S(2)}, u32[]{:S(2)}) collective-permute-start(bf16[64,1024]{1,0:T(8,128)(2,1)S(1)} %collective-permute-done.1), channel_id=1, source_target_pairs={{0,2},{4,0},{8,4},{12,8},{14,12},{10,14},{6,10},{2,6},{1,3},{5,1},... | collective-permute-start | bytes 393224 | tf_op jit(solution)/shard_map/ppermute | solution.py:50
  14.2 0.2 collective-permute-start.5
  14.3 0.7 bitcast_dynamic-update-slice_fusion.5
  15.0 4.3 %collective-permute-done.5 = bf16[64,1024]{1,0:T(8,128)(2,1)S(1)} collective-permute-done((bf16[64,1024]{1,0:T(8,128)(2,1)S(1)}, bf16[64,1024]{1,0:T(8,128)(2,1)S(1)}, u32[]{:S(2)}, u32[]{:S(2)}) %collective-permute-start.5) | collective-permute-done | bytes 131104 | tf_op jit(solution)/shard_map/ppermute | solution.py:46
  19.3 0.2 collective-permute-start.6
  19.5 0.7 bitcast_dynamic-update-slice_fusion.4
  20.2 4.1 %collective-permute-done.6 = bf16[64,1024]{1,0:T(8,128)(2,1)S(1)} collective-permute-done((bf16[64,1024]{1,0:T(8,128)(2,1)S(1)}, bf16[64,1024]{1,0:T(8,128)(2,1)S(1)}, u32[]{:S(2)}, u32[]{:S(2)}) %collective-permute-start.6) | collective-permute-done | bytes 131104 | tf_op jit(solution)/shard_map/ppermute | solution.py:46
  24.2 0.7 bitcast_dynamic-update-slice_fusion.3
  24.9 0.7 bitcast_dynamic-update-slice_fusion.2
  25.6 0.7 bitcast_dynamic-update-slice_fusion.1
  26.2 0.7 bitcast_dynamic-update-slice_fusion
  26.9 1.8 %gather_fusion = bf16[8,64,1024]{2,1,0:T(8,128)(2,1)S(1)} fusion(bf16[8,64,1024]{2,1,0:T(8,128)(2,1)} %bitcast_dynamic-update-slice_fusion, s32[1024]{0:T(1024)S(1)} %pad_clamp_fusion.3), kind=kCustom, calls=%fused_computation | custom fusion | bytes 2097184 | tf_op jit(solution)/shard_map/jit(_take)/gather | solution.py:55
  29.4 2.1 %collective-permute-done.7 = bf16[8,64,1024]{2,1,0:T(8,128)(2,1)} collective-permute-done((bf16[8,64,1024]{2,1,0:T(8,128)(2,1)S(1)}, bf16[8,64,1024]{2,1,0:T(8,128)(2,1)}, u32[]{:S(2)}, u32[]{:S(2)}) %collective-permute-start.7) | collective-permute-done | bytes 1048608 | tf_op jit(solution)/shard_map/ppermute | solution.py:30
  31.6 1.4 %broadcast_select_fusion.1 = (bf16[8,64,1024]{2,1,0:T(8,128)(2,1)S(1)}, bf16[8,64,1024]{2,1,0:T(8,128)(2,1)S(1)}) fusion(bf16[8,64,1024]{2,1,0:T(8,128)(2,1)S(1)} %gather_fusion, bf16[8,64,1024]{2,1,0:T(8,128)(2,1)} %collective-permute-done.7, pred[]{:T(512)S(6)} %eq.20), kind=kLoop, calls=%fused_computation.15 | loop fusion | flops 1048576 | bytes 4194305 | tf_op jit(solution)/shard_map/jit(_where)/select_n | solution.py:32
  32.9 0.2 pad_maximum_fusion
  33.2 3.7 %convert_bitcast_fusion = bf16[2,1024,512]{2,1,0:T(8,128)(2,1)} fusion(bf16[1024,1024,1]{1,0,2:T(8,128)(2,1)S(1)} %bitcast.58, bf16[2,1024,512]{2,1,0:T(8,128)(2,1)S(1)} %copy-done), kind=kOutput, calls=%fused_computation.7 | convolution fusion | flops 2148532224 | bytes 6291456 | tf_op jit(solution)/shard_map/sp,gsr->gpr/dot_general | solution.py:70
  36.9 0.1 collective-permute-start.8
  37.1 0.6 gather_fusion.1
  37.8 0.6 gather_fusion.2
  38.5 2.9 %fusion.2 = bf16[2,1024,256]{1,2,0:T(8,128)(2,1)S(1)} fusion(bf16[1024,1024,1]{1,0,2:T(8,128)(2,1)} %bitcast.59, s32[2,256]{1,0:T(2,128)S(1)} %bitcast_add_fusion), kind=kOutput, calls=%fused_computation.10 | convolution fusion | flops 1074790400 | bytes 3147776 | tf_op jit(solution)/shard_map/rc,gcj->grj/dot_general | solution.py:81
  41.4 2.3 %fusion.5 = f32[2,1024,256]{2,1,0:T(8,128)S(1)} fusion(bf16[2,1024,512]{2,1,0:T(8,128)(2,1)} %convert_bitcast_fusion, pred[]{:T(512)S(6)} %eq.20, bf16[2,1024,256]{1,2,0:T(8,128)(2,1)S(1)} %fusion.2), kind=kOutput, calls=%fused_computation.17 | convolution fusion | flops 537133056 | bytes 5242881 | tf_op jit(solution)/shard_map/gpr,grj->gpj/dot_general | solution.py:90
  43.8 3.3 %add_convert_fusion = bf16[2,1024,256]{2,1,0:T(8,128)(2,1)} fusion(f32[2,1024,256]{2,1,0:T(8,128)S(1)} %fusion.5, bf16[2,1024,512]{2,1,0:T(8,128)(2,1)} %collective-permute-done.8, pred[]{:T(512)S(6)} %eq.20, bf16[2,1024,256]{1,2,0:T(8,128)(2,1)S(1)} %fusion.2), kind=kOutput, calls=%fused_computation.5 | convolution fusion | flops 538181632 | bytes 6291457 | tf_op jit(solution)/shard_map/gpr,grj->gpj/dot_general | solution.py:91
  47.1 1.8 %gather_fusion.3 = bf16[8,2,128,256]{3,2,1,0:T(8,128)(2,1)S(1)} fusion(bf16[2,8,128,256]{3,2,1,0:T(8,128)(2,1)} %bitcast.57, s32[1024]{0:T(1024)S(1)} %pad_clamp_fusion), kind=kCustom, calls=%fused_computation.3 | custom fusion | bytes 2097184 | tf_op jit(solution)/shard_map/jit(_take)/gather | solution.py:114
  49.1 0.9 %copy-done.4 = bf16[2,256,512]{2,1,0:T(8,128)(2,1)S(1)} copy-done((bf16[2,256,512]{2,1,0:T(8,128)(2,1)S(1)}, bf16[2,256,512]{2,1,0:T(8,128)(2,1)}, u32[]{:S(2)}) %copy-start.4) | copy-done | bytes 524312
  50.0 0.5 convolution_bitcast_fusion.1
  50.5 0.3 collective-permute-start.9
  50.8 0.5 convolution_bitcast_fusion
  51.3 1.8 %collective-permute-start.16 = (f32[128,256]{0,1:T(8,128)S(1)}, f32[128,256]{0,1:T(8,128)S(1)}, u32[]{:S(2)}, u32[]{:S(2)}) collective-permute-start(f32[128,256]{0,1:T(8,128)S(1)} %slice.114), channel_id=1, source_target_pairs={{0,2},{4,0},{8,4},{12,8},{14,12},{10,14},{6,10},{2,6},{1,3},{5,1},... | collective-permute-start | bytes 393224 | tf_op jit(solution)/shard_map/ppermute | solution.py:131
  53.2 3.2 %collective-permute-done.9 = f32[128,256]{0,1:T(8,128)S(1)} collective-permute-done((f32[128,256]{0,1:T(8,128)S(1)}, f32[128,256]{0,1:T(8,128)S(1)}, u32[]{:S(2)}, u32[]{:S(2)}) %collective-permute-start.9) | collective-permute-done | bytes 131104 | tf_op jit(solution)/shard_map/ppermute | solution.py:130
  56.4 0.3 collective-permute-start.10
  56.7 0.9 collective-permute-done.16
  57.6 1.1 %collective-permute-start.17 = (f32[128,256]{0,1:T(8,128)S(1)}, f32[128,256]{0,1:T(8,128)S(1)}, u32[]{:S(2)}, u32[]{:S(2)}) collective-permute-start(f32[128,256]{0,1:T(8,128)S(1)} %slice_add_fusion.6), channel_id=1, source_target_pairs={{0,2},{4,0},{8,4},{12,8},{14,12},{10,14},{6,10},{2,6},{1,3},{5,1},... | collective-permute-start | bytes 393224 | tf_op jit(solution)/shard_map/ppermute | solution.py:131
  58.7 2.6 %collective-permute-done.10 = f32[128,256]{0,1:T(8,128)S(1)} collective-permute-done((f32[128,256]{0,1:T(8,128)S(1)}, f32[128,256]{0,1:T(8,128)S(1)}, u32[]{:S(2)}, u32[]{:S(2)}) %collective-permute-start.10) | collective-permute-done | bytes 131104 | tf_op jit(solution)/shard_map/ppermute | solution.py:130
  61.4 0.3 collective-permute-start.11
  61.8 0.9 collective-permute-done.17
  62.7 1.1 %collective-permute-start.18 = (f32[128,256]{0,1:T(8,128)S(1)}, f32[128,256]{0,1:T(8,128)S(1)}, u32[]{:S(2)}, u32[]{:S(2)}) collective-permute-start(f32[128,256]{0,1:T(8,128)S(1)} %slice_add_fusion.5), channel_id=1, source_target_pairs={{0,2},{4,0},{8,4},{12,8},{14,12},{10,14},{6,10},{2,6},{1,3},{5,1},... | collective-permute-start | bytes 393224 | tf_op jit(solution)/shard_map/ppermute | solution.py:131
  63.8 2.8 %collective-permute-done.11 = f32[128,256]{0,1:T(8,128)S(1)} collective-permute-done((f32[128,256]{0,1:T(8,128)S(1)}, f32[128,256]{0,1:T(8,128)S(1)}, u32[]{:S(2)}, u32[]{:S(2)}) %collective-permute-start.11) | collective-permute-done | bytes 131104 | tf_op jit(solution)/shard_map/ppermute | solution.py:130
  66.6 0.3 collective-permute-start.12
  66.9 0.8 collective-permute-done.18
  67.7 1.2 %collective-permute-start.19 = (f32[128,256]{0,1:T(8,128)S(1)}, f32[128,256]{0,1:T(8,128)S(1)}, u32[]{:S(2)}, u32[]{:S(2)}) collective-permute-start(f32[128,256]{0,1:T(8,128)S(1)} %slice_add_fusion.4), channel_id=1, source_target_pairs={{0,2},{4,0},{8,4},{12,8},{14,12},{10,14},{6,10},{2,6},{1,3},{5,1},... | collective-permute-start | bytes 393224 | tf_op jit(solution)/shard_map/ppermute | solution.py:131
  68.9 3.8 %collective-permute-done.12 = f32[128,256]{0,1:T(8,128)S(1)} collective-permute-done((f32[128,256]{0,1:T(8,128)S(1)}, f32[128,256]{0,1:T(8,128)S(1)}, u32[]{:S(2)}, u32[]{:S(2)}) %collective-permute-start.12) | collective-permute-done | bytes 131104 | tf_op jit(solution)/shard_map/ppermute | solution.py:130
  72.8 0.1 collective-permute-start.13
  72.9 0.6 collective-permute-done.19
  73.4 1.8 %collective-permute-start.20 = (f32[128,256]{0,1:T(8,128)S(1)}, f32[128,256]{0,1:T(8,128)S(1)}, u32[]{:S(2)}, u32[]{:S(2)}) collective-permute-start(f32[128,256]{0,1:T(8,128)S(1)} %slice_add_fusion.3), channel_id=1, source_target_pairs={{0,2},{4,0},{8,4},{12,8},{14,12},{10,14},{6,10},{2,6},{1,3},{5,1},... | collective-permute-start | bytes 393224 | tf_op jit(solution)/shard_map/ppermute | solution.py:131
  75.2 3.4 %collective-permute-done.13 = f32[128,256]{0,1:T(8,128)S(1)} collective-permute-done((f32[128,256]{0,1:T(8,128)S(1)}, f32[128,256]{0,1:T(8,128)S(1)}, u32[]{:S(2)}, u32[]{:S(2)}) %collective-permute-start.13) | collective-permute-done | bytes 131104 | tf_op jit(solution)/shard_map/ppermute | solution.py:130
  78.6 0.3 collective-permute-start.14
  79.0 0.6 collective-permute-done.20
  79.6 1.3 %collective-permute-start.21 = (f32[128,256]{0,1:T(8,128)S(1)}, f32[128,256]{0,1:T(8,128)S(1)}, u32[]{:S(2)}, u32[]{:S(2)}) collective-permute-start(f32[128,256]{0,1:T(8,128)S(1)} %slice_add_fusion.2), channel_id=1, source_target_pairs={{0,2},{4,0},{8,4},{12,8},{14,12},{10,14},{6,10},{2,6},{1,3},{5,1},... | collective-permute-start | bytes 393224 | tf_op jit(solution)/shard_map/ppermute | solution.py:131
  80.8 2.8 %collective-permute-done.14 = f32[128,256]{0,1:T(8,128)S(1)} collective-permute-done((f32[128,256]{0,1:T(8,128)S(1)}, f32[128,256]{0,1:T(8,128)S(1)}, u32[]{:S(2)}, u32[]{:S(2)}) %collective-permute-start.14) | collective-permute-done | bytes 131104 | tf_op jit(solution)/shard_map/ppermute | solution.py:130
  83.7 0.6 collective-permute-start.15
  84.2 0.5 collective-permute-done.21
  84.8 1.1 %collective-permute-start.22 = (f32[128,256]{0,1:T(8,128)S(1)}, f32[128,256]{0,1:T(8,128)S(1)}, u32[]{:S(2)}, u32[]{:S(2)}) collective-permute-start(f32[128,256]{0,1:T(8,128)S(1)} %slice_add_fusion.1), channel_id=1, source_target_pairs={{0,2},{4,0},{8,4},{12,8},{14,12},{10,14},{6,10},{2,6},{1,3},{5,1},... | collective-permute-start | bytes 393224 | tf_op jit(solution)/shard_map/ppermute | solution.py:131
  85.9 2.8 %collective-permute-done.15 = f32[128,256]{0,1:T(8,128)S(1)} collective-permute-done((f32[128,256]{0,1:T(8,128)S(1)}, f32[128,256]{0,1:T(8,128)S(1)}, u32[]{:S(2)}, u32[]{:S(2)}) %collective-permute-start.15) | collective-permute-done | bytes 131104 | tf_op jit(solution)/shard_map/ppermute | solution.py:130
  88.7 1.0 %collective-permute-done.22 = f32[128,256]{0,1:T(8,128)S(1)} collective-permute-done((f32[128,256]{0,1:T(8,128)S(1)}, f32[128,256]{0,1:T(8,128)S(1)}, u32[]{:S(2)}, u32[]{:S(2)}) %collective-permute-start.22) | collective-permute-done | bytes 131104 | tf_op jit(solution)/shard_map/ppermute | solution.py:131
  89.8 0.8 copy.24
  (45 shorter events, 0.8 us)
Async XLA Ops:
  0.0 33.1 %copy-start = (bf16[2,1024,512]{2,1,0:T(8,128)(2,1)S(1)}, bf16[2,1024,512]{2,1,0:T(8,128)(2,1)}, u32[]{:S(2)}) copy-start(bf16[2,1024,512]{2,1,0:T(8,128)(2,1)} %param.8) | copy-start | bytes 6291460
  0.0 7.3 %collective-permute-start = (bf16[64,1024]{1,0:T(8,128)(2,1)}, bf16[64,1024]{1,0:T(8,128)(2,1)S(1)}, u32[]{:S(2)}, u32[]{:S(2)}) collective-permute-start(bf16[64,1024]{1,0:T(8,128)(2,1)} %param.9), channel_id=1, source_target_pairs={{0,2},{4,0},{8,4},{12,8},{14,12},{10,14},{6,10},{2,6},{1,3},{5,1},... | collective-permute-start | bytes 393224 | tf_op jit(solution)/shard_map/ppermute | solution.py:50
  3.0 6.2 %collective-permute-start.3 = (bf16[64,1024]{1,0:T(8,128)(2,1)}, bf16[64,1024]{1,0:T(8,128)(2,1)S(1)}, u32[]{:S(2)}, u32[]{:S(2)}) collective-permute-start(bf16[64,1024]{1,0:T(8,128)(2,1)} %param.9), channel_id=1, source_target_pairs={{0,4},{4,8},{8,12},{12,14},{14,10},{10,6},{6,2},{2,0},{1,5},{5,9},... | collective-permute-start | bytes 393224 | tf_op jit(solution)/shard_map/ppermute | solution.py:46
  7.3 5.0 %collective-permute-start.1 = (bf16[64,1024]{1,0:T(8,128)(2,1)S(1)}, bf16[64,1024]{1,0:T(8,128)(2,1)S(1)}, u32[]{:S(2)}, u32[]{:S(2)}) collective-permute-start(bf16[64,1024]{1,0:T(8,128)(2,1)S(1)} %collective-permute-done), channel_id=1, source_target_pairs={{0,2},{4,0},{8,4},{12,8},{14,12},{10,14},{6,10},{2,6},{1,3},{5,1},... | collective-permute-start | bytes 393224 | tf_op jit(solution)/shard_map/ppermute | solution.py:50
  9.2 5.0 %collective-permute-start.4 = (bf16[64,1024]{1,0:T(8,128)(2,1)S(1)}, bf16[64,1024]{1,0:T(8,128)(2,1)S(1)}, u32[]{:S(2)}, u32[]{:S(2)}) collective-permute-start(bf16[64,1024]{1,0:T(8,128)(2,1)S(1)} %collective-permute-done.3), channel_id=1, source_target_pairs={{0,4},{4,8},{8,12},{12,14},{14,10},{10,6},{6,2},{2,0},{1,5},{5,9},... | collective-permute-start | bytes 393224 | tf_op jit(solution)/shard_map/ppermute | solution.py:46
  12.3 7.2 %collective-permute-start.2 = (bf16[64,1024]{1,0:T(8,128)(2,1)S(1)}, bf16[64,1024]{1,0:T(8,128)(2,1)S(1)}, u32[]{:S(2)}, u32[]{:S(2)}) collective-permute-start(bf16[64,1024]{1,0:T(8,128)(2,1)S(1)} %collective-permute-done.1), channel_id=1, source_target_pairs={{0,2},{4,0},{8,4},{12,8},{14,12},{10,14},{6,10},{2,6},{1,3},{5,1},... | collective-permute-start | bytes 393224 | tf_op jit(solution)/shard_map/ppermute | solution.py:50
  14.2 5.1 %collective-permute-start.5 = (bf16[64,1024]{1,0:T(8,128)(2,1)S(1)}, bf16[64,1024]{1,0:T(8,128)(2,1)S(1)}, u32[]{:S(2)}, u32[]{:S(2)}) collective-permute-start(bf16[64,1024]{1,0:T(8,128)(2,1)S(1)} %collective-permute-done.4), channel_id=1, source_target_pairs={{0,4},{4,8},{8,12},{12,14},{14,10},{10,6},{6,2},{2,0},{1,5},{5,9},... | collective-permute-start | bytes 393224 | tf_op jit(solution)/shard_map/ppermute | solution.py:46
  19.3 5.0 %collective-permute-start.6 = (bf16[64,1024]{1,0:T(8,128)(2,1)S(1)}, bf16[64,1024]{1,0:T(8,128)(2,1)S(1)}, u32[]{:S(2)}, u32[]{:S(2)}) collective-permute-start(bf16[64,1024]{1,0:T(8,128)(2,1)S(1)} %collective-permute-done.5), channel_id=1, source_target_pairs={{0,4},{4,8},{8,12},{12,14},{14,10},{10,6},{6,2},{2,0},{1,5},{5,9},... | collective-permute-start | bytes 393224 | tf_op jit(solution)/shard_map/ppermute | solution.py:46
  28.7 2.9 %collective-permute-start.7 = (bf16[8,64,1024]{2,1,0:T(8,128)(2,1)S(1)}, bf16[8,64,1024]{2,1,0:T(8,128)(2,1)}, u32[]{:S(2)}, u32[]{:S(2)}) collective-permute-start(bf16[8,64,1024]{2,1,0:T(8,128)(2,1)S(1)} %gather_fusion), channel_id=1, source_target_pairs={{0,1},{1,0},{2,3},{3,2},{4,5},{5,4},{6,7},{7,6},{8,9},{9,8},{10,11... | collective-permute-start | bytes 3145736 | tf_op jit(solution)/shard_map/ppermute | solution.py:30
  33.1 3.8 %copy-start.3 = (bf16[8,128,1024]{2,1,0:T(8,128)(2,1)}, bf16[8,128,1024]{2,1,0:T(8,128)(2,1)S(1)}, u32[]{:S(2)}) copy-start(bf16[8,128,1024]{2,1,0:T(8,128)(2,1)S(1)} %pad_maximum_fusion) | copy-start | bytes 6291460
  33.1 4.0 %copy-start.2 = (s32[8]{0:T(128)S(1)}, s32[8]{0:T(128)}, u32[]{:S(2)}) copy-start(s32[8]{0:T(128)} %constant.42.clone) | copy-start | bytes 100
  33.2 4.6 %copy-start.1 = (s32[8]{0:T(128)S(1)}, s32[8]{0:T(128)}, u32[]{:S(2)}) copy-start(s32[8]{0:T(128)} %param.12) | copy-start | bytes 100
  33.2 5.3 %copy-start.5 = (s32[2,2]{1,0:T(2,128)S(1)}, s32[2,2]{1,0:T(2,128)}, u32[]{:S(2)}) copy-start(s32[2,2]{1,0:T(2,128)} %param.10) | copy-start | bytes 52
  36.9 6.8 %collective-permute-start.8 = (bf16[2,1024,512]{2,1,0:T(8,128)(2,1)}, bf16[2,1024,512]{2,1,0:T(8,128)(2,1)}, u32[]{:S(2)}, u32[]{:S(2)}) collective-permute-start(bf16[2,1024,512]{2,1,0:T(8,128)(2,1)} %convert_bitcast_fusion), channel_id=1, source_target_pairs={{0,1},{1,0},{2,3},{3,2},{4,5},{5,4},{6,7},{7,6},{8,9},{9,8},{10,11... | collective-permute-start | bytes 6291464 | tf_op jit(solution)/shard_map/ppermute | solution.py:73
  49.0 1.0 %copy-start.4 = (bf16[2,256,512]{2,1,0:T(8,128)(2,1)S(1)}, bf16[2,256,512]{2,1,0:T(8,128)(2,1)}, u32[]{:S(2)}) copy-start(bf16[2,256,512]{2,1,0:T(8,128)(2,1)} %param.11) | copy-start | bytes 1572868
  50.5 5.8 %collective-permute-start.9 = (f32[128,256]{0,1:T(8,128)S(1)}, f32[128,256]{0,1:T(8,128)S(1)}, u32[]{:S(2)}, u32[]{:S(2)}) collective-permute-start(f32[128,256]{0,1:T(8,128)S(1)} %slice.106), channel_id=1, source_target_pairs={{0,4},{4,8},{8,12},{12,14},{14,10},{10,6},{6,2},{2,0},{1,5},{5,9},... | collective-permute-start | bytes 393224 | tf_op jit(solution)/shard_map/ppermute | solution.py:130
  51.3 6.3 %collective-permute-start.16 = (f32[128,256]{0,1:T(8,128)S(1)}, f32[128,256]{0,1:T(8,128)S(1)}, u32[]{:S(2)}, u32[]{:S(2)}) collective-permute-start(f32[128,256]{0,1:T(8,128)S(1)} %slice.114), channel_id=1, source_target_pairs={{0,2},{4,0},{8,4},{12,8},{14,12},{10,14},{6,10},{2,6},{1,3},{5,1},... | collective-permute-start | bytes 393224 | tf_op jit(solution)/shard_map/ppermute | solution.py:131
  56.4 5.0 %collective-permute-start.10 = (f32[128,256]{0,1:T(8,128)S(1)}, f32[128,256]{0,1:T(8,128)S(1)}, u32[]{:S(2)}, u32[]{:S(2)}) collective-permute-start(f32[128,256]{0,1:T(8,128)S(1)} %slice_add_fusion.13), channel_id=1, source_target_pairs={{0,4},{4,8},{8,12},{12,14},{14,10},{10,6},{6,2},{2,0},{1,5},{5,9},... | collective-permute-start | bytes 393224 | tf_op jit(solution)/shard_map/ppermute | solution.py:130
  57.6 5.0 %collective-permute-start.17 = (f32[128,256]{0,1:T(8,128)S(1)}, f32[128,256]{0,1:T(8,128)S(1)}, u32[]{:S(2)}, u32[]{:S(2)}) collective-permute-start(f32[128,256]{0,1:T(8,128)S(1)} %slice_add_fusion.6), channel_id=1, source_target_pairs={{0,2},{4,0},{8,4},{12,8},{14,12},{10,14},{6,10},{2,6},{1,3},{5,1},... | collective-permute-start | bytes 393224 | tf_op jit(solution)/shard_map/ppermute | solution.py:131
  61.4 5.1 %collective-permute-start.11 = (f32[128,256]{0,1:T(8,128)S(1)}, f32[128,256]{0,1:T(8,128)S(1)}, u32[]{:S(2)}, u32[]{:S(2)}) collective-permute-start(f32[128,256]{0,1:T(8,128)S(1)} %slice_add_fusion.12), channel_id=1, source_target_pairs={{0,4},{4,8},{8,12},{12,14},{14,10},{10,6},{6,2},{2,0},{1,5},{5,9},... | collective-permute-start | bytes 393224 | tf_op jit(solution)/shard_map/ppermute | solution.py:130
  62.7 5.0 %collective-permute-start.18 = (f32[128,256]{0,1:T(8,128)S(1)}, f32[128,256]{0,1:T(8,128)S(1)}, u32[]{:S(2)}, u32[]{:S(2)}) collective-permute-start(f32[128,256]{0,1:T(8,128)S(1)} %slice_add_fusion.5), channel_id=1, source_target_pairs={{0,2},{4,0},{8,4},{12,8},{14,12},{10,14},{6,10},{2,6},{1,3},{5,1},... | collective-permute-start | bytes 393224 | tf_op jit(solution)/shard_map/ppermute | solution.py:131
  66.6 6.1 %collective-permute-start.12 = (f32[128,256]{0,1:T(8,128)S(1)}, f32[128,256]{0,1:T(8,128)S(1)}, u32[]{:S(2)}, u32[]{:S(2)}) collective-permute-start(f32[128,256]{0,1:T(8,128)S(1)} %slice_add_fusion.11), channel_id=1, source_target_pairs={{0,4},{4,8},{8,12},{12,14},{14,10},{10,6},{6,2},{2,0},{1,5},{5,9},... | collective-permute-start | bytes 393224 | tf_op jit(solution)/shard_map/ppermute | solution.py:130
  67.7 5.7 %collective-permute-start.19 = (f32[128,256]{0,1:T(8,128)S(1)}, f32[128,256]{0,1:T(8,128)S(1)}, u32[]{:S(2)}, u32[]{:S(2)}) collective-permute-start(f32[128,256]{0,1:T(8,128)S(1)} %slice_add_fusion.4), channel_id=1, source_target_pairs={{0,2},{4,0},{8,4},{12,8},{14,12},{10,14},{6,10},{2,6},{1,3},{5,1},... | collective-permute-start | bytes 393224 | tf_op jit(solution)/shard_map/ppermute | solution.py:131
  72.8 5.9 %collective-permute-start.13 = (f32[128,256]{0,1:T(8,128)S(1)}, f32[128,256]{0,1:T(8,128)S(1)}, u32[]{:S(2)}, u32[]{:S(2)}) collective-permute-start(f32[128,256]{0,1:T(8,128)S(1)} %slice_add_fusion.10), channel_id=1, source_target_pairs={{0,4},{4,8},{8,12},{12,14},{14,10},{10,6},{6,2},{2,0},{1,5},{5,9},... | collective-permute-start | bytes 393224 | tf_op jit(solution)/shard_map/ppermute | solution.py:130
  73.4 6.1 %collective-permute-start.20 = (f32[128,256]{0,1:T(8,128)S(1)}, f32[128,256]{0,1:T(8,128)S(1)}, u32[]{:S(2)}, u32[]{:S(2)}) collective-permute-start(f32[128,256]{0,1:T(8,128)S(1)} %slice_add_fusion.3), channel_id=1, source_target_pairs={{0,2},{4,0},{8,4},{12,8},{14,12},{10,14},{6,10},{2,6},{1,3},{5,1},... | collective-permute-start | bytes 393224 | tf_op jit(solution)/shard_map/ppermute | solution.py:131
  78.6 5.0 %collective-permute-start.14 = (f32[128,256]{0,1:T(8,128)S(1)}, f32[128,256]{0,1:T(8,128)S(1)}, u32[]{:S(2)}, u32[]{:S(2)}) collective-permute-start(f32[128,256]{0,1:T(8,128)S(1)} %slice_add_fusion.9), channel_id=1, source_target_pairs={{0,4},{4,8},{8,12},{12,14},{14,10},{10,6},{6,2},{2,0},{1,5},{5,9},... | collective-permute-start | bytes 393224 | tf_op jit(solution)/shard_map/ppermute | solution.py:130
  79.6 5.2 %collective-permute-start.21 = (f32[128,256]{0,1:T(8,128)S(1)}, f32[128,256]{0,1:T(8,128)S(1)}, u32[]{:S(2)}, u32[]{:S(2)}) collective-permute-start(f32[128,256]{0,1:T(8,128)S(1)} %slice_add_fusion.2), channel_id=1, source_target_pairs={{0,2},{4,0},{8,4},{12,8},{14,12},{10,14},{6,10},{2,6},{1,3},{5,1},... | collective-permute-start | bytes 393224 | tf_op jit(solution)/shard_map/ppermute | solution.py:131
  83.7 5.0 %collective-permute-start.15 = (f32[128,256]{0,1:T(8,128)S(1)}, f32[128,256]{0,1:T(8,128)S(1)}, u32[]{:S(2)}, u32[]{:S(2)}) collective-permute-start(f32[128,256]{0,1:T(8,128)S(1)} %slice_add_fusion.8), channel_id=1, source_target_pairs={{0,4},{4,8},{8,12},{12,14},{14,10},{10,6},{6,2},{2,0},{1,5},{5,9},... | collective-permute-start | bytes 393224 | tf_op jit(solution)/shard_map/ppermute | solution.py:130
  84.8 5.0 %collective-permute-start.22 = (f32[128,256]{0,1:T(8,128)S(1)}, f32[128,256]{0,1:T(8,128)S(1)}, u32[]{:S(2)}, u32[]{:S(2)}) collective-permute-start(f32[128,256]{0,1:T(8,128)S(1)} %slice_add_fusion.1), channel_id=1, source_target_pairs={{0,2},{4,0},{8,4},{12,8},{14,12},{10,14},{6,10},{2,6},{1,3},{5,1},... | collective-permute-start | bytes 393224 | tf_op jit(solution)/shard_map/ppermute | solution.py:131

commit v4 on v3

--- a/solution.py
+++ b/solution.py
@@ -49,10 +49,14 @@
     for _ in range(nl):
         cur = lax.ppermute(cur, "vec", left)
         lb.append(cur)
-    stacked = jnp.stack([x] + lb + rb[::-1])
+    got = [x] + lb + rb[::-1]
     pos_of = jnp.asarray(np.argsort(np.array(ring)).astype(np.int32))
     pos = pos_of[lax.axis_index("vec")]
-    return jnp.take(stacked, (pos_of - pos) % n, axis=0, mode="clip")
+    offset = ((pos_of - pos) % n)[:, None, None]
+    out = jnp.zeros((n,) + x.shape, x.dtype)
+    for d, block in enumerate(got):
+        out = jnp.where(offset == d, block[None], out)
+    return out
 
 
 def make(mesh):

time: 91.1 us -> 88.5 us (0.971)
  local copies, waits for them, and re-layouts: 14.4 us -> 6.43 us
  starting transfers between devices: 19.4 us -> 24.2 us
  other arithmetic: 3.3 us -> 6.25 us
  waiting for transfers between devices: 39.4 us -> 36.9 us
    ppermute x7, starting transfers between devices: 2.22 us -> 11.1 us  [per_device(): acc_r = lax.ppermute(acc_r, 'vec', right) + part_r[k]]
    ppermute x4, starting transfers between devices: 0.68 us -> 8.72 us  [ring_all_gather(): cur = lax.ppermute(cur, 'vec', right)]
    ppermute x3, starting transfers between devices: 6.79 us -> 0.52 us  [ring_all_gather(): cur = lax.ppermute(cur, 'vec', left)]
    ppermute x7, starting transfers between devices: 9.47 us -> 3.68 us  [per_device(): lax.ppermute(acc_l, 'vec', left) + part_l[n - 2 - k if k < n - 1 else n - 1]]
    unnamed x20 -> x33, local copies, waits for them, and re-layouts: 6.57 us -> 1.08 us
    ppermute x7, waiting for transfers between devices: 5.28 us -> 2.02 us  [per_device(): lax.ppermute(acc_l, 'vec', left) + part_l[n - 2 - k if k < n - 1 else n - 1]]
    gather x1 -> x0, local copies, waits for them, and re-layouts: 1.84 us -> none  [ring_all_gather(): return jnp.take(stacked, (pos_of - pos) % n, axis=0, mode='clip')]
    ppermute x3, waiting for transfers between devices: 2.27 us -> 0.9 us  [ring_all_gather(): cur = lax.ppermute(cur, 'vec', left)]
  transfers between devices with their start and end apart: 23 -> 23, of which waited for: 18 -> 18; matrix products, arithmetic and copies ran while one was open for 15% -> 11% of each run, Pallas kernels for 0% -> 0%
where the time goes in v4:
time: 88.5 us; the launch traced here: 88.1 us
  waiting for transfers between devices  36.9 us (42%)
  starting transfers between devices  24.2 us (27%)
  matrix products  13.3 us (15%)
  local copies, waits for them, and re-layouts  6.43 us (7%)
  other arithmetic  6.25 us (7%)
  between operations  0.99 us (1%)
    ppermute x7, waiting for transfers between devices, per_device(): acc_r = lax.ppermute(acc_r, 'vec', right) + part_r[k]  22.6 us
    ppermute x7, starting transfers between devices, per_device(): acc_r = lax.ppermute(acc_r, 'vec', right) + part_r[k]  11.1 us
    ppermute x4, waiting for transfers between devices, ring_all_gather(): cur = lax.ppermute(cur, 'vec', right)  9.21 us
    ppermute x4, starting transfers between devices, ring_all_gather(): cur = lax.ppermute(cur, 'vec', right)  8.72 us
    dot_general x1, matrix products, per_device(): jnp.einsum('sp,gsr->gpr', whole, vectors, preferred_element_type=jnp.floa...  3.78 us
    ppermute x7, starting transfers between devices, per_device(): lax.ppermute(acc_l, 'vec', left) + part_l[n - 2 - k if k < n - 1 else n - 1]  3.68 us
    dot_general x1, matrix products, per_device(): jnp.einsum('gpr,grj->gpj', other_half, theirs, preferred_element_type=jnp...  3.33 us
    dot_general x1, matrix products, per_device(): jnp.einsum('rc,gcj->grj', whole, onehot, preferred_element_type=jnp.float32)  2.88 us
  transfers between devices with their start and end apart: 23, of which 18 were waited for; matrix products, arithmetic and copies ran while one was open for 11% of the time, Pallas kernels for 0%

profile of v4, /device:TPU:0, one launch (start us, length us, event | category | flops | bytes accessed | tf_op | source)
XLA Modules:
  0.0 88.1 jit_solution(10084108949741410929)
XLA Ops:
  0.0 3.1 %collective-permute-start = (bf16[64,1024]{1,0:T(8,128)(2,1)}, bf16[64,1024]{1,0:T(8,128)(2,1)S(1)}, u32[]{:S(2)}, u32[]{:S(2)}) collective-permute-start(bf16[64,1024]{1,0:T(8,128)(2,1)} %param.9), channel_id=1, source_target_pairs={{0,4},{4,8},{8,12},{12,14},{14,10},{10,6},{6,2},{2,0},{1,5},{5,9},... | collective-permute-start | bytes 393224 | tf_op jit(solution)/shard_map/ppermute | solution.py:46
  3.1 3.6 %collective-permute-done = bf16[64,1024]{1,0:T(8,128)(2,1)S(1)} collective-permute-done((bf16[64,1024]{1,0:T(8,128)(2,1)}, bf16[64,1024]{1,0:T(8,128)(2,1)S(1)}, u32[]{:S(2)}, u32[]{:S(2)}) %collective-permute-start) | collective-permute-done | bytes 131104 | tf_op jit(solution)/shard_map/ppermute | solution.py:46
  6.7 1.8 %collective-permute-start.1 = (bf16[64,1024]{1,0:T(8,128)(2,1)S(1)}, bf16[64,1024]{1,0:T(8,128)(2,1)S(1)}, u32[]{:S(2)}, u32[]{:S(2)}) collective-permute-start(bf16[64,1024]{1,0:T(8,128)(2,1)S(1)} %collective-permute-done), channel_id=1, source_target_pairs={{0,4},{4,8},{8,12},{12,14},{14,10},{10,6},{6,2},{2,0},{1,5},{5,9},... | collective-permute-start | bytes 393224 | tf_op jit(solution)/shard_map/ppermute | solution.py:46
  8.5 1.3 %dynamic_slice.6 = s32[1]{0:T(128)} dynamic-slice(s32[8]{0:T(128)} %constant.57.clone, s32[]{:T(128)S(6)} %select_n.92), dynamic_slice_sizes={1} | dynamic-slice | bytes 12 | tf_op jit(solution)/shard_map/dynamic_slice | solution.py:54
  9.8 0.2 collective-permute-start.5
  10.0 1.7 %collective-permute-done.1 = bf16[64,1024]{1,0:T(8,128)(2,1)S(1)} collective-permute-done((bf16[64,1024]{1,0:T(8,128)(2,1)S(1)}, bf16[64,1024]{1,0:T(8,128)(2,1)S(1)}, u32[]{:S(2)}, u32[]{:S(2)}) %collective-permute-start.1) | collective-permute-done | bytes 131104 | tf_op jit(solution)/shard_map/ppermute | solution.py:46
  11.7 1.8 %collective-permute-start.2 = (bf16[64,1024]{1,0:T(8,128)(2,1)S(1)}, bf16[64,1024]{1,0:T(8,128)(2,1)S(1)}, u32[]{:S(2)}, u32[]{:S(2)}) collective-permute-start(bf16[64,1024]{1,0:T(8,128)(2,1)S(1)} %collective-permute-done.1), channel_id=1, source_target_pairs={{0,4},{4,8},{8,12},{12,14},{14,10},{10,6},{6,2},{2,0},{1,5},{5,9},... | collective-permute-start | bytes 393224 | tf_op jit(solution)/shard_map/ppermute | solution.py:46
  13.5 1.3 %broadcast_compare_fusion.6 = (pred[8]{0:T(512)(128)(4,1)S(1)}, s32[8]{0:T(128)S(1)}) fusion(s32[8]{0:T(128)} %constant.57.clone, s32[]{:T(128)} %bitcast), kind=kLoop, calls=%fused_computation.67 | loop fusion | flops 104 | bytes 76 | tf_op jit(solution)/shard_map/eq | solution.py:58
  14.8 0.0 collective-permute-done.5
  14.8 0.0 copy-start.7
  14.8 0.3 collective-permute-start.6
  15.1 1.7 %collective-permute-done.2 = bf16[64,1024]{1,0:T(8,128)(2,1)S(1)} collective-permute-done((bf16[64,1024]{1,0:T(8,128)(2,1)S(1)}, bf16[64,1024]{1,0:T(8,128)(2,1)S(1)}, u32[]{:S(2)}, u32[]{:S(2)}) %collective-permute-start.2) | collective-permute-done | bytes 131104 | tf_op jit(solution)/shard_map/ppermute | solution.py:46
  16.8 2.1 %collective-permute-start.3 = (bf16[64,1024]{1,0:T(8,128)(2,1)S(1)}, bf16[64,1024]{1,0:T(8,128)(2,1)S(1)}, u32[]{:S(2)}, u32[]{:S(2)}) collective-permute-start(bf16[64,1024]{1,0:T(8,128)(2,1)S(1)} %collective-permute-done.2), channel_id=1, source_target_pairs={{0,4},{4,8},{8,12},{12,14},{14,10},{10,6},{6,2},{2,0},{1,5},{5,9},... | collective-permute-start | bytes 393224 | tf_op jit(solution)/shard_map/ppermute | solution.py:46
  18.9 0.9 %collective-permute-done.6 = bf16[64,1024]{1,0:T(8,128)(2,1)S(1)} collective-permute-done((bf16[64,1024]{1,0:T(8,128)(2,1)S(1)}, bf16[64,1024]{1,0:T(8,128)(2,1)S(1)}, u32[]{:S(2)}, u32[]{:S(2)}) %collective-permute-start.6) | collective-permute-done | bytes 131104 | tf_op jit(solution)/shard_map/ppermute | solution.py:50
  19.8 2.2 %collective-permute-done.3 = bf16[64,1024]{1,0:T(8,128)(2,1)S(1)} collective-permute-done((bf16[64,1024]{1,0:T(8,128)(2,1)S(1)}, bf16[64,1024]{1,0:T(8,128)(2,1)S(1)}, u32[]{:S(2)}, u32[]{:S(2)}) %collective-permute-start.3) | collective-permute-done | bytes 131104 | tf_op jit(solution)/shard_map/ppermute | solution.py:46
  22.0 2.5 %select_select_fusion = bf16[8,64,1024]{2,1,0:T(8,128)(2,1)} fusion(pred[8]{0:T(512)(128)(4,1)S(1)} %get-tuple-element.15, pred[8]{0:T(512)(128)(4,1)S(1)} %get-tuple-element.10, pred[8]{0:T(512)(128)(4,1)S(1)} %get-tuple-element.11, pred[8]{0:T(512)(128)(4,1)S(1)} %get-tuple-element.12, pred[8]{0:T(512)(128)(4,1)S(1)} %get-tuple-element.13, ...), kind=kLoop, calls=%fused_computation.13 | loop fusion | flops 4194304 | bytes 2097216 | tf_op jit(solution)/shard_map/jit(_where)/select_n | solution.py:58
  24.6 0.1 collective-permute-start.7
  25.3 2.2 %collective-permute-done.7 = bf16[8,64,1024]{2,1,0:T(8,128)(2,1)S(1)} collective-permute-done((bf16[8,64,1024]{2,1,0:T(8,128)(2,1)}, bf16[8,64,1024]{2,1,0:T(8,128)(2,1)S(1)}, u32[]{:S(2)}, u32[]{:S(2)}) %collective-permute-start.7) | collective-permute-done | bytes 1048608 | tf_op jit(solution)/shard_map/ppermute | solution.py:30
  27.5 1.8 %broadcast_select_fusion.1 = (bf16[8,64,1024]{2,1,0:T(8,128)(2,1)S(1)}, bf16[8,64,1024]{2,1,0:T(8,128)(2,1)S(1)}) fusion(bf16[8,64,1024]{2,1,0:T(8,128)(2,1)S(1)} %collective-permute-done.7, pred[]{:T(512)S(6)} %eq.52, bf16[64,1024]{1,0:T(8,128)(2,1)S(1)} %copy-done.5, pred[8]{0:T(512)(128)(4,1)} %copy-done.14, ...), kind=kLoop, calls=%fused_computation.15 | loop fusion | flops 5242880 | bytes 4194369 | tf_op jit(solution)/shard_map/jit(_where)/select_n | solution.py:32
  29.3 0.2 pad_maximum_fusion
  29.5 0.0 copy-start.2
  29.5 0.0 copy-start.1
  29.5 0.0 copy-start.15
  29.5 3.8 %convert_bitcast_fusion = bf16[2,1024,512]{2,1,0:T(8,128)(2,1)} fusion(bf16[1024,1024,1]{1,0,2:T(8,128)(2,1)S(1)} %bitcast.42, bf16[2,1024,512]{2,1,0:T(8,128)(2,1)S(1)} %copy-done), kind=kOutput, calls=%fused_computation.6 | convolution fusion | flops 2148532224 | bytes 6291456 | tf_op jit(solution)/shard_map/sp,gsr->gpr/dot_general | solution.py:74
  33.3 0.1 collective-permute-start.8
  33.5 0.6 gather_fusion
  34.2 0.6 gather_fusion.1
  34.9 0.1 broadcast_bitcast_fusion
  34.9 2.9 %fusion.2 = bf16[2,1024,256]{1,2,0:T(8,128)(2,1)S(1)} fusion(bf16[1024,1024,1]{1,0,2:T(8,128)(2,1)} %bitcast.43, s32[2,256]{1,0:T(2,128)S(1)} %bitcast_add_fusion), kind=kOutput, calls=%fused_computation.9 | convolution fusion | flops 1074790400 | bytes 3147776 | tf_op jit(solution)/shard_map/rc,gcj->grj/dot_general | solution.py:85
  37.8 2.3 %fusion.5 = f32[2,1024,256]{2,1,0:T(8,128)S(1)} fusion(bf16[2,1024,512]{2,1,0:T(8,128)(2,1)} %convert_bitcast_fusion, pred[]{:T(512)S(6)} %eq.52, bf16[2,1024,256]{1,2,0:T(8,128)(2,1)S(1)} %fusion.2), kind=kOutput, calls=%fused_computation.17 | convolution fusion | flops 537133056 | bytes 5242881 | tf_op jit(solution)/shard_map/gpr,grj->gpj/dot_general | solution.py:94
  40.2 3.3 %add_convert_fusion = bf16[2,1024,256]{2,1,0:T(8,128)(2,1)} fusion(f32[2,1024,256]{2,1,0:T(8,128)S(1)} %fusion.5, bf16[2,1024,512]{2,1,0:T(8,128)(2,1)} %collective-permute-done.8, pred[]{:T(512)S(6)} %eq.52, bf16[2,1024,256]{1,2,0:T(8,128)(2,1)S(1)} %fusion.2), kind=kOutput, calls=%fused_computation.4 | convolution fusion | flops 538181632 | bytes 6291457 | tf_op jit(solution)/shard_map/gpr,grj->gpj/dot_general | solution.py:95
  43.5 1.8 %gather_fusion.2 = bf16[8,2,128,256]{3,2,1,0:T(8,128)(2,1)S(1)} fusion(bf16[2,8,128,256]{3,2,1,0:T(8,128)(2,1)} %bitcast.41, s32[1024]{0:T(1024)S(1)} %pad_clamp_fusion), kind=kCustom, calls=%fused_computation.2 | custom fusion | bytes 2097184 | tf_op jit(solution)/shard_map/jit(_take)/gather | solution.py:118
  45.4 0.0 copy-start.4
  45.4 0.1 copy.43
  45.5 0.9 %copy-done.4 = bf16[2,256,512]{2,1,0:T(8,128)(2,1)S(1)} copy-done((bf16[2,256,512]{2,1,0:T(8,128)(2,1)S(1)}, bf16[2,256,512]{2,1,0:T(8,128)(2,1)}, u32[]{:S(2)}) %copy-start.4) | copy-done | bytes 524312
  46.4 0.5 convolution_bitcast_fusion.1
  46.9 1.9 %collective-permute-start.9 = (f32[128,256]{0,1:T(8,128)S(1)}, f32[128,256]{0,1:T(8,128)S(1)}, u32[]{:S(2)}, u32[]{:S(2)}) collective-permute-start(f32[128,256]{0,1:T(8,128)S(1)} %slice.104), channel_id=1, source_target_pairs={{0,4},{4,8},{8,12},{12,14},{14,10},{10,6},{6,2},{2,0},{1,5},{5,9},... | collective-permute-start | bytes 393224 | tf_op jit(solution)/shard_map/ppermute | solution.py:134
  48.8 0.5 convolution_bitcast_fusion
  49.3 0.2 collective-permute-start.16
  49.6 3.5 %collective-permute-done.9 = f32[128,256]{0,1:T(8,128)S(1)} collective-permute-done((f32[128,256]{0,1:T(8,128)S(1)}, f32[128,256]{0,1:T(8,128)S(1)}, u32[]{:S(2)}, u32[]{:S(2)}) %collective-permute-start.9) | collective-permute-done | bytes 131104 | tf_op jit(solution)/shard_map/ppermute | solution.py:134
  53.1 1.6 %collective-permute-start.10 = (f32[128,256]{0,1:T(8,128)S(1)}, f32[128,256]{0,1:T(8,128)S(1)}, u32[]{:S(2)}, u32[]{:S(2)}) collective-permute-start(f32[128,256]{0,1:T(8,128)S(1)} %slice_add_fusion.13), channel_id=1, source_target_pairs={{0,4},{4,8},{8,12},{12,14},{14,10},{10,6},{6,2},{2,0},{1,5},{5,9},... | collective-permute-start | bytes 393224 | tf_op jit(solution)/shard_map/ppermute | solution.py:134
  54.7 0.2 collective-permute-done.16
  54.9 0.5 collective-permute-start.17
  55.4 2.9 %collective-permute-done.10 = f32[128,256]{0,1:T(8,128)S(1)} collective-permute-done((f32[128,256]{0,1:T(8,128)S(1)}, f32[128,256]{0,1:T(8,128)S(1)}, u32[]{:S(2)}, u32[]{:S(2)}) %collective-permute-start.10) | collective-permute-done | bytes 131104 | tf_op jit(solution)/shard_map/ppermute | solution.py:134
  58.3 1.4 %collective-permute-start.11 = (f32[128,256]{0,1:T(8,128)S(1)}, f32[128,256]{0,1:T(8,128)S(1)}, u32[]{:S(2)}, u32[]{:S(2)}) collective-permute-start(f32[128,256]{0,1:T(8,128)S(1)} %slice_add_fusion.12), channel_id=1, source_target_pairs={{0,4},{4,8},{8,12},{12,14},{14,10},{10,6},{6,2},{2,0},{1,5},{5,9},... | collective-permute-start | bytes 393224 | tf_op jit(solution)/shard_map/ppermute | solution.py:134
  59.7 0.2 collective-permute-done.17
  60.0 0.5 collective-permute-start.18
  60.5 2.9 %collective-permute-done.11 = f32[128,256]{0,1:T(8,128)S(1)} collective-permute-done((f32[128,256]{0,1:T(8,128)S(1)}, f32[128,256]{0,1:T(8,128)S(1)}, u32[]{:S(2)}, u32[]{:S(2)}) %collective-permute-start.11) | collective-permute-done | bytes 131104 | tf_op jit(solution)/shard_map/ppermute | solution.py:134
  63.4 1.5 %collective-permute-start.12 = (f32[128,256]{0,1:T(8,128)S(1)}, f32[128,256]{0,1:T(8,128)S(1)}, u32[]{:S(2)}, u32[]{:S(2)}) collective-permute-start(f32[128,256]{0,1:T(8,128)S(1)} %slice_add_fusion.11), channel_id=1, source_target_pairs={{0,4},{4,8},{8,12},{12,14},{14,10},{10,6},{6,2},{2,0},{1,5},{5,9},... | collective-permute-start | bytes 393224 | tf_op jit(solution)/shard_map/ppermute | solution.py:134
  64.9 0.1 collective-permute-done.18
  65.0 0.5 collective-permute-start.19
  65.6 3.5 %collective-permute-done.12 = f32[128,256]{0,1:T(8,128)S(1)} collective-permute-done((f32[128,256]{0,1:T(8,128)S(1)}, f32[128,256]{0,1:T(8,128)S(1)}, u32[]{:S(2)}, u32[]{:S(2)}) %collective-permute-start.12) | collective-permute-done | bytes 131104 | tf_op jit(solution)/shard_map/ppermute | solution.py:134
  69.1 1.8 %collective-permute-start.13 = (f32[128,256]{0,1:T(8,128)S(1)}, f32[128,256]{0,1:T(8,128)S(1)}, u32[]{:S(2)}, u32[]{:S(2)}) collective-permute-start(f32[128,256]{0,1:T(8,128)S(1)} %slice_add_fusion.10), channel_id=1, source_target_pairs={{0,4},{4,8},{8,12},{12,14},{14,10},{10,6},{6,2},{2,0},{1,5},{5,9},... | collective-permute-start | bytes 393224 | tf_op jit(solution)/shard_map/ppermute | solution.py:134
  70.9 0.1 collective-permute-done.19
  71.0 0.5 collective-permute-start.20
  71.5 3.9 %collective-permute-done.13 = f32[128,256]{0,1:T(8,128)S(1)} collective-permute-done((f32[128,256]{0,1:T(8,128)S(1)}, f32[128,256]{0,1:T(8,128)S(1)}, u32[]{:S(2)}, u32[]{:S(2)}) %collective-permute-start.13) | collective-permute-done | bytes 131104 | tf_op jit(solution)/shard_map/ppermute | solution.py:134
  75.5 1.5 %collective-permute-start.14 = (f32[128,256]{0,1:T(8,128)S(1)}, f32[128,256]{0,1:T(8,128)S(1)}, u32[]{:S(2)}, u32[]{:S(2)}) collective-permute-start(f32[128,256]{0,1:T(8,128)S(1)} %slice_add_fusion.9), channel_id=1, source_target_pairs={{0,4},{4,8},{8,12},{12,14},{14,10},{10,6},{6,2},{2,0},{1,5},{5,9},... | collective-permute-start | bytes 393224 | tf_op jit(solution)/shard_map/ppermute | solution.py:134
  77.0 0.6 collective-permute-start.21
  77.6 3.1 %collective-permute-done.14 = f32[128,256]{0,1:T(8,128)S(1)} collective-permute-done((f32[128,256]{0,1:T(8,128)S(1)}, f32[128,256]{0,1:T(8,128)S(1)}, u32[]{:S(2)}, u32[]{:S(2)}) %collective-permute-start.14) | collective-permute-done | bytes 131104 | tf_op jit(solution)/shard_map/ppermute | solution.py:134
  80.8 1.4 %collective-permute-start.15 = (f32[128,256]{0,1:T(8,128)S(1)}, f32[128,256]{0,1:T(8,128)S(1)}, u32[]{:S(2)}, u32[]{:S(2)}) collective-permute-start(f32[128,256]{0,1:T(8,128)S(1)} %slice_add_fusion.8), channel_id=1, source_target_pairs={{0,4},{4,8},{8,12},{12,14},{14,10},{10,6},{6,2},{2,0},{1,5},{5,9},... | collective-permute-start | bytes 393224 | tf_op jit(solution)/shard_map/ppermute | solution.py:134
  82.2 0.8 collective-permute-start.22
  83.0 2.9 %collective-permute-done.15 = f32[128,256]{0,1:T(8,128)S(1)} collective-permute-done((f32[128,256]{0,1:T(8,128)S(1)}, f32[128,256]{0,1:T(8,128)S(1)}, u32[]{:S(2)}, u32[]{:S(2)}) %collective-permute-start.15) | collective-permute-done | bytes 131104 | tf_op jit(solution)/shard_map/ppermute | solution.py:134
  85.8 1.4 %collective-permute-done.22 = f32[128,256]{0,1:T(8,128)S(1)} collective-permute-done((f32[128,256]{0,1:T(8,128)S(1)}, f32[128,256]{0,1:T(8,128)S(1)}, u32[]{:S(2)}, u32[]{:S(2)}) %collective-permute-start.22) | collective-permute-done | bytes 131104 | tf_op jit(solution)/shard_map/ppermute | solution.py:135
  87.3 0.8 copy.46
  (57 shorter events, 0.6 us)
Async XLA Ops:
  0.0 29.5 %copy-start = (bf16[2,1024,512]{2,1,0:T(8,128)(2,1)S(1)}, bf16[2,1024,512]{2,1,0:T(8,128)(2,1)}, u32[]{:S(2)}) copy-start(bf16[2,1024,512]{2,1,0:T(8,128)(2,1)} %param.8) | copy-start | bytes 6291460
  0.0 27.5 %copy-start.5 = (bf16[64,1024]{1,0:T(8,128)(2,1)S(1)}, bf16[64,1024]{1,0:T(8,128)(2,1)}, u32[]{:S(2)}) copy-start(bf16[64,1024]{1,0:T(8,128)(2,1)} %param.9) | copy-start | bytes 393220
  0.0 6.7 %collective-permute-start = (bf16[64,1024]{1,0:T(8,128)(2,1)}, bf16[64,1024]{1,0:T(8,128)(2,1)S(1)}, u32[]{:S(2)}, u32[]{:S(2)}) collective-permute-start(bf16[64,1024]{1,0:T(8,128)(2,1)} %param.9), channel_id=1, source_target_pairs={{0,4},{4,8},{8,12},{12,14},{14,10},{10,6},{6,2},{2,0},{1,5},{5,9},... | collective-permute-start | bytes 393224 | tf_op jit(solution)/shard_map/ppermute | solution.py:46
  3.1 6.7 %collective-permute-start.4 = (bf16[64,1024]{1,0:T(8,128)(2,1)}, bf16[64,1024]{1,0:T(8,128)(2,1)S(1)}, u32[]{:S(2)}, u32[]{:S(2)}) collective-permute-start(bf16[64,1024]{1,0:T(8,128)(2,1)} %param.9), channel_id=1, source_target_pairs={{0,2},{4,0},{8,4},{12,8},{14,12},{10,14},{6,10},{2,6},{1,3},{5,1},... | collective-permute-start | bytes 393224 | tf_op jit(solution)/shard_map/ppermute | solution.py:50
  6.7 5.0 %collective-permute-start.1 = (bf16[64,1024]{1,0:T(8,128)(2,1)S(1)}, bf16[64,1024]{1,0:T(8,128)(2,1)S(1)}, u32[]{:S(2)}, u32[]{:S(2)}) collective-permute-start(bf16[64,1024]{1,0:T(8,128)(2,1)S(1)} %collective-permute-done), channel_id=1, source_target_pairs={{0,4},{4,8},{8,12},{12,14},{14,10},{10,6},{6,2},{2,0},{1,5},{5,9},... | collective-permute-start | bytes 393224 | tf_op jit(solution)/shard_map/ppermute | solution.py:46
  9.8 5.0 %collective-permute-start.5 = (bf16[64,1024]{1,0:T(8,128)(2,1)S(1)}, bf16[64,1024]{1,0:T(8,128)(2,1)S(1)}, u32[]{:S(2)}, u32[]{:S(2)}) collective-permute-start(bf16[64,1024]{1,0:T(8,128)(2,1)S(1)} %collective-permute-done.4), channel_id=1, source_target_pairs={{0,2},{4,0},{8,4},{12,8},{14,12},{10,14},{6,10},{2,6},{1,3},{5,1},... | collective-permute-start | bytes 393224 | tf_op jit(solution)/shard_map/ppermute | solution.py:50
  11.7 10.3 %copy-start.6 = (bf16[64,1024]{1,0:T(8,128)(2,1)}, bf16[64,1024]{1,0:T(8,128)(2,1)S(1)}, u32[]{:S(2)}) copy-start(bf16[64,1024]{1,0:T(8,128)(2,1)S(1)} %collective-permute-done.1) | copy-start | bytes 393220
  11.7 5.1 %collective-permute-start.2 = (bf16[64,1024]{1,0:T(8,128)(2,1)S(1)}, bf16[64,1024]{1,0:T(8,128)(2,1)S(1)}, u32[]{:S(2)}, u32[]{:S(2)}) collective-permute-start(bf16[64,1024]{1,0:T(8,128)(2,1)S(1)} %collective-permute-done.1), channel_id=1, source_target_pairs={{0,4},{4,8},{8,12},{12,14},{14,10},{10,6},{6,2},{2,0},{1,5},{5,9},... | collective-permute-start | bytes 393224 | tf_op jit(solution)/shard_map/ppermute | solution.py:46
  14.8 9.8 %copy-start.7 = (bf16[64,1024]{1,0:T(8,128)(2,1)}, bf16[64,1024]{1,0:T(8,128)(2,1)S(1)}, u32[]{:S(2)}) copy-start(bf16[64,1024]{1,0:T(8,128)(2,1)S(1)} %collective-permute-done.5) | copy-start | bytes 393220
  14.8 5.0 %collective-permute-start.6 = (bf16[64,1024]{1,0:T(8,128)(2,1)S(1)}, bf16[64,1024]{1,0:T(8,128)(2,1)S(1)}, u32[]{:S(2)}, u32[]{:S(2)}) collective-permute-start(bf16[64,1024]{1,0:T(8,128)(2,1)S(1)} %collective-permute-done.5), channel_id=1, source_target_pairs={{0,2},{4,0},{8,4},{12,8},{14,12},{10,14},{6,10},{2,6},{1,3},{5,1},... | collective-permute-start | bytes 393224 | tf_op jit(solution)/shard_map/ppermute | solution.py:50
  16.8 7.7 %copy-start.8 = (bf16[64,1024]{1,0:T(8,128)(2,1)}, bf16[64,1024]{1,0:T(8,128)(2,1)S(1)}, u32[]{:S(2)}) copy-start(bf16[64,1024]{1,0:T(8,128)(2,1)S(1)} %collective-permute-done.2) | copy-start | bytes 393220
  16.8 5.2 %collective-permute-start.3 = (bf16[64,1024]{1,0:T(8,128)(2,1)S(1)}, bf16[64,1024]{1,0:T(8,128)(2,1)S(1)}, u32[]{:S(2)}, u32[]{:S(2)}) collective-permute-start(bf16[64,1024]{1,0:T(8,128)(2,1)S(1)} %collective-permute-done.2), channel_id=1, source_target_pairs={{0,4},{4,8},{8,12},{12,14},{14,10},{10,6},{6,2},{2,0},{1,5},{5,9},... | collective-permute-start | bytes 393224 | tf_op jit(solution)/shard_map/ppermute | solution.py:46
  18.9 3.1 %copy-start.11 = (pred[8]{0:T(512)(128)(4,1)}, pred[8]{0:T(512)(128)(4,1)S(1)}, u32[]{:S(2)}) copy-start(pred[8]{0:T(512)(128)(4,1)S(1)} %get-tuple-element.12) | copy-start | bytes 28
  18.9 3.1 %copy-start.12 = (pred[8]{0:T(512)(128)(4,1)}, pred[8]{0:T(512)(128)(4,1)S(1)}, u32[]{:S(2)}) copy-start(pred[8]{0:T(512)(128)(4,1)S(1)} %get-tuple-element.13) | copy-start | bytes 28
  18.9 3.1 %copy-start.13 = (pred[8]{0:T(512)(128)(4,1)}, pred[8]{0:T(512)(128)(4,1)S(1)}, u32[]{:S(2)}) copy-start(pred[8]{0:T(512)(128)(4,1)S(1)} %get-tuple-element.14) | copy-start | bytes 28
  18.9 3.1 %copy-start.14 = (pred[8]{0:T(512)(128)(4,1)}, pred[8]{0:T(512)(128)(4,1)S(1)}, u32[]{:S(2)}) copy-start(pred[8]{0:T(512)(128)(4,1)S(1)} %get-tuple-element.15) | copy-start | bytes 28
  19.8 4.7 %copy-start.9 = (bf16[64,1024]{1,0:T(8,128)(2,1)}, bf16[64,1024]{1,0:T(8,128)(2,1)S(1)}, u32[]{:S(2)}) copy-start(bf16[64,1024]{1,0:T(8,128)(2,1)S(1)} %collective-permute-done.6) | copy-start | bytes 393220
  22.0 2.6 %copy-start.10 = (bf16[64,1024]{1,0:T(8,128)(2,1)}, bf16[64,1024]{1,0:T(8,128)(2,1)S(1)}, u32[]{:S(2)}) copy-start(bf16[64,1024]{1,0:T(8,128)(2,1)S(1)} %collective-permute-done.3) | copy-start | bytes 393220
  24.6 2.9 %collective-permute-start.7 = (bf16[8,64,1024]{2,1,0:T(8,128)(2,1)}, bf16[8,64,1024]{2,1,0:T(8,128)(2,1)S(1)}, u32[]{:S(2)}, u32[]{:S(2)}) collective-permute-start(bf16[8,64,1024]{2,1,0:T(8,128)(2,1)} %select_select_fusion), channel_id=1, source_target_pairs={{0,1},{1,0},{2,3},{3,2},{4,5},{5,4},{6,7},{7,6},{8,9},{9,8},{10,11... | collective-permute-start | bytes 3145736 | tf_op jit(solution)/shard_map/ppermute | solution.py:30
  29.5 3.8 %copy-start.3 = (bf16[8,128,1024]{2,1,0:T(8,128)(2,1)}, bf16[8,128,1024]{2,1,0:T(8,128)(2,1)S(1)}, u32[]{:S(2)}) copy-start(bf16[8,128,1024]{2,1,0:T(8,128)(2,1)S(1)} %pad_maximum_fusion) | copy-start | bytes 6291460
  29.5 4.0 %copy-start.2 = (s32[8]{0:T(128)S(1)}, s32[8]{0:T(128)}, u32[]{:S(2)}) copy-start(s32[8]{0:T(128)} %constant.58.clone) | copy-start | bytes 100
  29.5 4.6 %copy-start.1 = (s32[8]{0:T(128)S(1)}, s32[8]{0:T(128)}, u32[]{:S(2)}) copy-start(s32[8]{0:T(128)} %param.12) | copy-start | bytes 100
  29.5 5.3 %copy-start.15 = (s32[2,2]{1,0:T(2,128)S(1)}, s32[2,2]{1,0:T(2,128)}, u32[]{:S(2)}) copy-start(s32[2,2]{1,0:T(2,128)} %param.10) | copy-start | bytes 52
  33.3 6.8 %collective-permute-start.8 = (bf16[2,1024,512]{2,1,0:T(8,128)(2,1)}, bf16[2,1024,512]{2,1,0:T(8,128)(2,1)}, u32[]{:S(2)}, u32[]{:S(2)}) collective-permute-start(bf16[2,1024,512]{2,1,0:T(8,128)(2,1)} %convert_bitcast_fusion), channel_id=1, source_target_pairs={{0,1},{1,0},{2,3},{3,2},{4,5},{5,4},{6,7},{7,6},{8,9},{9,8},{10,11... | collective-permute-start | bytes 6291464 | tf_op jit(solution)/shard_map/ppermute | solution.py:77
  45.4 1.0 %copy-start.4 = (bf16[2,256,512]{2,1,0:T(8,128)(2,1)S(1)}, bf16[2,256,512]{2,1,0:T(8,128)(2,1)}, u32[]{:S(2)}) copy-start(bf16[2,256,512]{2,1,0:T(8,128)(2,1)} %param.11) | copy-start | bytes 1572868
  46.9 6.1 %collective-permute-start.9 = (f32[128,256]{0,1:T(8,128)S(1)}, f32[128,256]{0,1:T(8,128)S(1)}, u32[]{:S(2)}, u32[]{:S(2)}) collective-permute-start(f32[128,256]{0,1:T(8,128)S(1)} %slice.104), channel_id=1, source_target_pairs={{0,4},{4,8},{8,12},{12,14},{14,10},{10,6},{6,2},{2,0},{1,5},{5,9},... | collective-permute-start | bytes 393224 | tf_op jit(solution)/shard_map/ppermute | solution.py:134
  49.3 5.6 %collective-permute-start.16 = (f32[128,256]{0,1:T(8,128)S(1)}, f32[128,256]{0,1:T(8,128)S(1)}, u32[]{:S(2)}, u32[]{:S(2)}) collective-permute-start(f32[128,256]{0,1:T(8,128)S(1)} %slice.112), channel_id=1, source_target_pairs={{0,2},{4,0},{8,4},{12,8},{14,12},{10,14},{6,10},{2,6},{1,3},{5,1},... | collective-permute-start | bytes 393224 | tf_op jit(solution)/shard_map/ppermute | solution.py:135
  53.1 5.3 %collective-permute-start.10 = (f32[128,256]{0,1:T(8,128)S(1)}, f32[128,256]{0,1:T(8,128)S(1)}, u32[]{:S(2)}, u32[]{:S(2)}) collective-permute-start(f32[128,256]{0,1:T(8,128)S(1)} %slice_add_fusion.13), channel_id=1, source_target_pairs={{0,4},{4,8},{8,12},{12,14},{14,10},{10,6},{6,2},{2,0},{1,5},{5,9},... | collective-permute-start | bytes 393224 | tf_op jit(solution)/shard_map/ppermute | solution.py:134
  54.9 5.0 %collective-permute-start.17 = (f32[128,256]{0,1:T(8,128)S(1)}, f32[128,256]{0,1:T(8,128)S(1)}, u32[]{:S(2)}, u32[]{:S(2)}) collective-permute-start(f32[128,256]{0,1:T(8,128)S(1)} %slice_add_fusion.6), channel_id=1, source_target_pairs={{0,2},{4,0},{8,4},{12,8},{14,12},{10,14},{6,10},{2,6},{1,3},{5,1},... | collective-permute-start | bytes 393224 | tf_op jit(solution)/shard_map/ppermute | solution.py:135
  58.3 5.0 %collective-permute-start.11 = (f32[128,256]{0,1:T(8,128)S(1)}, f32[128,256]{0,1:T(8,128)S(1)}, u32[]{:S(2)}, u32[]{:S(2)}) collective-permute-start(f32[128,256]{0,1:T(8,128)S(1)} %slice_add_fusion.12), channel_id=1, source_target_pairs={{0,4},{4,8},{8,12},{12,14},{14,10},{10,6},{6,2},{2,0},{1,5},{5,9},... | collective-permute-start | bytes 393224 | tf_op jit(solution)/shard_map/ppermute | solution.py:134
  60.0 5.0 %collective-permute-start.18 = (f32[128,256]{0,1:T(8,128)S(1)}, f32[128,256]{0,1:T(8,128)S(1)}, u32[]{:S(2)}, u32[]{:S(2)}) collective-permute-start(f32[128,256]{0,1:T(8,128)S(1)} %slice_add_fusion.5), channel_id=1, source_target_pairs={{0,2},{4,0},{8,4},{12,8},{14,12},{10,14},{6,10},{2,6},{1,3},{5,1},... | collective-permute-start | bytes 393224 | tf_op jit(solution)/shard_map/ppermute | solution.py:135
  63.4 5.6 %collective-permute-start.12 = (f32[128,256]{0,1:T(8,128)S(1)}, f32[128,256]{0,1:T(8,128)S(1)}, u32[]{:S(2)}, u32[]{:S(2)}) collective-permute-start(f32[128,256]{0,1:T(8,128)S(1)} %slice_add_fusion.11), channel_id=1, source_target_pairs={{0,4},{4,8},{8,12},{12,14},{14,10},{10,6},{6,2},{2,0},{1,5},{5,9},... | collective-permute-start | bytes 393224 | tf_op jit(solution)/shard_map/ppermute | solution.py:134
  65.0 5.9 %collective-permute-start.19 = (f32[128,256]{0,1:T(8,128)S(1)}, f32[128,256]{0,1:T(8,128)S(1)}, u32[]{:S(2)}, u32[]{:S(2)}) collective-permute-start(f32[128,256]{0,1:T(8,128)S(1)} %slice_add_fusion.4), channel_id=1, source_target_pairs={{0,2},{4,0},{8,4},{12,8},{14,12},{10,14},{6,10},{2,6},{1,3},{5,1},... | collective-permute-start | bytes 393224 | tf_op jit(solution)/shard_map/ppermute | solution.py:135
  69.1 6.4 %collective-permute-start.13 = (f32[128,256]{0,1:T(8,128)S(1)}, f32[128,256]{0,1:T(8,128)S(1)}, u32[]{:S(2)}, u32[]{:S(2)}) collective-permute-start(f32[128,256]{0,1:T(8,128)S(1)} %slice_add_fusion.10), channel_id=1, source_target_pairs={{0,4},{4,8},{8,12},{12,14},{14,10},{10,6},{6,2},{2,0},{1,5},{5,9},... | collective-permute-start | bytes 393224 | tf_op jit(solution)/shard_map/ppermute | solution.py:134
  71.0 5.9 %collective-permute-start.20 = (f32[128,256]{0,1:T(8,128)S(1)}, f32[128,256]{0,1:T(8,128)S(1)}, u32[]{:S(2)}, u32[]{:S(2)}) collective-permute-start(f32[128,256]{0,1:T(8,128)S(1)} %slice_add_fusion.3), channel_id=1, source_target_pairs={{0,2},{4,0},{8,4},{12,8},{14,12},{10,14},{6,10},{2,6},{1,3},{5,1},... | collective-permute-start | bytes 393224 | tf_op jit(solution)/shard_map/ppermute | solution.py:135
  75.5 5.3 %collective-permute-start.14 = (f32[128,256]{0,1:T(8,128)S(1)}, f32[128,256]{0,1:T(8,128)S(1)}, u32[]{:S(2)}, u32[]{:S(2)}) collective-permute-start(f32[128,256]{0,1:T(8,128)S(1)} %slice_add_fusion.9), channel_id=1, source_target_pairs={{0,4},{4,8},{8,12},{12,14},{14,10},{10,6},{6,2},{2,0},{1,5},{5,9},... | collective-permute-start | bytes 393224 | tf_op jit(solution)/shard_map/ppermute | solution.py:134
  77.0 5.2 %collective-permute-start.21 = (f32[128,256]{0,1:T(8,128)S(1)}, f32[128,256]{0,1:T(8,128)S(1)}, u32[]{:S(2)}, u32[]{:S(2)}) collective-permute-start(f32[128,256]{0,1:T(8,128)S(1)} %slice_add_fusion.2), channel_id=1, source_target_pairs={{0,2},{4,0},{8,4},{12,8},{14,12},{10,14},{6,10},{2,6},{1,3},{5,1},... | collective-permute-start | bytes 393224 | tf_op jit(solution)/shard_map/ppermute | solution.py:135
  80.8 5.0 %collective-permute-start.15 = (f32[128,256]{0,1:T(8,128)S(1)}, f32[128,256]{0,1:T(8,128)S(1)}, u32[]{:S(2)}, u32[]{:S(2)}) collective-permute-start(f32[128,256]{0,1:T(8,128)S(1)} %slice_add_fusion.8), channel_id=1, source_target_pairs={{0,4},{4,8},{8,12},{12,14},{14,10},{10,6},{6,2},{2,0},{1,5},{5,9},... | collective-permute-start | bytes 393224 | tf_op jit(solution)/shard_map/ppermute | solution.py:134
  82.2 5.0 %collective-permute-start.22 = (f32[128,256]{0,1:T(8,128)S(1)}, f32[128,256]{0,1:T(8,128)S(1)}, u32[]{:S(2)}, u32[]{:S(2)}) collective-permute-start(f32[128,256]{0,1:T(8,128)S(1)} %slice_add_fusion.1), channel_id=1, source_target_pairs={{0,2},{4,0},{8,4},{12,8},{14,12},{10,14},{6,10},{2,6},{1,3},{5,1},... | collective-permute-start | bytes 393224 | tf_op jit(solution)/shard_map/ppermute | solution.py:135

commit v5 on v4

--- a/solution.py
+++ b/solution.py
@@ -50,12 +50,15 @@
         cur = lax.ppermute(cur, "vec", left)
         lb.append(cur)
     got = [x] + lb + rb[::-1]
+    theirs = lax.ppermute(tuple(got), "orb", [(0, 1), (1, 0)])
     pos_of = jnp.asarray(np.argsort(np.array(ring)).astype(np.int32))
     pos = pos_of[lax.axis_index("vec")]
-    offset = ((pos_of - pos) % n)[:, None, None]
-    out = jnp.zeros((n,) + x.shape, x.dtype)
-    for d, block in enumerate(got):
-        out = jnp.where(offset == d, block[None], out)
+    offset = ((pos_of - pos) % n)[:, None, None, None]
+    first = lax.axis_index("orb") == 0
+    out = jnp.zeros((n, 2) + x.shape, x.dtype)
+    for d in range(n):
+        pair = jnp.where(first, jnp.stack([got[d], theirs[d]]), jnp.stack([theirs[d], got[d]]))
+        out = jnp.where(offset == d, pair[None], out)
     return out
 
 
@@ -66,8 +69,7 @@
 
     def per_device(vectors, rotation, active, factors, owner):
         if use_ring:
-            part = ring_all_gather(rotation, ring)
-            whole = swap_orb(part, 1).reshape(-1, rotation.shape[1])
+            whole = ring_all_gather(rotation, ring).reshape(-1, rotation.shape[1])
         else:
             whole = lax.all_gather(rotation, ("vec", "orb"), axis=0, tiled=True)
         orbitals = whole.shape[0]

time: 88.5 us -> 85 us (0.960)
  waiting for transfers between devices: 36.9 us -> 33.2 us
  other arithmetic: 6.25 us -> 4.93 us
  local copies, waits for them, and re-layouts: 6.43 us -> 7.69 us
    ppermute x4, waiting for transfers between devices: 9.21 us -> 3.25 us  [ring_all_gather(): cur = lax.ppermute(cur, 'vec', right)]
    ppermute x3, waiting for transfers between devices: 0.9 us -> 4.41 us  [ring_all_gather(): cur = lax.ppermute(cur, 'vec', left)]
    ppermute x7, starting transfers between devices: 11.1 us -> 12.8 us  [per_device(): acc_r = lax.ppermute(acc_r, 'vec', right) + part_r[k]]
    ppermute x7, starting transfers between devices: 3.68 us -> 2.2 us  [per_device(): lax.ppermute(acc_l, 'vec', left) + part_l[n - 2 - k if k < n - 1 else n - 1]]
    broadcast_in_dim x0 -> x16, local copies, waits for them, and re-layouts: none -> 1.32 us  [ring_all_gather(): out = jnp.where(offset == d, pair[None], out)]
    ppermute x7, waiting for transfers between devices: 22.6 us -> 21.3 us  [per_device(): acc_r = lax.ppermute(acc_r, 'vec', right) + part_r[k]]
    select_n x2 -> x9, other arithmetic: 4.32 us -> 3.17 us  [the longest x1 1.96 us: ring_all_gather(): out = jnp.where(offset == d, pair[None], out)]
    ppermute x1 -> x8, waiting for transfers between devices: 2.22 us -> 1.29 us  [ring_all_gather(): theirs = lax.ppermute(tuple(got), 'orb', [(0, 1), (1, 0)])]
  transfers between devices with their start and end apart: 23 -> 30, of which waited for: 18 -> 19; matrix products, arithmetic and copies ran while one was open for 11% -> 15% of each run, Pallas kernels for 0% -> 0%
where the time goes in v5:
time: 85 us; the launch traced here: 84.7 us
  waiting for transfers between devices  33.2 us (39%)
  starting transfers between devices  24.6 us (29%)
  matrix products  13.3 us (16%)
  local copies, waits for them, and re-layouts  7.69 us (9%)
  other arithmetic  4.93 us (6%)
  between operations  0.99 us (1%)
    ppermute x7, waiting for transfers between devices, per_device(): acc_r = lax.ppermute(acc_r, 'vec', right) + part_r[k]  21.3 us
    ppermute x7, starting transfers between devices, per_device(): acc_r = lax.ppermute(acc_r, 'vec', right) + part_r[k]  12.8 us
    ppermute x4, starting transfers between devices, ring_all_gather(): cur = lax.ppermute(cur, 'vec', right)  8.43 us
    ppermute x3, waiting for transfers between devices, ring_all_gather(): cur = lax.ppermute(cur, 'vec', left)  4.41 us
    dot_general x1, matrix products, per_device(): jnp.einsum('sp,gsr->gpr', whole, vectors, preferred_element_type=jnp.floa...  3.78 us
    dot_general x1, matrix products, per_device(): jnp.einsum('gpr,grj->gpj', other_half, theirs, preferred_element_type=jnp...  3.35 us
    ppermute x4, waiting for transfers between devices, ring_all_gather(): cur = lax.ppermute(cur, 'vec', right)  3.25 us
    ppermute x7, waiting for transfers between devices, per_device(): lax.ppermute(acc_l, 'vec', left) + part_l[n - 2 - k if k < n - 1 else n - 1]  2.9 us
  transfers between devices with their start and end apart: 30, of which 19 were waited for; matrix products, arithmetic and copies ran while one was open for 15% of the time, Pallas kernels for 0%

profile of v5, /device:TPU:0, one launch (start us, length us, event | category | flops | bytes accessed | tf_op | source)
XLA Modules:
  0.0 84.7 jit_solution(2951182675272463385)
XLA Ops:
  0.0 3.1 %collective-permute-start = (bf16[64,1024]{1,0:T(8,128)(2,1)}, bf16[64,1024]{1,0:T(8,128)(2,1)S(1)}, u32[]{:S(2)}, u32[]{:S(2)}) collective-permute-start(bf16[64,1024]{1,0:T(8,128)(2,1)} %param.9), channel_id=1, source_target_pairs={{0,4},{4,8},{8,12},{12,14},{14,10},{10,6},{6,2},{2,0},{1,5},{5,9},... | collective-permute-start | bytes 393224 | tf_op jit(solution)/shard_map/ppermute | solution.py:46
  3.1 1.2 %dynamic_slice.6 = s32[1]{0:T(128)} dynamic-slice(s32[8]{0:T(128)} %constant.57.clone, s32[]{:T(128)S(6)} %select_n.155), dynamic_slice_sizes={1} | dynamic-slice | bytes 12 | tf_op jit(solution)/shard_map/dynamic_slice | solution.py:55
  4.3 1.3 %broadcast_compare_fusion.6 = (pred[8]{0:T(512)(128)(4,1)S(1)}, s32[8]{0:T(128)S(1)}) fusion(s32[8]{0:T(128)} %constant.57.clone, s32[]{:T(128)} %bitcast), kind=kLoop, calls=%fused_computation.82 | loop fusion | flops 104 | bytes 76 | tf_op jit(solution)/shard_map/eq | solution.py:61
  5.6 1.1 %collective-permute-done = bf16[64,1024]{1,0:T(8,128)(2,1)S(1)} collective-permute-done((bf16[64,1024]{1,0:T(8,128)(2,1)}, bf16[64,1024]{1,0:T(8,128)(2,1)S(1)}, u32[]{:S(2)}, u32[]{:S(2)}) %collective-permute-start) | collective-permute-done | bytes 131104 | tf_op jit(solution)/shard_map/ppermute | solution.py:46
  6.7 1.8 %collective-permute-start.2 = (bf16[64,1024]{1,0:T(8,128)(2,1)S(1)}, bf16[64,1024]{1,0:T(8,128)(2,1)S(1)}, u32[]{:S(2)}, u32[]{:S(2)}) collective-permute-start(bf16[64,1024]{1,0:T(8,128)(2,1)S(1)} %collective-permute-done), channel_id=1, source_target_pairs={{0,4},{4,8},{8,12},{12,14},{14,10},{10,6},{6,2},{2,0},{1,5},{5,9},... | collective-permute-start | bytes 393224 | tf_op jit(solution)/shard_map/ppermute | solution.py:46
  8.6 0.1 broadcast_in_dim.159
  8.8 0.1 broadcast_in_dim.164
  8.9 0.1 broadcast_in_dim.169
  9.1 0.1 broadcast_in_dim.174
  9.3 0.1 broadcast_in_dim.179
  9.4 0.1 broadcast_in_dim.184
  9.6 0.1 broadcast_in_dim.189
  9.8 0.1 broadcast_in_dim.154
  10.5 0.2 collective-permute-start.9
  10.8 0.4 collective-permute-start.13
  11.2 1.0 %maximum_select_fusion.7 = bf16[2,64,1024]{2,1,0:T(8,128)(2,1)S(1)} fusion(bf16[1,64,1024]{2,1,0:T(8,128)(2,1)S(1)} %bitcast.96, bf16[1,64,1024]{2,1,0:T(8,128)(2,1)} %bitcast.92, pred[]{:T(512)S(6)} %eq.53), kind=kLoop, calls=%fused_computation.39 | loop fusion | flops 393216 | bytes 524289 | tf_op jit(solution)/shard_map/jit(_where)/select_n | solution.py:60
  12.2 1.7 %collective-permute-start.4 = (bf16[64,1024]{1,0:T(8,128)(2,1)S(1)}, bf16[64,1024]{1,0:T(8,128)(2,1)S(1)}, u32[]{:S(2)}, u32[]{:S(2)}) collective-permute-start(bf16[64,1024]{1,0:T(8,128)(2,1)S(1)} %collective-permute-done.2), channel_id=1, source_target_pairs={{0,4},{4,8},{8,12},{12,14},{14,10},{10,6},{6,2},{2,0},{1,5},{5,9},... | collective-permute-start | bytes 393224 | tf_op jit(solution)/shard_map/ppermute | solution.py:46
  14.0 2.5 %collective-permute-done.9 = bf16[64,1024]{1,0:T(8,128)(2,1)S(1)} collective-permute-done((bf16[64,1024]{1,0:T(8,128)(2,1)S(1)}, bf16[64,1024]{1,0:T(8,128)(2,1)S(1)}, u32[]{:S(2)}, u32[]{:S(2)}) %collective-permute-start.9) | collective-permute-done | bytes 131104 | tf_op jit(solution)/shard_map/ppermute | solution.py:50
  16.5 0.3 collective-permute-start.10
  16.8 1.0 %collective-permute-done.4 = bf16[64,1024]{1,0:T(8,128)(2,1)S(1)} collective-permute-done((bf16[64,1024]{1,0:T(8,128)(2,1)S(1)}, bf16[64,1024]{1,0:T(8,128)(2,1)S(1)}, u32[]{:S(2)}, u32[]{:S(2)}) %collective-permute-start.4) | collective-permute-done | bytes 131104 | tf_op jit(solution)/shard_map/ppermute | solution.py:46
  17.8 1.8 %collective-permute-start.6 = (bf16[64,1024]{1,0:T(8,128)(2,1)S(1)}, bf16[64,1024]{1,0:T(8,128)(2,1)S(1)}, u32[]{:S(2)}, u32[]{:S(2)}) collective-permute-start(bf16[64,1024]{1,0:T(8,128)(2,1)S(1)} %collective-permute-done.4), channel_id=1, source_target_pairs={{0,4},{4,8},{8,12},{12,14},{14,10},{10,6},{6,2},{2,0},{1,5},{5,9},... | collective-permute-start | bytes 393224 | tf_op jit(solution)/shard_map/ppermute | solution.py:46
  19.6 1.9 %collective-permute-done.10 = bf16[64,1024]{1,0:T(8,128)(2,1)S(1)} collective-permute-done((bf16[64,1024]{1,0:T(8,128)(2,1)S(1)}, bf16[64,1024]{1,0:T(8,128)(2,1)S(1)}, u32[]{:S(2)}, u32[]{:S(2)}) %collective-permute-start.10) | collective-permute-done | bytes 131104 | tf_op jit(solution)/shard_map/ppermute | solution.py:50
  21.6 1.2 %collective-permute-done.6 = bf16[64,1024]{1,0:T(8,128)(2,1)S(1)} collective-permute-done((bf16[64,1024]{1,0:T(8,128)(2,1)S(1)}, bf16[64,1024]{1,0:T(8,128)(2,1)S(1)}, u32[]{:S(2)}, u32[]{:S(2)}) %collective-permute-start.6) | collective-permute-done | bytes 131104 | tf_op jit(solution)/shard_map/ppermute | solution.py:46
  22.9 1.2 %collective-permute-done.7 = bf16[64,1024]{1,0:T(8,128)(2,1)S(1)} collective-permute-done((bf16[64,1024]{1,0:T(8,128)(2,1)S(1)}, bf16[64,1024]{1,0:T(8,128)(2,1)S(1)}, u32[]{:S(2)}, u32[]{:S(2)}) %collective-permute-start.7) | collective-permute-done | bytes 131104 | tf_op jit(solution)/shard_map/ppermute | solution.py:53
  24.2 2.0 %fusion.10 = bf16[1024,1024]{1,0:T(8,128)(2,1)S(1)} fusion(pred[1024]{0:T(1024)(128)(4,1)S(1)} %broadcast_in_dim.189, pred[1024]{0:T(1024)(128)(4,1)S(1)} %broadcast_in_dim.184, pred[1024]{0:T(1024)(128)(4,1)S(1)} %broadcast_in_dim.179, pred[1024]{0:T(1024)(128)(4,1)S(1)} %broadcast_in_dim.174, pred[1024]{0:T(1024)(128)(4,1)S(1)} %broadcast_in_dim.169, ...), kind=kLoop, calls=%fused_computation.14 | loop fusion | flops 8388608 | bytes 4202496 | tf_op jit(solution)/shard_map/jit(_where)/select_n | solution.py:61
  26.2 3.8 %convert_bitcast_fusion = bf16[2,1024,512]{2,1,0:T(8,128)(2,1)} fusion(bf16[2,1024,512]{2,1,0:T(8,128)(2,1)S(1)} %copy-done, bf16[1024,1024]{1,0:T(8,128)(2,1)S(1)} %fusion.10), kind=kOutput, calls=%fused_computation.17 | convolution fusion | flops 2148532224 | bytes 6291456 | tf_op jit(solution)/shard_map/sp,gsr->gpr/dot_general | solution.py:76
  30.0 0.1 collective-permute-start.15
  30.2 0.6 gather_fusion
  30.8 0.6 gather_fusion.1
  31.6 2.9 %fusion.16 = bf16[2,1024,256]{1,2,0:T(8,128)(2,1)S(1)} fusion(bf16[1024,1024]{1,0:T(8,128)(2,1)} %copy-done.3, s32[2,256]{1,0:T(2,128)S(1)} %bitcast_add_fusion), kind=kOutput, calls=%fused_computation.19 | convolution fusion | flops 1074790400 | bytes 3147776 | tf_op jit(solution)/shard_map/rc,gcj->grj/dot_general | solution.py:87
  34.5 2.3 %fusion.21 = f32[2,1024,256]{2,1,0:T(8,128)S(1)} fusion(bf16[2,1024,512]{2,1,0:T(8,128)(2,1)} %convert_bitcast_fusion, pred[]{:T(512)S(6)} %eq.53, bf16[2,1024,256]{1,2,0:T(8,128)(2,1)S(1)} %fusion.16), kind=kOutput, calls=%fused_computation.24 | convolution fusion | flops 537133056 | bytes 5242881 | tf_op jit(solution)/shard_map/gpr,grj->gpj/dot_general | solution.py:96
  36.8 3.3 %add_convert_fusion = bf16[2,1024,256]{2,1,0:T(8,128)(2,1)} fusion(f32[2,1024,256]{2,1,0:T(8,128)S(1)} %fusion.21, bf16[2,1024,512]{2,1,0:T(8,128)(2,1)} %collective-permute-done.15, pred[]{:T(512)S(6)} %eq.53, bf16[2,1024,256]{1,2,0:T(8,128)(2,1)S(1)} %fusion.16), kind=kOutput, calls=%fused_computation.15 | convolution fusion | flops 538181632 | bytes 6291457 | tf_op jit(solution)/shard_map/gpr,grj->gpj/dot_general | solution.py:97
  40.2 1.8 %gather_fusion.2 = bf16[8,2,128,256]{3,2,1,0:T(8,128)(2,1)S(1)} fusion(bf16[2,8,128,256]{3,2,1,0:T(8,128)(2,1)} %bitcast.91, s32[1024]{0:T(1024)S(1)} %pad_clamp_fusion), kind=kCustom, calls=%fused_computation.2 | custom fusion | bytes 2097184 | tf_op jit(solution)/shard_map/jit(_take)/gather | solution.py:120
  42.0 0.1 copy.19
  42.1 0.9 %copy-done.4 = bf16[2,256,512]{2,1,0:T(8,128)(2,1)S(1)} copy-done((bf16[2,256,512]{2,1,0:T(8,128)(2,1)S(1)}, bf16[2,256,512]{2,1,0:T(8,128)(2,1)}, u32[]{:S(2)}) %copy-start.4) | copy-done | bytes 524312
  43.1 0.5 convolution_bitcast_fusion.1
  43.6 1.8 %collective-permute-start.16 = (f32[128,256]{0,1:T(8,128)S(1)}, f32[128,256]{0,1:T(8,128)S(1)}, u32[]{:S(2)}, u32[]{:S(2)}) collective-permute-start(f32[128,256]{0,1:T(8,128)S(1)} %slice.104), channel_id=1, source_target_pairs={{0,4},{4,8},{8,12},{12,14},{14,10},{10,6},{6,2},{2,0},{1,5},{5,9},... | collective-permute-start | bytes 393224 | tf_op jit(solution)/shard_map/ppermute | solution.py:136
  45.4 0.5 convolution_bitcast_fusion
  45.9 0.3 collective-permute-start.23
  46.2 3.2 %collective-permute-done.16 = f32[128,256]{0,1:T(8,128)S(1)} collective-permute-done((f32[128,256]{0,1:T(8,128)S(1)}, f32[128,256]{0,1:T(8,128)S(1)}, u32[]{:S(2)}, u32[]{:S(2)}) %collective-permute-start.16) | collective-permute-done | bytes 131104 | tf_op jit(solution)/shard_map/ppermute | solution.py:136
  49.4 1.8 %collective-permute-start.17 = (f32[128,256]{0,1:T(8,128)S(1)}, f32[128,256]{0,1:T(8,128)S(1)}, u32[]{:S(2)}, u32[]{:S(2)}) collective-permute-start(f32[128,256]{0,1:T(8,128)S(1)} %slice_add_fusion.13), channel_id=1, source_target_pairs={{0,4},{4,8},{8,12},{12,14},{14,10},{10,6},{6,2},{2,0},{1,5},{5,9},... | collective-permute-start | bytes 393224 | tf_op jit(solution)/shard_map/ppermute | solution.py:136
  51.3 0.2 collective-permute-done.23
  51.5 0.3 collective-permute-start.24
  51.8 2.6 %collective-permute-done.17 = f32[128,256]{0,1:T(8,128)S(1)} collective-permute-done((f32[128,256]{0,1:T(8,128)S(1)}, f32[128,256]{0,1:T(8,128)S(1)}, u32[]{:S(2)}, u32[]{:S(2)}) %collective-permute-start.17) | collective-permute-done | bytes 131104 | tf_op jit(solution)/shard_map/ppermute | solution.py:136
  54.5 1.8 %collective-permute-start.18 = (f32[128,256]{0,1:T(8,128)S(1)}, f32[128,256]{0,1:T(8,128)S(1)}, u32[]{:S(2)}, u32[]{:S(2)}) collective-permute-start(f32[128,256]{0,1:T(8,128)S(1)} %slice_add_fusion.12), channel_id=1, source_target_pairs={{0,4},{4,8},{8,12},{12,14},{14,10},{10,6},{6,2},{2,0},{1,5},{5,9},... | collective-permute-start | bytes 393224 | tf_op jit(solution)/shard_map/ppermute | solution.py:136
  56.3 0.2 collective-permute-done.24
  56.6 0.3 collective-permute-start.25
  56.9 2.7 %collective-permute-done.18 = f32[128,256]{0,1:T(8,128)S(1)} collective-permute-done((f32[128,256]{0,1:T(8,128)S(1)}, f32[128,256]{0,1:T(8,128)S(1)}, u32[]{:S(2)}, u32[]{:S(2)}) %collective-permute-start.18) | collective-permute-done | bytes 131104 | tf_op jit(solution)/shard_map/ppermute | solution.py:136
  59.6 1.8 %collective-permute-start.19 = (f32[128,256]{0,1:T(8,128)S(1)}, f32[128,256]{0,1:T(8,128)S(1)}, u32[]{:S(2)}, u32[]{:S(2)}) collective-permute-start(f32[128,256]{0,1:T(8,128)S(1)} %slice_add_fusion.11), channel_id=1, source_target_pairs={{0,4},{4,8},{8,12},{12,14},{14,10},{10,6},{6,2},{2,0},{1,5},{5,9},... | collective-permute-start | bytes 393224 | tf_op jit(solution)/shard_map/ppermute | solution.py:136
  61.5 0.2 collective-permute-done.25
  61.7 0.3 collective-permute-start.26
  62.0 3.6 %collective-permute-done.19 = f32[128,256]{0,1:T(8,128)S(1)} collective-permute-done((f32[128,256]{0,1:T(8,128)S(1)}, f32[128,256]{0,1:T(8,128)S(1)}, u32[]{:S(2)}, u32[]{:S(2)}) %collective-permute-start.19) | collective-permute-done | bytes 131104 | tf_op jit(solution)/shard_map/ppermute | solution.py:136
  65.7 1.8 %collective-permute-start.20 = (f32[128,256]{0,1:T(8,128)S(1)}, f32[128,256]{0,1:T(8,128)S(1)}, u32[]{:S(2)}, u32[]{:S(2)}) collective-permute-start(f32[128,256]{0,1:T(8,128)S(1)} %slice_add_fusion.10), channel_id=1, source_target_pairs={{0,4},{4,8},{8,12},{12,14},{14,10},{10,6},{6,2},{2,0},{1,5},{5,9},... | collective-permute-start | bytes 393224 | tf_op jit(solution)/shard_map/ppermute | solution.py:136
  67.5 0.5 collective-permute-done.26
  68.0 0.3 collective-permute-start.27
  68.3 3.4 %collective-permute-done.20 = f32[128,256]{0,1:T(8,128)S(1)} collective-permute-done((f32[128,256]{0,1:T(8,128)S(1)}, f32[128,256]{0,1:T(8,128)S(1)}, u32[]{:S(2)}, u32[]{:S(2)}) %collective-permute-start.20) | collective-permute-done | bytes 131104 | tf_op jit(solution)/shard_map/ppermute | solution.py:136
  71.7 1.8 %collective-permute-start.21 = (f32[128,256]{0,1:T(8,128)S(1)}, f32[128,256]{0,1:T(8,128)S(1)}, u32[]{:S(2)}, u32[]{:S(2)}) collective-permute-start(f32[128,256]{0,1:T(8,128)S(1)} %slice_add_fusion.9), channel_id=1, source_target_pairs={{0,4},{4,8},{8,12},{12,14},{14,10},{10,6},{6,2},{2,0},{1,5},{5,9},... | collective-permute-start | bytes 393224 | tf_op jit(solution)/shard_map/ppermute | solution.py:136
  73.6 0.3 collective-permute-start.28
  73.9 2.9 %collective-permute-done.21 = f32[128,256]{0,1:T(8,128)S(1)} collective-permute-done((f32[128,256]{0,1:T(8,128)S(1)}, f32[128,256]{0,1:T(8,128)S(1)}, u32[]{:S(2)}, u32[]{:S(2)}) %collective-permute-start.21) | collective-permute-done | bytes 131104 | tf_op jit(solution)/shard_map/ppermute | solution.py:136
  76.9 1.8 %collective-permute-start.22 = (f32[128,256]{0,1:T(8,128)S(1)}, f32[128,256]{0,1:T(8,128)S(1)}, u32[]{:S(2)}, u32[]{:S(2)}) collective-permute-start(f32[128,256]{0,1:T(8,128)S(1)} %slice_add_fusion.8), channel_id=1, source_target_pairs={{0,4},{4,8},{8,12},{12,14},{14,10},{10,6},{6,2},{2,0},{1,5},{5,9},... | collective-permute-start | bytes 393224 | tf_op jit(solution)/shard_map/ppermute | solution.py:136
  78.8 0.3 collective-permute-start.29
  79.0 2.9 %collective-permute-done.22 = f32[128,256]{0,1:T(8,128)S(1)} collective-permute-done((f32[128,256]{0,1:T(8,128)S(1)}, f32[128,256]{0,1:T(8,128)S(1)}, u32[]{:S(2)}, u32[]{:S(2)}) %collective-permute-start.22) | collective-permute-done | bytes 131104 | tf_op jit(solution)/shard_map/ppermute | solution.py:136
  81.9 1.8 %collective-permute-done.29 = f32[128,256]{0,1:T(8,128)S(1)} collective-permute-done((f32[128,256]{0,1:T(8,128)S(1)}, f32[128,256]{0,1:T(8,128)S(1)}, u32[]{:S(2)}, u32[]{:S(2)}) %collective-permute-start.29) | collective-permute-done | bytes 131104 | tf_op jit(solution)/shard_map/ppermute | solution.py:137
  83.8 0.8 copy.22
  (73 shorter events, 1.5 us)
Async XLA Ops:
  0.0 26.1 %copy-start = (bf16[2,1024,512]{2,1,0:T(8,128)(2,1)S(1)}, bf16[2,1024,512]{2,1,0:T(8,128)(2,1)}, u32[]{:S(2)}) copy-start(bf16[2,1024,512]{2,1,0:T(8,128)(2,1)} %param.8) | copy-start | bytes 6291460
  0.0 6.7 %collective-permute-start = (bf16[64,1024]{1,0:T(8,128)(2,1)}, bf16[64,1024]{1,0:T(8,128)(2,1)S(1)}, u32[]{:S(2)}, u32[]{:S(2)}) collective-permute-start(bf16[64,1024]{1,0:T(8,128)(2,1)} %param.9), channel_id=1, source_target_pairs={{0,4},{4,8},{8,12},{12,14},{14,10},{10,6},{6,2},{2,0},{1,5},{5,9},... | collective-permute-start | bytes 393224 | tf_op jit(solution)/shard_map/ppermute | solution.py:46
  3.1 7.5 %collective-permute-start.8 = (bf16[64,1024]{1,0:T(8,128)(2,1)}, bf16[64,1024]{1,0:T(8,128)(2,1)S(1)}, u32[]{:S(2)}, u32[]{:S(2)}) collective-permute-start(bf16[64,1024]{1,0:T(8,128)(2,1)} %param.9), channel_id=1, source_target_pairs={{0,2},{4,0},{8,4},{12,8},{14,12},{10,14},{6,10},{2,6},{1,3},{5,1},... | collective-permute-start | bytes 393224 | tf_op jit(solution)/shard_map/ppermute | solution.py:50
  3.1 8.1 %collective-permute-start.14 = (bf16[64,1024]{1,0:T(8,128)(2,1)}, bf16[64,1024]{1,0:T(8,128)(2,1)S(1)}, u32[]{:S(2)}, u32[]{:S(2)}) collective-permute-start(bf16[64,1024]{1,0:T(8,128)(2,1)} %param.9), channel_id=1, source_target_pairs={{0,1},{1,0},{2,3},{3,2},{4,5},{5,4},{6,7},{7,6},{8,9},{9,8},{10,11... | collective-permute-start | bytes 393224 | tf_op jit(solution)/shard_map/ppermute | solution.py:53
  6.7 5.5 %collective-permute-start.2 = (bf16[64,1024]{1,0:T(8,128)(2,1)S(1)}, bf16[64,1024]{1,0:T(8,128)(2,1)S(1)}, u32[]{:S(2)}, u32[]{:S(2)}) collective-permute-start(bf16[64,1024]{1,0:T(8,128)(2,1)S(1)} %collective-permute-done), channel_id=1, source_target_pairs={{0,4},{4,8},{8,12},{12,14},{14,10},{10,6},{6,2},{2,0},{1,5},{5,9},... | collective-permute-start | bytes 393224 | tf_op jit(solution)/shard_map/ppermute | solution.py:46
  8.5 5.4 %collective-permute-start.1 = (bf16[64,1024]{1,0:T(8,128)(2,1)S(1)}, bf16[64,1024]{1,0:T(8,128)(2,1)S(1)}, u32[]{:S(2)}, u32[]{:S(2)}) collective-permute-start(bf16[64,1024]{1,0:T(8,128)(2,1)S(1)} %collective-permute-done), channel_id=1, source_target_pairs={{0,1},{1,0},{2,3},{3,2},{4,5},{5,4},{6,7},{7,6},{8,9},{9,8},{10,11... | collective-permute-start | bytes 393224 | tf_op jit(solution)/shard_map/ppermute | solution.py:53
  10.5 6.0 %collective-permute-start.9 = (bf16[64,1024]{1,0:T(8,128)(2,1)S(1)}, bf16[64,1024]{1,0:T(8,128)(2,1)S(1)}, u32[]{:S(2)}, u32[]{:S(2)}) collective-permute-start(bf16[64,1024]{1,0:T(8,128)(2,1)S(1)} %collective-permute-done.8), channel_id=1, source_target_pairs={{0,2},{4,0},{8,4},{12,8},{14,12},{10,14},{6,10},{2,6},{1,3},{5,1},... | collective-permute-start | bytes 393224 | tf_op jit(solution)/shard_map/ppermute | solution.py:50
  10.8 6.0 %collective-permute-start.13 = (bf16[64,1024]{1,0:T(8,128)(2,1)S(1)}, bf16[64,1024]{1,0:T(8,128)(2,1)S(1)}, u32[]{:S(2)}, u32[]{:S(2)}) collective-permute-start(bf16[64,1024]{1,0:T(8,128)(2,1)S(1)} %collective-permute-done.8), channel_id=1, source_target_pairs={{0,1},{1,0},{2,3},{3,2},{4,5},{5,4},{6,7},{7,6},{8,9},{9,8},{10,11... | collective-permute-start | bytes 393224 | tf_op jit(solution)/shard_map/ppermute | solution.py:53
  12.2 5.6 %collective-permute-start.4 = (bf16[64,1024]{1,0:T(8,128)(2,1)S(1)}, bf16[64,1024]{1,0:T(8,128)(2,1)S(1)}, u32[]{:S(2)}, u32[]{:S(2)}) collective-permute-start(bf16[64,1024]{1,0:T(8,128)(2,1)S(1)} %collective-permute-done.2), channel_id=1, source_target_pairs={{0,4},{4,8},{8,12},{12,14},{14,10},{10,6},{6,2},{2,0},{1,5},{5,9},... | collective-permute-start | bytes 393224 | tf_op jit(solution)/shard_map/ppermute | solution.py:46
  13.9 5.7 %collective-permute-start.3 = (bf16[64,1024]{1,0:T(8,128)(2,1)S(1)}, bf16[64,1024]{1,0:T(8,128)(2,1)S(1)}, u32[]{:S(2)}, u32[]{:S(2)}) collective-permute-start(bf16[64,1024]{1,0:T(8,128)(2,1)S(1)} %collective-permute-done.2), channel_id=1, source_target_pairs={{0,1},{1,0},{2,3},{3,2},{4,5},{5,4},{6,7},{7,6},{8,9},{9,8},{10,11... | collective-permute-start | bytes 393224 | tf_op jit(solution)/shard_map/ppermute | solution.py:53
  16.5 5.0 %collective-permute-start.10 = (bf16[64,1024]{1,0:T(8,128)(2,1)S(1)}, bf16[64,1024]{1,0:T(8,128)(2,1)S(1)}, u32[]{:S(2)}, u32[]{:S(2)}) collective-permute-start(bf16[64,1024]{1,0:T(8,128)(2,1)S(1)} %collective-permute-done.9), channel_id=1, source_target_pairs={{0,2},{4,0},{8,4},{12,8},{14,12},{10,14},{6,10},{2,6},{1,3},{5,1},... | collective-permute-start | bytes 393224 | tf_op jit(solution)/shard_map/ppermute | solution.py:50
  16.8 4.8 %collective-permute-start.12 = (bf16[64,1024]{1,0:T(8,128)(2,1)S(1)}, bf16[64,1024]{1,0:T(8,128)(2,1)S(1)}, u32[]{:S(2)}, u32[]{:S(2)}) collective-permute-start(bf16[64,1024]{1,0:T(8,128)(2,1)S(1)} %collective-permute-done.9), channel_id=1, source_target_pairs={{0,1},{1,0},{2,3},{3,2},{4,5},{5,4},{6,7},{7,6},{8,9},{9,8},{10,11... | collective-permute-start | bytes 393224 | tf_op jit(solution)/shard_map/ppermute | solution.py:53
  17.8 5.0 %collective-permute-start.6 = (bf16[64,1024]{1,0:T(8,128)(2,1)S(1)}, bf16[64,1024]{1,0:T(8,128)(2,1)S(1)}, u32[]{:S(2)}, u32[]{:S(2)}) collective-permute-start(bf16[64,1024]{1,0:T(8,128)(2,1)S(1)} %collective-permute-done.4), channel_id=1, source_target_pairs={{0,4},{4,8},{8,12},{12,14},{14,10},{10,6},{6,2},{2,0},{1,5},{5,9},... | collective-permute-start | bytes 393224 | tf_op jit(solution)/shard_map/ppermute | solution.py:46
  19.6 3.2 %collective-permute-start.5 = (bf16[64,1024]{1,0:T(8,128)(2,1)S(1)}, bf16[64,1024]{1,0:T(8,128)(2,1)S(1)}, u32[]{:S(2)}, u32[]{:S(2)}) collective-permute-start(bf16[64,1024]{1,0:T(8,128)(2,1)S(1)} %collective-permute-done.4), channel_id=1, source_target_pairs={{0,1},{1,0},{2,3},{3,2},{4,5},{5,4},{6,7},{7,6},{8,9},{9,8},{10,11... | collective-permute-start | bytes 393224 | tf_op jit(solution)/shard_map/ppermute | solution.py:53
  21.5 1.3 %collective-permute-start.11 = (bf16[64,1024]{1,0:T(8,128)(2,1)S(1)}, bf16[64,1024]{1,0:T(8,128)(2,1)S(1)}, u32[]{:S(2)}, u32[]{:S(2)}) collective-permute-start(bf16[64,1024]{1,0:T(8,128)(2,1)S(1)} %collective-permute-done.10), channel_id=1, source_target_pairs={{0,1},{1,0},{2,3},{3,2},{4,5},{5,4},{6,7},{7,6},{8,9},{9,8},{10,11... | collective-permute-start | bytes 393224 | tf_op jit(solution)/shard_map/ppermute | solution.py:53
  22.8 1.3 %collective-permute-start.7 = (bf16[64,1024]{1,0:T(8,128)(2,1)S(1)}, bf16[64,1024]{1,0:T(8,128)(2,1)S(1)}, u32[]{:S(2)}, u32[]{:S(2)}) collective-permute-start(bf16[64,1024]{1,0:T(8,128)(2,1)S(1)} %collective-permute-done.6), channel_id=1, source_target_pairs={{0,1},{1,0},{2,3},{3,2},{4,5},{5,4},{6,7},{7,6},{8,9},{9,8},{10,11... | collective-permute-start | bytes 393224 | tf_op jit(solution)/shard_map/ppermute | solution.py:53
  26.1 3.8 %copy-start.3 = (bf16[1024,1024]{1,0:T(8,128)(2,1)}, bf16[1024,1024]{1,0:T(8,128)(2,1)S(1)}, u32[]{:S(2)}) copy-start(bf16[1024,1024]{1,0:T(8,128)(2,1)S(1)} %fusion.10) | copy-start | bytes 6291460
  26.1 4.0 %copy-start.2 = (s32[8]{0:T(128)S(1)}, s32[8]{0:T(128)}, u32[]{:S(2)}) copy-start(s32[8]{0:T(128)} %constant.58.clone) | copy-start | bytes 100
  26.2 4.7 %copy-start.1 = (s32[8]{0:T(128)S(1)}, s32[8]{0:T(128)}, u32[]{:S(2)}) copy-start(s32[8]{0:T(128)} %param.12) | copy-start | bytes 100
  26.2 5.3 %copy-start.5 = (s32[2,2]{1,0:T(2,128)S(1)}, s32[2,2]{1,0:T(2,128)}, u32[]{:S(2)}) copy-start(s32[2,2]{1,0:T(2,128)} %param.10) | copy-start | bytes 52
  30.0 6.9 %collective-permute-start.15 = (bf16[2,1024,512]{2,1,0:T(8,128)(2,1)}, bf16[2,1024,512]{2,1,0:T(8,128)(2,1)}, u32[]{:S(2)}, u32[]{:S(2)}) collective-permute-start(bf16[2,1024,512]{2,1,0:T(8,128)(2,1)} %convert_bitcast_fusion), channel_id=1, source_target_pairs={{0,1},{1,0},{2,3},{3,2},{4,5},{5,4},{6,7},{7,6},{8,9},{9,8},{10,11... | collective-permute-start | bytes 6291464 | tf_op jit(solution)/shard_map/ppermute | solution.py:79
  42.0 1.0 %copy-start.4 = (bf16[2,256,512]{2,1,0:T(8,128)(2,1)S(1)}, bf16[2,256,512]{2,1,0:T(8,128)(2,1)}, u32[]{:S(2)}) copy-start(bf16[2,256,512]{2,1,0:T(8,128)(2,1)} %param.11) | copy-start | bytes 1572868
  43.6 5.8 %collective-permute-start.16 = (f32[128,256]{0,1:T(8,128)S(1)}, f32[128,256]{0,1:T(8,128)S(1)}, u32[]{:S(2)}, u32[]{:S(2)}) collective-permute-start(f32[128,256]{0,1:T(8,128)S(1)} %slice.104), channel_id=1, source_target_pairs={{0,4},{4,8},{8,12},{12,14},{14,10},{10,6},{6,2},{2,0},{1,5},{5,9},... | collective-permute-start | bytes 393224 | tf_op jit(solution)/shard_map/ppermute | solution.py:136
  45.9 5.5 %collective-permute-start.23 = (f32[128,256]{0,1:T(8,128)S(1)}, f32[128,256]{0,1:T(8,128)S(1)}, u32[]{:S(2)}, u32[]{:S(2)}) collective-permute-start(f32[128,256]{0,1:T(8,128)S(1)} %slice.112), channel_id=1, source_target_pairs={{0,2},{4,0},{8,4},{12,8},{14,12},{10,14},{6,10},{2,6},{1,3},{5,1},... | collective-permute-start | bytes 393224 | tf_op jit(solution)/shard_map/ppermute | solution.py:137
  49.4 5.0 %collective-permute-start.17 = (f32[128,256]{0,1:T(8,128)S(1)}, f32[128,256]{0,1:T(8,128)S(1)}, u32[]{:S(2)}, u32[]{:S(2)}) collective-permute-start(f32[128,256]{0,1:T(8,128)S(1)} %slice_add_fusion.13), channel_id=1, source_target_pairs={{0,4},{4,8},{8,12},{12,14},{14,10},{10,6},{6,2},{2,0},{1,5},{5,9},... | collective-permute-start | bytes 393224 | tf_op jit(solution)/shard_map/ppermute | solution.py:136
  51.5 5.0 %collective-permute-start.24 = (f32[128,256]{0,1:T(8,128)S(1)}, f32[128,256]{0,1:T(8,128)S(1)}, u32[]{:S(2)}, u32[]{:S(2)}) collective-permute-start(f32[128,256]{0,1:T(8,128)S(1)} %slice_add_fusion.6), channel_id=1, source_target_pairs={{0,2},{4,0},{8,4},{12,8},{14,12},{10,14},{6,10},{2,6},{1,3},{5,1},... | collective-permute-start | bytes 393224 | tf_op jit(solution)/shard_map/ppermute | solution.py:137
  54.5 5.1 %collective-permute-start.18 = (f32[128,256]{0,1:T(8,128)S(1)}, f32[128,256]{0,1:T(8,128)S(1)}, u32[]{:S(2)}, u32[]{:S(2)}) collective-permute-start(f32[128,256]{0,1:T(8,128)S(1)} %slice_add_fusion.12), channel_id=1, source_target_pairs={{0,4},{4,8},{8,12},{12,14},{14,10},{10,6},{6,2},{2,0},{1,5},{5,9},... | collective-permute-start | bytes 393224 | tf_op jit(solution)/shard_map/ppermute | solution.py:136
  56.6 5.1 %collective-permute-start.25 = (f32[128,256]{0,1:T(8,128)S(1)}, f32[128,256]{0,1:T(8,128)S(1)}, u32[]{:S(2)}, u32[]{:S(2)}) collective-permute-start(f32[128,256]{0,1:T(8,128)S(1)} %slice_add_fusion.5), channel_id=1, source_target_pairs={{0,2},{4,0},{8,4},{12,8},{14,12},{10,14},{6,10},{2,6},{1,3},{5,1},... | collective-permute-start | bytes 393224 | tf_op jit(solution)/shard_map/ppermute | solution.py:137
  59.6 6.0 %collective-permute-start.19 = (f32[128,256]{0,1:T(8,128)S(1)}, f32[128,256]{0,1:T(8,128)S(1)}, u32[]{:S(2)}, u32[]{:S(2)}) collective-permute-start(f32[128,256]{0,1:T(8,128)S(1)} %slice_add_fusion.11), channel_id=1, source_target_pairs={{0,4},{4,8},{8,12},{12,14},{14,10},{10,6},{6,2},{2,0},{1,5},{5,9},... | collective-permute-start | bytes 393224 | tf_op jit(solution)/shard_map/ppermute | solution.py:136
  61.7 6.3 %collective-permute-start.26 = (f32[128,256]{0,1:T(8,128)S(1)}, f32[128,256]{0,1:T(8,128)S(1)}, u32[]{:S(2)}, u32[]{:S(2)}) collective-permute-start(f32[128,256]{0,1:T(8,128)S(1)} %slice_add_fusion.4), channel_id=1, source_target_pairs={{0,2},{4,0},{8,4},{12,8},{14,12},{10,14},{6,10},{2,6},{1,3},{5,1},... | collective-permute-start | bytes 393224 | tf_op jit(solution)/shard_map/ppermute | solution.py:137
  65.7 6.0 %collective-permute-start.20 = (f32[128,256]{0,1:T(8,128)S(1)}, f32[128,256]{0,1:T(8,128)S(1)}, u32[]{:S(2)}, u32[]{:S(2)}) collective-permute-start(f32[128,256]{0,1:T(8,128)S(1)} %slice_add_fusion.10), channel_id=1, source_target_pairs={{0,4},{4,8},{8,12},{12,14},{14,10},{10,6},{6,2},{2,0},{1,5},{5,9},... | collective-permute-start | bytes 393224 | tf_op jit(solution)/shard_map/ppermute | solution.py:136
  68.0 5.6 %collective-permute-start.27 = (f32[128,256]{0,1:T(8,128)S(1)}, f32[128,256]{0,1:T(8,128)S(1)}, u32[]{:S(2)}, u32[]{:S(2)}) collective-permute-start(f32[128,256]{0,1:T(8,128)S(1)} %slice_add_fusion.3), channel_id=1, source_target_pairs={{0,2},{4,0},{8,4},{12,8},{14,12},{10,14},{6,10},{2,6},{1,3},{5,1},... | collective-permute-start | bytes 393224 | tf_op jit(solution)/shard_map/ppermute | solution.py:137
  71.7 5.1 %collective-permute-start.21 = (f32[128,256]{0,1:T(8,128)S(1)}, f32[128,256]{0,1:T(8,128)S(1)}, u32[]{:S(2)}, u32[]{:S(2)}) collective-permute-start(f32[128,256]{0,1:T(8,128)S(1)} %slice_add_fusion.9), channel_id=1, source_target_pairs={{0,4},{4,8},{8,12},{12,14},{14,10},{10,6},{6,2},{2,0},{1,5},{5,9},... | collective-permute-start | bytes 393224 | tf_op jit(solution)/shard_map/ppermute | solution.py:136
  73.6 5.1 %collective-permute-start.28 = (f32[128,256]{0,1:T(8,128)S(1)}, f32[128,256]{0,1:T(8,128)S(1)}, u32[]{:S(2)}, u32[]{:S(2)}) collective-permute-start(f32[128,256]{0,1:T(8,128)S(1)} %slice_add_fusion.2), channel_id=1, source_target_pairs={{0,2},{4,0},{8,4},{12,8},{14,12},{10,14},{6,10},{2,6},{1,3},{5,1},... | collective-permute-start | bytes 393224 | tf_op jit(solution)/shard_map/ppermute | solution.py:137
  76.9 5.0 %collective-permute-start.22 = (f32[128,256]{0,1:T(8,128)S(1)}, f32[128,256]{0,1:T(8,128)S(1)}, u32[]{:S(2)}, u32[]{:S(2)}) collective-permute-start(f32[128,256]{0,1:T(8,128)S(1)} %slice_add_fusion.8), channel_id=1, source_target_pairs={{0,4},{4,8},{8,12},{12,14},{14,10},{10,6},{6,2},{2,0},{1,5},{5,9},... | collective-permute-start | bytes 393224 | tf_op jit(solution)/shard_map/ppermute | solution.py:136
  78.8 5.0 %collective-permute-start.29 = (f32[128,256]{0,1:T(8,128)S(1)}, f32[128,256]{0,1:T(8,128)S(1)}, u32[]{:S(2)}, u32[]{:S(2)}) collective-permute-start(f32[128,256]{0,1:T(8,128)S(1)} %slice_add_fusion.1), channel_id=1, source_target_pairs={{0,2},{4,0},{8,4},{12,8},{14,12},{10,14},{6,10},{2,6},{1,3},{5,1},... | collective-permute-start | bytes 393224 | tf_op jit(solution)/shard_map/ppermute | solution.py:137

commit v6 on v5

--- a/solution.py
+++ b/solution.py
@@ -109,18 +109,18 @@
 
         per = orbitals // n
         held = owner.reshape(n, -1)
-        ring_arr = jnp.asarray(np.array(ring, np.int32))
-        pos_of = jnp.asarray(np.argsort(np.array(ring)).astype(np.int32))
-        pos = pos_of[lax.axis_index("vec")]
-        steps = jnp.arange(n, dtype=jnp.int32)
         by_group = active_rotated.reshape(active_rotated.shape[0], groups, group_rows, -1)
-
-        def in_step_order(order):
-            picked_groups = held[ring_arr[order % n]].reshape(-1)
-            taken = jnp.take(by_group, picked_groups, axis=1, mode="clip")
-            return taken.reshape(active_rotated.shape)
-
-        ordered = in_step_order(pos - 1 - steps)
+        me = lax.axis_index("vec")
+        table = np.array([[ring[(p - 1 - k) % n] for k in range(n)] for p in range(n)], np.int32)
+        pos_of = np.argsort(np.array(ring))
+        by_vec = jnp.asarray(table[pos_of])
+        hits = (jnp.arange(n, dtype=jnp.int32) == me)[:, None]
+        dest = jnp.sum(jnp.where(hits, by_vec, 0), axis=0)
+        order = jnp.sum(
+            jnp.where(dest[:, None, None] == jnp.arange(n, dtype=jnp.int32)[None, :, None], held[None], 0),
+            axis=1,
+        ).reshape(-1)
+        ordered = jnp.take(by_group, order, axis=1, mode="clip").reshape(active_rotated.shape)
         cols = factors.shape[2] // 2
         part_r = jnp.einsum(
             "gpj,gjq->pq", ordered, factors[:, :, :cols], preferred_element_type=jnp.float32

time: 85 us -> 78.5 us (0.924)
  matrix products: 13.3 us -> 7.16 us
  local copies, waits for them, and re-layouts: 7.69 us -> 6.4 us
  starting transfers between devices: 24.6 us -> 25.5 us
    dot_general x1, matrix products: 3.35 us -> 1.73 us  [per_device(): jnp.einsum('gpr,grj->gpj', other_half, theirs, preferred_element_type=jnp...]
    dot_general x1, matrix products: 2.34 us -> 0.74 us  [per_device(): jnp.einsum('gpr,grj->gpj', half_rotated, mine, preferred_element_type=jnp...]
    dot_general x1, matrix products: 2.88 us -> 1.32 us  [per_device(): jnp.einsum('rc,gcj->grj', whole, onehot, preferred_element_type=jnp.float32)]
    ppermute x1, waiting for transfers between devices: 0.01 us -> 1.56 us  [per_device(): other_half = lax.ppermute(half_rotated, 'orb', [(0, 1), (1, 0)])]
    dot_general x1, matrix products: 3.78 us -> 2.41 us  [per_device(): jnp.einsum('sp,gsr->gpr', whole, vectors, preferred_element_type=jnp.floa...]
    gather x4 -> x2, local copies, waits for them, and re-layouts: 3.21 us -> 1.93 us  [per_device(): jnp.take(by_group, order, axis=1, mode='clip').reshape(active_rotated.shape)]
    ppermute x7, starting transfers between devices: 12.8 us -> 13.8 us  [per_device(): acc_r = lax.ppermute(acc_r, 'vec', right) + part_r[k]]
  transfers between devices with their start and end apart: 30 -> 30, of which waited for: 19 -> 20; matrix products, arithmetic and copies ran while one was open for 15% -> 11% of each run, Pallas kernels for 0% -> 0%
where the time goes in v6:
time: 78.5 us; the launch traced here: 78.2 us
  waiting for transfers between devices  33.7 us (43%)
  starting transfers between devices  25.5 us (32%)
  matrix products  7.16 us (9%)
  local copies, waits for them, and re-layouts  6.4 us (8%)
  other arithmetic  5.17 us (7%)
    ppermute x7, waiting for transfers between devices, per_device(): acc_r = lax.ppermute(acc_r, 'vec', right) + part_r[k]  20.6 us
    ppermute x7, starting transfers between devices, per_device(): acc_r = lax.ppermute(acc_r, 'vec', right) + part_r[k]  13.8 us
    ppermute x4, starting transfers between devices, ring_all_gather(): cur = lax.ppermute(cur, 'vec', right)  8.53 us
    ppermute x3, waiting for transfers between devices, ring_all_gather(): cur = lax.ppermute(cur, 'vec', left)  4.02 us
    ppermute x4, waiting for transfers between devices, ring_all_gather(): cur = lax.ppermute(cur, 'vec', right)  3.57 us
    ppermute x7, waiting for transfers between devices, per_device(): lax.ppermute(acc_l, 'vec', left) + part_l[n - 2 - k if k < n - 1 else n - 1]  2.62 us
    dot_general x1, matrix products, per_device(): jnp.einsum('sp,gsr->gpr', whole, vectors, preferred_element_type=jnp.floa...  2.41 us
    ppermute x7, starting transfers between devices, per_device(): lax.ppermute(acc_l, 'vec', left) + part_l[n - 2 - k if k < n - 1 else n - 1]  2.14 us
  transfers between devices with their start and end apart: 30, of which 20 were waited for; matrix products, arithmetic and copies ran while one was open for 11% of the time, Pallas kernels for 0%

profile of v6, /device:TPU:0, one launch (start us, length us, event | category | flops | bytes accessed | tf_op | source)
XLA Modules:
  0.0 78.2 jit_solution(5062470020433694470)
XLA Ops:
  0.0 3.1 %collective-permute-start = (bf16[64,1024]{1,0:T(8,128)(2,1)}, bf16[64,1024]{1,0:T(8,128)(2,1)S(1)}, u32[]{:S(2)}, u32[]{:S(2)}) collective-permute-start(bf16[64,1024]{1,0:T(8,128)(2,1)} %param.8), channel_id=1, source_target_pairs={{0,4},{4,8},{8,12},{12,14},{14,10},{10,6},{6,2},{2,0},{1,5},{5,9},... | collective-permute-start | bytes 393224 | tf_op jit(solution)/shard_map/ppermute | solution.py:46
  3.1 1.2 %dynamic_slice.3 = s32[1]{0:T(128)} dynamic-slice(s32[8]{0:T(128)} %constant.46.clone, s32[]{:T(128)S(6)} %select_n.139), dynamic_slice_sizes={1} | dynamic-slice | bytes 12 | tf_op jit(solution)/shard_map/dynamic_slice | solution.py:55
  4.3 1.3 %broadcast_compare_fusion.6 = (pred[8]{0:T(512)(128)(4,1)S(1)}, s32[8]{0:T(128)S(1)}) fusion(s32[8]{0:T(128)} %constant.46.clone, s32[]{:T(128)} %bitcast), kind=kLoop, calls=%fused_computation.74 | loop fusion | flops 104 | bytes 76 | tf_op jit(solution)/shard_map/eq | solution.py:61
  5.6 1.1 %collective-permute-done = bf16[64,1024]{1,0:T(8,128)(2,1)S(1)} collective-permute-done((bf16[64,1024]{1,0:T(8,128)(2,1)}, bf16[64,1024]{1,0:T(8,128)(2,1)S(1)}, u32[]{:S(2)}, u32[]{:S(2)}) %collective-permute-start) | collective-permute-done | bytes 131104 | tf_op jit(solution)/shard_map/ppermute | solution.py:46
  6.7 1.8 %collective-permute-start.2 = (bf16[64,1024]{1,0:T(8,128)(2,1)S(1)}, bf16[64,1024]{1,0:T(8,128)(2,1)S(1)}, u32[]{:S(2)}, u32[]{:S(2)}) collective-permute-start(bf16[64,1024]{1,0:T(8,128)(2,1)S(1)} %collective-permute-done), channel_id=1, source_target_pairs={{0,4},{4,8},{8,12},{12,14},{14,10},{10,6},{6,2},{2,0},{1,5},{5,9},... | collective-permute-start | bytes 393224 | tf_op jit(solution)/shard_map/ppermute | solution.py:46
  8.6 0.1 broadcast_in_dim.184
  8.8 0.1 broadcast_in_dim.189
  8.9 0.1 broadcast_in_dim.194
  9.1 0.1 broadcast_in_dim.199
  9.3 0.1 broadcast_in_dim.204
  9.4 0.1 broadcast_in_dim.209
  9.6 0.1 broadcast_in_dim.214
  9.8 0.1 broadcast_in_dim.179
  9.9 0.2 collective-permute-start.9
  10.1 0.4 collective-permute-start.13
  10.4 1.0 %maximum_select_fusion.7 = bf16[2,64,1024]{2,1,0:T(8,128)(2,1)S(1)} fusion(bf16[1,64,1024]{2,1,0:T(8,128)(2,1)S(1)} %bitcast.89, bf16[1,64,1024]{2,1,0:T(8,128)(2,1)} %bitcast.85, pred[]{:T(512)S(6)} %eq.83), kind=kLoop, calls=%fused_computation.37 | loop fusion | flops 393216 | bytes 524289 | tf_op jit(solution)/shard_map/jit(_where)/select_n | solution.py:60
  11.5 0.3 collective-permute-done.2
  11.8 1.8 %collective-permute-start.4 = (bf16[64,1024]{1,0:T(8,128)(2,1)S(1)}, bf16[64,1024]{1,0:T(8,128)(2,1)S(1)}, u32[]{:S(2)}, u32[]{:S(2)}) collective-permute-start(bf16[64,1024]{1,0:T(8,128)(2,1)S(1)} %collective-permute-done.2), channel_id=1, source_target_pairs={{0,4},{4,8},{8,12},{12,14},{14,10},{10,6},{6,2},{2,0},{1,5},{5,9},... | collective-permute-start | bytes 393224 | tf_op jit(solution)/shard_map/ppermute | solution.py:46
  13.6 2.1 %collective-permute-done.9 = bf16[64,1024]{1,0:T(8,128)(2,1)S(1)} collective-permute-done((bf16[64,1024]{1,0:T(8,128)(2,1)S(1)}, bf16[64,1024]{1,0:T(8,128)(2,1)S(1)}, u32[]{:S(2)}, u32[]{:S(2)}) %collective-permute-start.9) | collective-permute-done | bytes 131104 | tf_op jit(solution)/shard_map/ppermute | solution.py:50
  15.8 0.3 collective-permute-start.10
  16.1 1.0 %collective-permute-done.4 = bf16[64,1024]{1,0:T(8,128)(2,1)S(1)} collective-permute-done((bf16[64,1024]{1,0:T(8,128)(2,1)S(1)}, bf16[64,1024]{1,0:T(8,128)(2,1)S(1)}, u32[]{:S(2)}, u32[]{:S(2)}) %collective-permute-start.4) | collective-permute-done | bytes 131104 | tf_op jit(solution)/shard_map/ppermute | solution.py:46
  17.1 1.8 %collective-permute-start.6 = (bf16[64,1024]{1,0:T(8,128)(2,1)S(1)}, bf16[64,1024]{1,0:T(8,128)(2,1)S(1)}, u32[]{:S(2)}, u32[]{:S(2)}) collective-permute-start(bf16[64,1024]{1,0:T(8,128)(2,1)S(1)} %collective-permute-done.4), channel_id=1, source_target_pairs={{0,4},{4,8},{8,12},{12,14},{14,10},{10,6},{6,2},{2,0},{1,5},{5,9},... | collective-permute-start | bytes 393224 | tf_op jit(solution)/shard_map/ppermute | solution.py:46
  18.9 1.9 %collective-permute-done.10 = bf16[64,1024]{1,0:T(8,128)(2,1)S(1)} collective-permute-done((bf16[64,1024]{1,0:T(8,128)(2,1)S(1)}, bf16[64,1024]{1,0:T(8,128)(2,1)S(1)}, u32[]{:S(2)}, u32[]{:S(2)}) %collective-permute-start.10) | collective-permute-done | bytes 131104 | tf_op jit(solution)/shard_map/ppermute | solution.py:50
  20.9 1.2 %collective-permute-done.6 = bf16[64,1024]{1,0:T(8,128)(2,1)S(1)} collective-permute-done((bf16[64,1024]{1,0:T(8,128)(2,1)S(1)}, bf16[64,1024]{1,0:T(8,128)(2,1)S(1)}, u32[]{:S(2)}, u32[]{:S(2)}) %collective-permute-start.6) | collective-permute-done | bytes 131104 | tf_op jit(solution)/shard_map/ppermute | solution.py:46
  22.2 1.2 %collective-permute-done.7 = bf16[64,1024]{1,0:T(8,128)(2,1)S(1)} collective-permute-done((bf16[64,1024]{1,0:T(8,128)(2,1)S(1)}, bf16[64,1024]{1,0:T(8,128)(2,1)S(1)}, u32[]{:S(2)}, u32[]{:S(2)}) %collective-permute-start.7) | collective-permute-done | bytes 131104 | tf_op jit(solution)/shard_map/ppermute | solution.py:53
  23.4 2.0 %fusion.10 = bf16[1024,1024]{1,0:T(8,128)(2,1)S(1)} fusion(pred[1024]{0:T(1024)(128)(4,1)S(1)} %broadcast_in_dim.214, pred[1024]{0:T(1024)(128)(4,1)S(1)} %broadcast_in_dim.209, pred[1024]{0:T(1024)(128)(4,1)S(1)} %broadcast_in_dim.204, pred[1024]{0:T(1024)(128)(4,1)S(1)} %broadcast_in_dim.199, pred[1024]{0:T(1024)(128)(4,1)S(1)} %broadcast_in_dim.194, ...), kind=kLoop, calls=%fused_computation.12 | loop fusion | flops 8388608 | bytes 4202496 | tf_op jit(solution)/shard_map/jit(_where)/select_n | solution.py:61
  25.5 2.4 %convert_bitcast_fusion = bf16[2,1024,512]{2,1,0:T(8,128)(2,1)S(1)} fusion(bf16[2,1024,512]{2,1,0:T(8,128)(2,1)S(1)} %copy-done, bf16[1024,1024]{1,0:T(8,128)(2,1)S(1)} %fusion.10), kind=kOutput, calls=%fused_computation.15 | convolution fusion | flops 2148532224 | bytes 6291456 | tf_op jit(solution)/shard_map/sp,gsr->gpr/dot_general | solution.py:76
  27.9 0.2 collective-permute-start.15
  28.2 0.2 select_reduce_fusion
  28.5 1.3 %fusion.16 = bf16[2,1024,256]{1,2,0:T(8,128)(2,1)S(1)} fusion(bf16[1024,1024]{1,0:T(8,128)(2,1)S(1)} %fusion.10, s32[2,256]{1,0:T(2,128)S(1)} %bitcast_add_fusion), kind=kOutput, calls=%fused_computation.17 | convolution fusion | flops 1074790400 | bytes 3147776 | tf_op jit(solution)/shard_map/rc,gcj->grj/dot_general | solution.py:87
  29.8 0.7 fusion.21
  30.5 1.6 %collective-permute-done.15 = bf16[2,1024,512]{2,1,0:T(8,128)(2,1)S(1)} collective-permute-done((bf16[2,1024,512]{2,1,0:T(8,128)(2,1)S(1)}, bf16[2,1024,512]{2,1,0:T(8,128)(2,1)S(1)}, u32[]{:S(2)}, u32[]{:S(2)}) %collective-permute-start.15) | collective-permute-done | bytes 2097184 | tf_op jit(solution)/shard_map/ppermute | solution.py:79
  32.1 1.7 %add_convert_fusion = bf16[2,1024,256]{2,1,0:T(8,128)(2,1)} fusion(f32[2,1024,256]{2,1,0:T(8,128)S(1)} %fusion.21, bf16[2,1024,512]{2,1,0:T(8,128)(2,1)S(1)} %collective-permute-done.15, pred[]{:T(512)S(6)} %eq.83, bf16[2,1024,256]{1,2,0:T(8,128)(2,1)S(1)} %fusion.16), kind=kOutput, calls=%fused_computation.13 | convolution fusion | flops 538181632 | bytes 6291457 | tf_op jit(solution)/shard_map/gpr,grj->gpj/dot_general | solution.py:97
  33.8 1.8 %gather_fusion = bf16[8,2,128,256]{3,2,1,0:T(8,128)(2,1)S(1)} fusion(bf16[2,8,128,256]{3,2,1,0:T(8,128)(2,1)} %bitcast.84, s32[1024]{0:T(1024)S(1)} %pad_clamp_fusion), kind=kCustom, calls=%fused_computation | custom fusion | bytes 2097184 | tf_op jit(solution)/shard_map/jit(_take)/gather | solution.py:123
  35.7 0.1 copy.25
  35.8 0.9 %copy-done.1 = bf16[2,256,512]{2,1,0:T(8,128)(2,1)S(1)} copy-done((bf16[2,256,512]{2,1,0:T(8,128)(2,1)S(1)}, bf16[2,256,512]{2,1,0:T(8,128)(2,1)}, u32[]{:S(2)}) %copy-start.1) | copy-done | bytes 524312
  36.7 0.5 convolution_bitcast_fusion.1
  37.2 1.8 %collective-permute-start.16 = (f32[128,256]{0,1:T(8,128)S(1)}, f32[128,256]{0,1:T(8,128)S(1)}, u32[]{:S(2)}, u32[]{:S(2)}) collective-permute-start(f32[128,256]{0,1:T(8,128)S(1)} %slice.100), channel_id=1, source_target_pairs={{0,4},{4,8},{8,12},{12,14},{14,10},{10,6},{6,2},{2,0},{1,5},{5,9},... | collective-permute-start | bytes 393224 | tf_op jit(solution)/shard_map/ppermute | solution.py:136
  39.1 0.5 convolution_bitcast_fusion
  39.6 0.3 collective-permute-start.23
  39.9 3.0 %collective-permute-done.16 = f32[128,256]{0,1:T(8,128)S(1)} collective-permute-done((f32[128,256]{0,1:T(8,128)S(1)}, f32[128,256]{0,1:T(8,128)S(1)}, u32[]{:S(2)}, u32[]{:S(2)}) %collective-permute-start.16) | collective-permute-done | bytes 131104 | tf_op jit(solution)/shard_map/ppermute | solution.py:136
  42.9 1.8 %collective-permute-start.17 = (f32[128,256]{0,1:T(8,128)S(1)}, f32[128,256]{0,1:T(8,128)S(1)}, u32[]{:S(2)}, u32[]{:S(2)}) collective-permute-start(f32[128,256]{0,1:T(8,128)S(1)} %slice_add_fusion.13), channel_id=1, source_target_pairs={{0,4},{4,8},{8,12},{12,14},{14,10},{10,6},{6,2},{2,0},{1,5},{5,9},... | collective-permute-start | bytes 393224 | tf_op jit(solution)/shard_map/ppermute | solution.py:136
  44.7 0.2 collective-permute-done.23
  45.0 0.3 collective-permute-start.24
  45.3 2.6 %collective-permute-done.17 = f32[128,256]{0,1:T(8,128)S(1)} collective-permute-done((f32[128,256]{0,1:T(8,128)S(1)}, f32[128,256]{0,1:T(8,128)S(1)}, u32[]{:S(2)}, u32[]{:S(2)}) %collective-permute-start.17) | collective-permute-done | bytes 131104 | tf_op jit(solution)/shard_map/ppermute | solution.py:136
  47.9 1.8 %collective-permute-start.18 = (f32[128,256]{0,1:T(8,128)S(1)}, f32[128,256]{0,1:T(8,128)S(1)}, u32[]{:S(2)}, u32[]{:S(2)}) collective-permute-start(f32[128,256]{0,1:T(8,128)S(1)} %slice_add_fusion.12), channel_id=1, source_target_pairs={{0,4},{4,8},{8,12},{12,14},{14,10},{10,6},{6,2},{2,0},{1,5},{5,9},... | collective-permute-start | bytes 393224 | tf_op jit(solution)/shard_map/ppermute | solution.py:136
  49.8 0.2 collective-permute-done.24
  50.0 0.3 collective-permute-start.25
  50.4 2.8 %collective-permute-done.18 = f32[128,256]{0,1:T(8,128)S(1)} collective-permute-done((f32[128,256]{0,1:T(8,128)S(1)}, f32[128,256]{0,1:T(8,128)S(1)}, u32[]{:S(2)}, u32[]{:S(2)}) %collective-permute-start.18) | collective-permute-done | bytes 131104 | tf_op jit(solution)/shard_map/ppermute | solution.py:136
  53.1 2.0 %collective-permute-start.19 = (f32[128,256]{0,1:T(8,128)S(1)}, f32[128,256]{0,1:T(8,128)S(1)}, u32[]{:S(2)}, u32[]{:S(2)}) collective-permute-start(f32[128,256]{0,1:T(8,128)S(1)} %slice_add_fusion.11), channel_id=1, source_target_pairs={{0,4},{4,8},{8,12},{12,14},{14,10},{10,6},{6,2},{2,0},{1,5},{5,9},... | collective-permute-start | bytes 393224 | tf_op jit(solution)/shard_map/ppermute | solution.py:136
  55.2 0.3 collective-permute-start.26
  55.5 3.6 %collective-permute-done.19 = f32[128,256]{0,1:T(8,128)S(1)} collective-permute-done((f32[128,256]{0,1:T(8,128)S(1)}, f32[128,256]{0,1:T(8,128)S(1)}, u32[]{:S(2)}, u32[]{:S(2)}) %collective-permute-start.19) | collective-permute-done | bytes 131104 | tf_op jit(solution)/shard_map/ppermute | solution.py:136
  59.2 2.2 %collective-permute-start.20 = (f32[128,256]{0,1:T(8,128)S(1)}, f32[128,256]{0,1:T(8,128)S(1)}, u32[]{:S(2)}, u32[]{:S(2)}) collective-permute-start(f32[128,256]{0,1:T(8,128)S(1)} %slice_add_fusion.10), channel_id=1, source_target_pairs={{0,4},{4,8},{8,12},{12,14},{14,10},{10,6},{6,2},{2,0},{1,5},{5,9},... | collective-permute-start | bytes 393224 | tf_op jit(solution)/shard_map/ppermute | solution.py:136
  61.4 0.1 collective-permute-done.26
  61.6 0.3 collective-permute-start.27
  61.9 3.3 %collective-permute-done.20 = f32[128,256]{0,1:T(8,128)S(1)} collective-permute-done((f32[128,256]{0,1:T(8,128)S(1)}, f32[128,256]{0,1:T(8,128)S(1)}, u32[]{:S(2)}, u32[]{:S(2)}) %collective-permute-start.20) | collective-permute-done | bytes 131104 | tf_op jit(solution)/shard_map/ppermute | solution.py:136
  65.2 2.0 %collective-permute-start.21 = (f32[128,256]{0,1:T(8,128)S(1)}, f32[128,256]{0,1:T(8,128)S(1)}, u32[]{:S(2)}, u32[]{:S(2)}) collective-permute-start(f32[128,256]{0,1:T(8,128)S(1)} %slice_add_fusion.9), channel_id=1, source_target_pairs={{0,4},{4,8},{8,12},{12,14},{14,10},{10,6},{6,2},{2,0},{1,5},{5,9},... | collective-permute-start | bytes 393224 | tf_op jit(solution)/shard_map/ppermute | solution.py:136
  67.2 0.3 collective-permute-start.28
  67.5 2.7 %collective-permute-done.21 = f32[128,256]{0,1:T(8,128)S(1)} collective-permute-done((f32[128,256]{0,1:T(8,128)S(1)}, f32[128,256]{0,1:T(8,128)S(1)}, u32[]{:S(2)}, u32[]{:S(2)}) %collective-permute-start.21) | collective-permute-done | bytes 131104 | tf_op jit(solution)/shard_map/ppermute | solution.py:136
  70.2 2.0 %collective-permute-start.22 = (f32[128,256]{0,1:T(8,128)S(1)}, f32[128,256]{0,1:T(8,128)S(1)}, u32[]{:S(2)}, u32[]{:S(2)}) collective-permute-start(f32[128,256]{0,1:T(8,128)S(1)} %slice_add_fusion.8), channel_id=1, source_target_pairs={{0,4},{4,8},{8,12},{12,14},{14,10},{10,6},{6,2},{2,0},{1,5},{5,9},... | collective-permute-start | bytes 393224 | tf_op jit(solution)/shard_map/ppermute | solution.py:136
  72.3 0.3 collective-permute-start.29
  72.5 2.7 %collective-permute-done.22 = f32[128,256]{0,1:T(8,128)S(1)} collective-permute-done((f32[128,256]{0,1:T(8,128)S(1)}, f32[128,256]{0,1:T(8,128)S(1)}, u32[]{:S(2)}, u32[]{:S(2)}) %collective-permute-start.22) | collective-permute-done | bytes 131104 | tf_op jit(solution)/shard_map/ppermute | solution.py:136
  75.3 2.0 %collective-permute-done.29 = f32[128,256]{0,1:T(8,128)S(1)} collective-permute-done((f32[128,256]{0,1:T(8,128)S(1)}, f32[128,256]{0,1:T(8,128)S(1)}, u32[]{:S(2)}, u32[]{:S(2)}) %collective-permute-start.29) | collective-permute-done | bytes 131104 | tf_op jit(solution)/shard_map/ppermute | solution.py:137
  77.4 0.8 %copy.28 = f32[128,512]{1,0:T(8,128)} copy(f32[128,512]{0,1:T(8,128)S(1)} %pad_maximum_fusion) | data formatting | bytes 524288 | tf_op jit(solution)/shard_map/concatenate | solution.py:138
  (68 shorter events, 1.6 us)
Async XLA Ops:
  0.0 25.4 %copy-start = (bf16[2,1024,512]{2,1,0:T(8,128)(2,1)S(1)}, bf16[2,1024,512]{2,1,0:T(8,128)(2,1)}, u32[]{:S(2)}) copy-start(bf16[2,1024,512]{2,1,0:T(8,128)(2,1)} %param.7) | copy-start | bytes 6291460
  0.0 6.7 %collective-permute-start = (bf16[64,1024]{1,0:T(8,128)(2,1)}, bf16[64,1024]{1,0:T(8,128)(2,1)S(1)}, u32[]{:S(2)}, u32[]{:S(2)}) collective-permute-start(bf16[64,1024]{1,0:T(8,128)(2,1)} %param.8), channel_id=1, source_target_pairs={{0,4},{4,8},{8,12},{12,14},{14,10},{10,6},{6,2},{2,0},{1,5},{5,9},... | collective-permute-start | bytes 393224 | tf_op jit(solution)/shard_map/ppermute | solution.py:46
  3.1 6.8 %collective-permute-start.8 = (bf16[64,1024]{1,0:T(8,128)(2,1)}, bf16[64,1024]{1,0:T(8,128)(2,1)S(1)}, u32[]{:S(2)}, u32[]{:S(2)}) collective-permute-start(bf16[64,1024]{1,0:T(8,128)(2,1)} %param.8), channel_id=1, source_target_pairs={{0,2},{4,0},{8,4},{12,8},{14,12},{10,14},{6,10},{2,6},{1,3},{5,1},... | collective-permute-start | bytes 393224 | tf_op jit(solution)/shard_map/ppermute | solution.py:50
  3.1 7.4 %collective-permute-start.14 = (bf16[64,1024]{1,0:T(8,128)(2,1)}, bf16[64,1024]{1,0:T(8,128)(2,1)S(1)}, u32[]{:S(2)}, u32[]{:S(2)}) collective-permute-start(bf16[64,1024]{1,0:T(8,128)(2,1)} %param.8), channel_id=1, source_target_pairs={{0,1},{1,0},{2,3},{3,2},{4,5},{5,4},{6,7},{7,6},{8,9},{9,8},{10,11... | collective-permute-start | bytes 393224 | tf_op jit(solution)/shard_map/ppermute | solution.py:53
  6.7 5.1 %collective-permute-start.2 = (bf16[64,1024]{1,0:T(8,128)(2,1)S(1)}, bf16[64,1024]{1,0:T(8,128)(2,1)S(1)}, u32[]{:S(2)}, u32[]{:S(2)}) collective-permute-start(bf16[64,1024]{1,0:T(8,128)(2,1)S(1)} %collective-permute-done), channel_id=1, source_target_pairs={{0,4},{4,8},{8,12},{12,14},{14,10},{10,6},{6,2},{2,0},{1,5},{5,9},... | collective-permute-start | bytes 393224 | tf_op jit(solution)/shard_map/ppermute | solution.py:46
  8.5 5.1 %collective-permute-start.1 = (bf16[64,1024]{1,0:T(8,128)(2,1)S(1)}, bf16[64,1024]{1,0:T(8,128)(2,1)S(1)}, u32[]{:S(2)}, u32[]{:S(2)}) collective-permute-start(bf16[64,1024]{1,0:T(8,128)(2,1)S(1)} %collective-permute-done), channel_id=1, source_target_pairs={{0,1},{1,0},{2,3},{3,2},{4,5},{5,4},{6,7},{7,6},{8,9},{9,8},{10,11... | collective-permute-start | bytes 393224 | tf_op jit(solution)/shard_map/ppermute | solution.py:53
  9.9 5.9 %collective-permute-start.9 = (bf16[64,1024]{1,0:T(8,128)(2,1)S(1)}, bf16[64,1024]{1,0:T(8,128)(2,1)S(1)}, u32[]{:S(2)}, u32[]{:S(2)}) collective-permute-start(bf16[64,1024]{1,0:T(8,128)(2,1)S(1)} %collective-permute-done.8), channel_id=1, source_target_pairs={{0,2},{4,0},{8,4},{12,8},{14,12},{10,14},{6,10},{2,6},{1,3},{5,1},... | collective-permute-start | bytes 393224 | tf_op jit(solution)/shard_map/ppermute | solution.py:50
  10.1 6.0 %collective-permute-start.13 = (bf16[64,1024]{1,0:T(8,128)(2,1)S(1)}, bf16[64,1024]{1,0:T(8,128)(2,1)S(1)}, u32[]{:S(2)}, u32[]{:S(2)}) collective-permute-start(bf16[64,1024]{1,0:T(8,128)(2,1)S(1)} %collective-permute-done.8), channel_id=1, source_target_pairs={{0,1},{1,0},{2,3},{3,2},{4,5},{5,4},{6,7},{7,6},{8,9},{9,8},{10,11... | collective-permute-start | bytes 393224 | tf_op jit(solution)/shard_map/ppermute | solution.py:53
  11.8 5.3 %collective-permute-start.4 = (bf16[64,1024]{1,0:T(8,128)(2,1)S(1)}, bf16[64,1024]{1,0:T(8,128)(2,1)S(1)}, u32[]{:S(2)}, u32[]{:S(2)}) collective-permute-start(bf16[64,1024]{1,0:T(8,128)(2,1)S(1)} %collective-permute-done.2), channel_id=1, source_target_pairs={{0,4},{4,8},{8,12},{12,14},{14,10},{10,6},{6,2},{2,0},{1,5},{5,9},... | collective-permute-start | bytes 393224 | tf_op jit(solution)/shard_map/ppermute | solution.py:46
  13.6 5.3 %collective-permute-start.3 = (bf16[64,1024]{1,0:T(8,128)(2,1)S(1)}, bf16[64,1024]{1,0:T(8,128)(2,1)S(1)}, u32[]{:S(2)}, u32[]{:S(2)}) collective-permute-start(bf16[64,1024]{1,0:T(8,128)(2,1)S(1)} %collective-permute-done.2), channel_id=1, source_target_pairs={{0,1},{1,0},{2,3},{3,2},{4,5},{5,4},{6,7},{7,6},{8,9},{9,8},{10,11... | collective-permute-start | bytes 393224 | tf_op jit(solution)/shard_map/ppermute | solution.py:53
  15.8 5.0 %collective-permute-start.10 = (bf16[64,1024]{1,0:T(8,128)(2,1)S(1)}, bf16[64,1024]{1,0:T(8,128)(2,1)S(1)}, u32[]{:S(2)}, u32[]{:S(2)}) collective-permute-start(bf16[64,1024]{1,0:T(8,128)(2,1)S(1)} %collective-permute-done.9), channel_id=1, source_target_pairs={{0,2},{4,0},{8,4},{12,8},{14,12},{10,14},{6,10},{2,6},{1,3},{5,1},... | collective-permute-start | bytes 393224 | tf_op jit(solution)/shard_map/ppermute | solution.py:50
  16.1 4.8 %collective-permute-start.12 = (bf16[64,1024]{1,0:T(8,128)(2,1)S(1)}, bf16[64,1024]{1,0:T(8,128)(2,1)S(1)}, u32[]{:S(2)}, u32[]{:S(2)}) collective-permute-start(bf16[64,1024]{1,0:T(8,128)(2,1)S(1)} %collective-permute-done.9), channel_id=1, source_target_pairs={{0,1},{1,0},{2,3},{3,2},{4,5},{5,4},{6,7},{7,6},{8,9},{9,8},{10,11... | collective-permute-start | bytes 393224 | tf_op jit(solution)/shard_map/ppermute | solution.py:53
  17.1 5.0 %collective-permute-start.6 = (bf16[64,1024]{1,0:T(8,128)(2,1)S(1)}, bf16[64,1024]{1,0:T(8,128)(2,1)S(1)}, u32[]{:S(2)}, u32[]{:S(2)}) collective-permute-start(bf16[64,1024]{1,0:T(8,128)(2,1)S(1)} %collective-permute-done.4), channel_id=1, source_target_pairs={{0,4},{4,8},{8,12},{12,14},{14,10},{10,6},{6,2},{2,0},{1,5},{5,9},... | collective-permute-start | bytes 393224 | tf_op jit(solution)/shard_map/ppermute | solution.py:46
  18.9 3.2 %collective-permute-start.5 = (bf16[64,1024]{1,0:T(8,128)(2,1)S(1)}, bf16[64,1024]{1,0:T(8,128)(2,1)S(1)}, u32[]{:S(2)}, u32[]{:S(2)}) collective-permute-start(bf16[64,1024]{1,0:T(8,128)(2,1)S(1)} %collective-permute-done.4), channel_id=1, source_target_pairs={{0,1},{1,0},{2,3},{3,2},{4,5},{5,4},{6,7},{7,6},{8,9},{9,8},{10,11... | collective-permute-start | bytes 393224 | tf_op jit(solution)/shard_map/ppermute | solution.py:53
  20.8 1.3 %collective-permute-start.11 = (bf16[64,1024]{1,0:T(8,128)(2,1)S(1)}, bf16[64,1024]{1,0:T(8,128)(2,1)S(1)}, u32[]{:S(2)}, u32[]{:S(2)}) collective-permute-start(bf16[64,1024]{1,0:T(8,128)(2,1)S(1)} %collective-permute-done.10), channel_id=1, source_target_pairs={{0,1},{1,0},{2,3},{3,2},{4,5},{5,4},{6,7},{7,6},{8,9},{9,8},{10,11... | collective-permute-start | bytes 393224 | tf_op jit(solution)/shard_map/ppermute | solution.py:53
  22.1 1.3 %collective-permute-start.7 = (bf16[64,1024]{1,0:T(8,128)(2,1)S(1)}, bf16[64,1024]{1,0:T(8,128)(2,1)S(1)}, u32[]{:S(2)}, u32[]{:S(2)}) collective-permute-start(bf16[64,1024]{1,0:T(8,128)(2,1)S(1)} %collective-permute-done.6), channel_id=1, source_target_pairs={{0,1},{1,0},{2,3},{3,2},{4,5},{5,4},{6,7},{7,6},{8,9},{9,8},{10,11... | collective-permute-start | bytes 393224 | tf_op jit(solution)/shard_map/ppermute | solution.py:53
  25.4 2.7 %copy-start.2 = (s32[8,8]{1,0:T(8,128)S(1)}, s32[8,8]{1,0:T(8,128)}, u32[]{:S(2)}) copy-start(s32[8,8]{1,0:T(8,128)} %constant.47.clone) | copy-start | bytes 772
  25.4 2.8 %copy-start.4 = (s32[8]{0:T(128)S(1)}, s32[8]{0:T(128)}, u32[]{:S(2)}) copy-start(s32[8]{0:T(128)} %param.11) | copy-start | bytes 100
  25.4 2.9 %copy-start.3 = (s32[2,2]{1,0:T(2,128)S(1)}, s32[2,2]{1,0:T(2,128)}, u32[]{:S(2)}) copy-start(s32[2,2]{1,0:T(2,128)} %param.9) | copy-start | bytes 52
  27.9 4.2 %collective-permute-start.15 = (bf16[2,1024,512]{2,1,0:T(8,128)(2,1)S(1)}, bf16[2,1024,512]{2,1,0:T(8,128)(2,1)S(1)}, u32[]{:S(2)}, u32[]{:S(2)}) collective-permute-start(bf16[2,1024,512]{2,1,0:T(8,128)(2,1)S(1)} %convert_bitcast_fusion), channel_id=1, source_target_pairs={{0,1},{1,0},{2,3},{3,2},{4,5},{5,4},{6,7},{7,6},{8,9},{9,8},{10,11... | collective-permute-start | bytes 6291464 | tf_op jit(solution)/shard_map/ppermute | solution.py:79
  35.7 1.0 %copy-start.1 = (bf16[2,256,512]{2,1,0:T(8,128)(2,1)S(1)}, bf16[2,256,512]{2,1,0:T(8,128)(2,1)}, u32[]{:S(2)}) copy-start(bf16[2,256,512]{2,1,0:T(8,128)(2,1)} %param.10) | copy-start | bytes 1572868
  37.2 5.6 %collective-permute-start.16 = (f32[128,256]{0,1:T(8,128)S(1)}, f32[128,256]{0,1:T(8,128)S(1)}, u32[]{:S(2)}, u32[]{:S(2)}) collective-permute-start(f32[128,256]{0,1:T(8,128)S(1)} %slice.100), channel_id=1, source_target_pairs={{0,4},{4,8},{8,12},{12,14},{14,10},{10,6},{6,2},{2,0},{1,5},{5,9},... | collective-permute-start | bytes 393224 | tf_op jit(solution)/shard_map/ppermute | solution.py:136
  39.6 5.3 %collective-permute-start.23 = (f32[128,256]{0,1:T(8,128)S(1)}, f32[128,256]{0,1:T(8,128)S(1)}, u32[]{:S(2)}, u32[]{:S(2)}) collective-permute-start(f32[128,256]{0,1:T(8,128)S(1)} %slice.108), channel_id=1, source_target_pairs={{0,2},{4,0},{8,4},{12,8},{14,12},{10,14},{6,10},{2,6},{1,3},{5,1},... | collective-permute-start | bytes 393224 | tf_op jit(solution)/shard_map/ppermute | solution.py:137
  42.9 5.0 %collective-permute-start.17 = (f32[128,256]{0,1:T(8,128)S(1)}, f32[128,256]{0,1:T(8,128)S(1)}, u32[]{:S(2)}, u32[]{:S(2)}) collective-permute-start(f32[128,256]{0,1:T(8,128)S(1)} %slice_add_fusion.13), channel_id=1, source_target_pairs={{0,4},{4,8},{8,12},{12,14},{14,10},{10,6},{6,2},{2,0},{1,5},{5,9},... | collective-permute-start | bytes 393224 | tf_op jit(solution)/shard_map/ppermute | solution.py:136
  45.0 5.0 %collective-permute-start.24 = (f32[128,256]{0,1:T(8,128)S(1)}, f32[128,256]{0,1:T(8,128)S(1)}, u32[]{:S(2)}, u32[]{:S(2)}) collective-permute-start(f32[128,256]{0,1:T(8,128)S(1)} %slice_add_fusion.6), channel_id=1, source_target_pairs={{0,2},{4,0},{8,4},{12,8},{14,12},{10,14},{6,10},{2,6},{1,3},{5,1},... | collective-permute-start | bytes 393224 | tf_op jit(solution)/shard_map/ppermute | solution.py:137
  47.9 5.2 %collective-permute-start.18 = (f32[128,256]{0,1:T(8,128)S(1)}, f32[128,256]{0,1:T(8,128)S(1)}, u32[]{:S(2)}, u32[]{:S(2)}) collective-permute-start(f32[128,256]{0,1:T(8,128)S(1)} %slice_add_fusion.12), channel_id=1, source_target_pairs={{0,4},{4,8},{8,12},{12,14},{14,10},{10,6},{6,2},{2,0},{1,5},{5,9},... | collective-permute-start | bytes 393224 | tf_op jit(solution)/shard_map/ppermute | solution.py:136
  50.0 5.2 %collective-permute-start.25 = (f32[128,256]{0,1:T(8,128)S(1)}, f32[128,256]{0,1:T(8,128)S(1)}, u32[]{:S(2)}, u32[]{:S(2)}) collective-permute-start(f32[128,256]{0,1:T(8,128)S(1)} %slice_add_fusion.5), channel_id=1, source_target_pairs={{0,2},{4,0},{8,4},{12,8},{14,12},{10,14},{6,10},{2,6},{1,3},{5,1},... | collective-permute-start | bytes 393224 | tf_op jit(solution)/shard_map/ppermute | solution.py:137
  53.1 6.0 %collective-permute-start.19 = (f32[128,256]{0,1:T(8,128)S(1)}, f32[128,256]{0,1:T(8,128)S(1)}, u32[]{:S(2)}, u32[]{:S(2)}) collective-permute-start(f32[128,256]{0,1:T(8,128)S(1)} %slice_add_fusion.11), channel_id=1, source_target_pairs={{0,4},{4,8},{8,12},{12,14},{14,10},{10,6},{6,2},{2,0},{1,5},{5,9},... | collective-permute-start | bytes 393224 | tf_op jit(solution)/shard_map/ppermute | solution.py:136
  55.2 6.3 %collective-permute-start.26 = (f32[128,256]{0,1:T(8,128)S(1)}, f32[128,256]{0,1:T(8,128)S(1)}, u32[]{:S(2)}, u32[]{:S(2)}) collective-permute-start(f32[128,256]{0,1:T(8,128)S(1)} %slice_add_fusion.4), channel_id=1, source_target_pairs={{0,2},{4,0},{8,4},{12,8},{14,12},{10,14},{6,10},{2,6},{1,3},{5,1},... | collective-permute-start | bytes 393224 | tf_op jit(solution)/shard_map/ppermute | solution.py:137
  59.2 6.0 %collective-permute-start.20 = (f32[128,256]{0,1:T(8,128)S(1)}, f32[128,256]{0,1:T(8,128)S(1)}, u32[]{:S(2)}, u32[]{:S(2)}) collective-permute-start(f32[128,256]{0,1:T(8,128)S(1)} %slice_add_fusion.10), channel_id=1, source_target_pairs={{0,4},{4,8},{8,12},{12,14},{14,10},{10,6},{6,2},{2,0},{1,5},{5,9},... | collective-permute-start | bytes 393224 | tf_op jit(solution)/shard_map/ppermute | solution.py:136
  61.6 5.7 %collective-permute-start.27 = (f32[128,256]{0,1:T(8,128)S(1)}, f32[128,256]{0,1:T(8,128)S(1)}, u32[]{:S(2)}, u32[]{:S(2)}) collective-permute-start(f32[128,256]{0,1:T(8,128)S(1)} %slice_add_fusion.3), channel_id=1, source_target_pairs={{0,2},{4,0},{8,4},{12,8},{14,12},{10,14},{6,10},{2,6},{1,3},{5,1},... | collective-permute-start | bytes 393224 | tf_op jit(solution)/shard_map/ppermute | solution.py:137
  65.2 5.0 %collective-permute-start.21 = (f32[128,256]{0,1:T(8,128)S(1)}, f32[128,256]{0,1:T(8,128)S(1)}, u32[]{:S(2)}, u32[]{:S(2)}) collective-permute-start(f32[128,256]{0,1:T(8,128)S(1)} %slice_add_fusion.9), channel_id=1, source_target_pairs={{0,4},{4,8},{8,12},{12,14},{14,10},{10,6},{6,2},{2,0},{1,5},{5,9},... | collective-permute-start | bytes 393224 | tf_op jit(solution)/shard_map/ppermute | solution.py:136
  67.2 5.0 %collective-permute-start.28 = (f32[128,256]{0,1:T(8,128)S(1)}, f32[128,256]{0,1:T(8,128)S(1)}, u32[]{:S(2)}, u32[]{:S(2)}) collective-permute-start(f32[128,256]{0,1:T(8,128)S(1)} %slice_add_fusion.2), channel_id=1, source_target_pairs={{0,2},{4,0},{8,4},{12,8},{14,12},{10,14},{6,10},{2,6},{1,3},{5,1},... | collective-permute-start | bytes 393224 | tf_op jit(solution)/shard_map/ppermute | solution.py:137
  70.2 5.0 %collective-permute-start.22 = (f32[128,256]{0,1:T(8,128)S(1)}, f32[128,256]{0,1:T(8,128)S(1)}, u32[]{:S(2)}, u32[]{:S(2)}) collective-permute-start(f32[128,256]{0,1:T(8,128)S(1)} %slice_add_fusion.8), channel_id=1, source_target_pairs={{0,4},{4,8},{8,12},{12,14},{14,10},{10,6},{6,2},{2,0},{1,5},{5,9},... | collective-permute-start | bytes 393224 | tf_op jit(solution)/shard_map/ppermute | solution.py:136
  72.3 5.0 %collective-permute-start.29 = (f32[128,256]{0,1:T(8,128)S(1)}, f32[128,256]{0,1:T(8,128)S(1)}, u32[]{:S(2)}, u32[]{:S(2)}) collective-permute-start(f32[128,256]{0,1:T(8,128)S(1)} %slice_add_fusion.1), channel_id=1, source_target_pairs={{0,2},{4,0},{8,4},{12,8},{14,12},{10,14},{6,10},{2,6},{1,3},{5,1},... | collective-permute-start | bytes 393224 | tf_op jit(solution)/shard_map/ppermute | solution.py:137

commit v7 on v6

--- a/solution.py
+++ b/solution.py
@@ -73,10 +73,12 @@
         else:
             whole = lax.all_gather(rotation, ("vec", "orb"), axis=0, tiled=True)
         orbitals = whole.shape[0]
-        half_rotated = jnp.einsum(
-            "sp,gsr->gpr", whole, vectors, preferred_element_type=jnp.float32
-        ).astype(jnp.bfloat16)
-        other_half = lax.ppermute(half_rotated, "orb", [(0, 1), (1, 0)])
+        halves = [
+            jnp.einsum("sp,sr->pr", whole, v, preferred_element_type=jnp.float32).astype(jnp.bfloat16)
+            for v in vectors
+        ]
+        other_half = jnp.stack([lax.ppermute(h, "orb", [(0, 1), (1, 0)]) for h in halves])
+        half_rotated = jnp.stack(halves)
 
         columns = (active[:, :, None] * B + jnp.arange(B, dtype=jnp.int32)).reshape(
             active.shape[0], -1
@@ -111,7 +113,10 @@
         held = owner.reshape(n, -1)
         by_group = active_rotated.reshape(active_rotated.shape[0], groups, group_rows, -1)
         me = lax.axis_index("vec")
-        table = np.array([[ring[(p - 1 - k) % n] for k in range(n)] for p in range(n)], np.int32)
+        reach = n // 2
+        back = n - 1 - reach
+        shifts = list(range(reach, 0, -1)) + list(range(-back, 0)) + [0]
+        table = np.array([[ring[(p + d) % n] for d in shifts] for p in range(n)], np.int32)
         pos_of = np.argsort(np.array(ring))
         by_vec = jnp.asarray(table[pos_of])
         hits = (jnp.arange(n, dtype=jnp.int32) == me)[:, None]
@@ -121,21 +126,22 @@
             axis=1,
         ).reshape(-1)
         ordered = jnp.take(by_group, order, axis=1, mode="clip").reshape(active_rotated.shape)
-        cols = factors.shape[2] // 2
-        part_r = jnp.einsum(
-            "gpj,gjq->pq", ordered, factors[:, :, :cols], preferred_element_type=jnp.float32
-        ).reshape(n, per, cols)
-        part_l = jnp.einsum(
-            "gpj,gjq->pq", ordered, factors[:, :, cols:], preferred_element_type=jnp.float32
+        part = jnp.einsum(
+            "gpj,gjq->pq", ordered, factors, preferred_element_type=jnp.float32
         ).reshape(n, per, -1)
         right = [(ring[i], ring[(i + 1) % n]) for i in range(n)]
         left = [(ring[i], ring[(i - 1) % n]) for i in range(n)]
-        acc_r = part_r[0]
-        acc_l = part_l[n - 2]
-        for k in range(1, n):
-            acc_r = lax.ppermute(acc_r, "vec", right) + part_r[k]
-            acc_l = lax.ppermute(acc_l, "vec", left) + part_l[n - 2 - k if k < n - 1 else n - 1]
-        return jnp.concatenate([acc_r, acc_l], axis=1)
+        total = part[n - 1]
+        acc = part[0]
+        for k in range(1, reach):
+            acc = lax.ppermute(acc, "vec", right) + part[k]
+        total = total + lax.ppermute(acc, "vec", right)
+        if back:
+            acc = part[reach]
+            for k in range(1, back):
+                acc = lax.ppermute(acc, "vec", left) + part[reach + k]
+            total = total + lax.ppermute(acc, "vec", left)
+        return total
 
     return per_device
 

time: 78.5 us -> 71.2 us (0.907)
  starting transfers between devices: 25.5 us -> 18 us
  other arithmetic: 5.17 us -> 8.59 us
  local copies, waits for them, and re-layouts: 6.4 us -> 3.99 us
  matrix products: 7.16 us -> 6.05 us
    ppermute x15 -> x9, starting transfers between devices: 16.1 us -> 8.52 us  [the longest x3 5.07 us: per_device(): acc = lax.ppermute(acc, 'vec', right) + part[k]]
    ppermute x3, waiting for transfers between devices: 4.02 us -> 2.56 us  [ring_all_gather(): cur = lax.ppermute(cur, 'vec', left)]
    ppermute x4, waiting for transfers between devices: 3.57 us -> 4.9 us  [ring_all_gather(): cur = lax.ppermute(cur, 'vec', right)]
    gather x2, local copies, waits for them, and re-layouts: 1.93 us -> 0.68 us  [per_device(): jnp.take(by_group, order, axis=1, mode='clip').reshape(active_rotated.shape)]
    dot_general x1, matrix products: 1.73 us -> 0.76 us  [per_device(): jnp.einsum('gpr,grj->gpj', other_half, theirs, preferred_element_type=jnp...]
    concatenate x1 -> x0, local copies, waits for them, and re-layouts: 0.84 us -> none  [per_device(): return jnp.concatenate([acc_r, acc_l], axis=1)]
    select_n x1 -> x2, other arithmetic: 1.96 us -> 2.75 us  [ring_all_gather(): out = jnp.where(offset == d, pair[None], out)]
    ppermute x15 -> x9, waiting for transfers between devices: 24.8 us -> 25.4 us  [the longest x3 16.5 us: per_device(): acc = lax.ppermute(acc, 'vec', right) + part[k]]
  transfers between devices with their start and end apart: 30 -> 24, of which waited for: 20 -> 13; matrix products, arithmetic and copies ran while one was open for 11% -> 16% of each run, Pallas kernels for 0% -> 0%
where the time goes in v7:
time: 71.2 us; the launch traced here: 71 us
  waiting for transfers between devices  34.2 us (48%)
  starting transfers between devices  18 us (25%)
  other arithmetic  8.59 us (12%)
  matrix products  6.05 us (8%)
  local copies, waits for them, and re-layouts  3.99 us (6%)
    ppermute x3, waiting for transfers between devices, per_device(): acc = lax.ppermute(acc, 'vec', right) + part[k]  16.5 us
    ppermute x4, starting transfers between devices, ring_all_gather(): cur = lax.ppermute(cur, 'vec', right)  8.58 us
    ppermute x3, starting transfers between devices, per_device(): acc = lax.ppermute(acc, 'vec', right) + part[k]  5.07 us
    ppermute x4, waiting for transfers between devices, ring_all_gather(): cur = lax.ppermute(cur, 'vec', right)  4.9 us
    ppermute x1, waiting for transfers between devices, per_device(): total = total + lax.ppermute(acc, 'vec', right)  4.35 us
    ppermute x2, waiting for transfers between devices, per_device(): acc = lax.ppermute(acc, 'vec', left) + part[reach + k]  2.98 us
    select_n x2, other arithmetic, ring_all_gather(): out = jnp.where(offset == d, pair[None], out)  2.75 us
    ppermute x3, waiting for transfers between devices, ring_all_gather(): cur = lax.ppermute(cur, 'vec', left)  2.56 us
  transfers between devices with their start and end apart: 24, of which 13 were waited for; matrix products, arithmetic and copies ran while one was open for 16% of the time, Pallas kernels for 0%

profile of v7, /device:TPU:0, one launch (start us, length us, event | category | flops | bytes accessed | tf_op | source)
XLA Modules:
  0.0 71.0 jit_solution(7039635003822014296)
XLA Ops:
  0.0 3.1 %collective-permute-start = (bf16[64,1024]{1,0:T(8,128)(2,1)}, bf16[64,1024]{1,0:T(8,128)(2,1)S(1)}, u32[]{:S(2)}, u32[]{:S(2)}) collective-permute-start(bf16[64,1024]{1,0:T(8,128)(2,1)} %param.8), channel_id=1, source_target_pairs={{0,4},{4,8},{8,12},{12,14},{14,10},{10,6},{6,2},{2,0},{1,5},{5,9},... | collective-permute-start | bytes 393224 | tf_op jit(solution)/shard_map/ppermute | solution.py:46
  3.1 1.2 %dynamic_slice.3 = s32[1]{0:T(128)} dynamic-slice(s32[8]{0:T(128)} %constant.46.clone, s32[]{:T(128)S(6)} %select_n.245), dynamic_slice_sizes={1} | dynamic-slice | bytes 12 | tf_op jit(solution)/shard_map/dynamic_slice | solution.py:55
  4.3 1.3 %broadcast_compare_fusion.6 = (pred[8]{0:T(512)(128)(4,1)S(1)}, s32[8]{0:T(128)S(1)}) fusion(s32[8]{0:T(128)} %constant.46.clone, s32[]{:T(128)} %bitcast), kind=kLoop, calls=%fused_computation.74 | loop fusion | flops 104 | bytes 76 | tf_op jit(solution)/shard_map/eq | solution.py:61
  5.6 0.7 broadcast_multiply_fusion
  6.3 0.8 %select_reduce_fusion.1 = s32[8]{0:T(128)S(1)} fusion(s32[8,8]{1,0:T(8,128)} %constant.47.clone, pred[8]{0:T(512)(128)(4,1)S(1)} %iota_compare_fusion.7), kind=kLoop, calls=%fused_computation.58 | loop fusion | flops 120 | bytes 296 | tf_op jit(solution)/shard_map/reduce_sum | solution.py:123
  7.1 0.8 %select_reduce_fusion = s32[8]{0:T(128)S(1)} fusion(s32[8]{0:T(128)} %param.11, s32[8]{0:T(128)S(1)} %select_reduce_fusion.1), kind=kLoop, calls=%fused_computation.56 | loop fusion | flops 184 | bytes 96 | tf_op jit(solution)/shard_map/reduce_sum | solution.py:124
  7.9 2.1 %collective-permute-start.2 = (bf16[64,1024]{1,0:T(8,128)(2,1)S(1)}, bf16[64,1024]{1,0:T(8,128)(2,1)S(1)}, u32[]{:S(2)}, u32[]{:S(2)}) collective-permute-start(bf16[64,1024]{1,0:T(8,128)(2,1)S(1)} %collective-permute-done), channel_id=1, source_target_pairs={{0,4},{4,8},{8,12},{12,14},{14,10},{10,6},{6,2},{2,0},{1,5},{5,9},... | collective-permute-start | bytes 393224 | tf_op jit(solution)/shard_map/ppermute | solution.py:46
  10.0 0.2 collective-permute-start.1
  10.2 0.1 broadcast_in_dim.217
  10.3 0.1 broadcast_in_dim.218
  10.4 0.1 broadcast_in_dim.221
  10.5 0.1 broadcast_in_dim.222
  10.6 0.1 broadcast_in_dim.225
  10.6 0.1 broadcast_in_dim.226
  10.7 0.1 broadcast_in_dim.229
  10.8 0.1 broadcast_in_dim.230
  10.9 0.1 broadcast_in_dim.233
  11.0 0.1 broadcast_in_dim.234
  11.1 0.1 broadcast_in_dim.237
  11.1 0.1 broadcast_in_dim.238
  11.2 0.1 broadcast_in_dim.241
  11.3 0.1 broadcast_in_dim.242
  11.4 0.1 broadcast_in_dim.213
  11.5 0.1 broadcast_in_dim.214
  11.6 0.3 collective-permute-start.9
  11.9 1.0 %maximum_select_fusion.7 = bf16[2,64,1024]{2,1,0:T(8,128)(2,1)S(1)} fusion(bf16[1,64,1024]{2,1,0:T(8,128)(2,1)S(1)} %bitcast.91, bf16[1,64,1024]{2,1,0:T(8,128)(2,1)} %bitcast.87, pred[]{:T(512)S(6)} %eq.83), kind=kLoop, calls=%fused_computation.54 | loop fusion | flops 393216 | bytes 524289 | tf_op jit(solution)/shard_map/jit(_where)/select_n | solution.py:60
  13.0 1.1 %collective-permute-done.2 = bf16[64,1024]{1,0:T(8,128)(2,1)S(1)} collective-permute-done((bf16[64,1024]{1,0:T(8,128)(2,1)S(1)}, bf16[64,1024]{1,0:T(8,128)(2,1)S(1)}, u32[]{:S(2)}, u32[]{:S(2)}) %collective-permute-start.2) | collective-permute-done | bytes 131104 | tf_op jit(solution)/shard_map/ppermute | solution.py:46
  14.1 1.8 %collective-permute-start.4 = (bf16[64,1024]{1,0:T(8,128)(2,1)S(1)}, bf16[64,1024]{1,0:T(8,128)(2,1)S(1)}, u32[]{:S(2)}, u32[]{:S(2)}) collective-permute-start(bf16[64,1024]{1,0:T(8,128)(2,1)S(1)} %collective-permute-done.2), channel_id=1, source_target_pairs={{0,4},{4,8},{8,12},{12,14},{14,10},{10,6},{6,2},{2,0},{1,5},{5,9},... | collective-permute-start | bytes 393224 | tf_op jit(solution)/shard_map/ppermute | solution.py:46
  16.0 1.3 %collective-permute-done.9 = bf16[64,1024]{1,0:T(8,128)(2,1)S(1)} collective-permute-done((bf16[64,1024]{1,0:T(8,128)(2,1)S(1)}, bf16[64,1024]{1,0:T(8,128)(2,1)S(1)}, u32[]{:S(2)}, u32[]{:S(2)}) %collective-permute-start.9) | collective-permute-done | bytes 131104 | tf_op jit(solution)/shard_map/ppermute | solution.py:50
  17.3 0.3 collective-permute-start.10
  17.6 1.7 %collective-permute-done.4 = bf16[64,1024]{1,0:T(8,128)(2,1)S(1)} collective-permute-done((bf16[64,1024]{1,0:T(8,128)(2,1)S(1)}, bf16[64,1024]{1,0:T(8,128)(2,1)S(1)}, u32[]{:S(2)}, u32[]{:S(2)}) %collective-permute-start.4) | collective-permute-done | bytes 131104 | tf_op jit(solution)/shard_map/ppermute | solution.py:46
  19.3 1.6 %collective-permute-start.6 = (bf16[64,1024]{1,0:T(8,128)(2,1)S(1)}, bf16[64,1024]{1,0:T(8,128)(2,1)S(1)}, u32[]{:S(2)}, u32[]{:S(2)}) collective-permute-start(bf16[64,1024]{1,0:T(8,128)(2,1)S(1)} %collective-permute-done.4), channel_id=1, source_target_pairs={{0,4},{4,8},{8,12},{12,14},{14,10},{10,6},{6,2},{2,0},{1,5},{5,9},... | collective-permute-start | bytes 393224 | tf_op jit(solution)/shard_map/ppermute | solution.py:46
  21.0 1.2 %collective-permute-done.10 = bf16[64,1024]{1,0:T(8,128)(2,1)S(1)} collective-permute-done((bf16[64,1024]{1,0:T(8,128)(2,1)S(1)}, bf16[64,1024]{1,0:T(8,128)(2,1)S(1)}, u32[]{:S(2)}, u32[]{:S(2)}) %collective-permute-start.10) | collective-permute-done | bytes 131104 | tf_op jit(solution)/shard_map/ppermute | solution.py:50
  22.3 2.0 %collective-permute-done.6 = bf16[64,1024]{1,0:T(8,128)(2,1)S(1)} collective-permute-done((bf16[64,1024]{1,0:T(8,128)(2,1)S(1)}, bf16[64,1024]{1,0:T(8,128)(2,1)S(1)}, u32[]{:S(2)}, u32[]{:S(2)}) %collective-permute-start.6) | collective-permute-done | bytes 131104 | tf_op jit(solution)/shard_map/ppermute | solution.py:46
  24.4 1.3 %collective-permute-done.7 = bf16[64,1024]{1,0:T(8,128)(2,1)S(1)} collective-permute-done((bf16[64,1024]{1,0:T(8,128)(2,1)S(1)}, bf16[64,1024]{1,0:T(8,128)(2,1)S(1)}, u32[]{:S(2)}, u32[]{:S(2)}) %collective-permute-start.7) | collective-permute-done | bytes 131104 | tf_op jit(solution)/shard_map/ppermute | solution.py:53
  25.7 0.9 %select_select_fusion = bf16[8,2,64,1024]{3,2,1,0:T(8,128)(2,1)S(1)} fusion(pred[8]{0:T(512)(128)(4,1)S(1)} %get-tuple-element.19, pred[8]{0:T(512)(128)(4,1)S(1)} %get-tuple-element.14, pred[8]{0:T(512)(128)(4,1)S(1)} %get-tuple-element.15, pred[8]{0:T(512)(128)(4,1)S(1)} %get-tuple-element.16, pred[8]{0:T(512)(128)(4,1)S(1)} %get-tuple-element.17, ...), kind=kLoop, calls=%fused_computation.21 | loop fusion | flops 8388608 | bytes 4194368 | tf_op jit(solution)/shard_map/jit(_where)/select_n | solution.py:61
  26.6 0.6 copy-done.1
  27.3 1.3 %convolution_convert_fusion.1 = bf16[1024,512]{1,0:T(8,128)(2,1)S(1)} fusion(bf16[1024,1024]{1,0:T(8,128)(2,1)S(1)} %bitcast.84, bf16[2,1024,512]{2,1,0:T(8,128)(2,1)S(1)} %copy-done.1), kind=kOutput, calls=%fused_computation.25 | convolution fusion | flops 1074266112 | bytes 4194304 | tf_op jit(solution)/shard_map/sp,sr->pr/dot_general | solution.py:77
  28.6 1.3 %convolution_convert_fusion = bf16[1024,512]{1,0:T(8,128)(2,1)S(1)} fusion(bf16[1024,1024]{1,0:T(8,128)(2,1)S(1)} %bitcast.85, bf16[2,1024,512]{2,1,0:T(8,128)(2,1)S(1)} %copy-done.1), kind=kOutput, calls=%fused_computation.24 | convolution fusion | flops 1074266112 | bytes 4194304 | tf_op jit(solution)/shard_map/sp,sr->pr/dot_general | solution.py:77
  29.9 0.2 collective-permute-start.15
  30.1 0.4 collective-permute-start.16
  30.5 1.8 %fusion.16 = bf16[1024,1024]{1,0:T(8,128)(2,1)S(1)} fusion(pred[1024]{0:T(1024)(128)(4,1)S(1)} %broadcast_in_dim.242, pred[1024]{0:T(1024)(128)(4,1)S(1)} %broadcast_in_dim.238, pred[1024]{0:T(1024)(128)(4,1)S(1)} %broadcast_in_dim.234, pred[1024]{0:T(1024)(128)(4,1)S(1)} %broadcast_in_dim.230, pred[1024]{0:T(1024)(128)(4,1)S(1)} %broadcast_in_dim.226, ...), kind=kLoop, calls=%fused_computation.18 | loop fusion | flops 8388608 | bytes 4202496 | tf_op jit(solution)/shard_map/jit(_where)/select_n | solution.py:61
  32.3 1.3 %fusion.22 = bf16[2,1024,256]{1,2,0:T(8,128)(2,1)S(1)} fusion(bf16[1024,1024]{1,0:T(8,128)(2,1)S(1)} %fusion.16, s32[2,256]{1,0:T(2,128)S(1)} %bitcast_add_fusion), kind=kOutput, calls=%fused_computation.26 | convolution fusion | flops 1074790400 | bytes 3147776 | tf_op jit(solution)/shard_map/rc,gcj->grj/dot_general | solution.py:89
  33.6 0.7 %fusion = f32[2,1024,256]{2,1,0:T(8,128)S(1)} fusion(bf16[1,1024,512]{2,1,0:T(8,128)(2,1)S(1)} %bitcast.104, bf16[1,1024,512]{2,1,0:T(8,128)(2,1)S(1)} %bitcast.106, pred[]{:T(512)S(6)} %eq.83, bf16[2,1024,256]{1,2,0:T(8,128)(2,1)S(1)} %fusion.22), kind=kOutput, calls=%fused_computation.1 | convolution fusion | flops 538181632 | bytes 5242881 | tf_op jit(solution)/shard_map/gpr,grj->gpj/dot_general | solution.py:98
  34.4 0.8 %add_convert_fusion = bf16[2,1024,256]{2,1,0:T(8,128)(2,1)S(1)} fusion(f32[2,1024,256]{2,1,0:T(8,128)S(1)} %fusion, bf16[1,1024,512]{2,1,0:T(8,128)(2,1)S(1)} %bitcast.105, bf16[1,1024,512]{2,1,0:T(8,128)(2,1)S(1)} %bitcast.103, pred[]{:T(512)S(6)} %eq.83, bf16[2,1024,256]{1,2,0:T(8,128)(2,1)S(1)} %fusion.22), kind=kOutput, calls=%fused_computation.19 | convolution fusion | flops 539230208 | bytes 6291457 | tf_op jit(solution)/shard_map/gpr,grj->gpj/dot_general | solution.py:99
  35.2 0.6 gather_fusion
  35.9 0.7 convolution_bitcast_fusion
  36.6 1.7 %collective-permute-start.17 = (f32[128,512]{1,0:T(8,128)S(1)}, f32[128,512]{1,0:T(8,128)S(1)}, u32[]{:S(2)}, u32[]{:S(2)}) collective-permute-start(f32[128,512]{1,0:T(8,128)S(1)} %slice.53), channel_id=1, source_target_pairs={{0,4},{4,8},{8,12},{12,14},{14,10},{10,6},{6,2},{2,0},{1,5},{5,9},... | collective-permute-start | bytes 786440 | tf_op jit(solution)/shard_map/ppermute | solution.py:137
  38.3 6.7 %collective-permute-done.17 = f32[128,512]{1,0:T(8,128)S(1)} collective-permute-done((f32[128,512]{1,0:T(8,128)S(1)}, f32[128,512]{1,0:T(8,128)S(1)}, u32[]{:S(2)}, u32[]{:S(2)}) %collective-permute-start.17) | collective-permute-done | bytes 262176 | tf_op jit(solution)/shard_map/ppermute | solution.py:137
  45.1 1.7 %collective-permute-start.18 = (f32[128,512]{1,0:T(8,128)S(1)}, f32[128,512]{1,0:T(8,128)S(1)}, u32[]{:S(2)}, u32[]{:S(2)}) collective-permute-start(f32[128,512]{1,0:T(8,128)S(1)} %get-tuple-element.11), channel_id=1, source_target_pairs={{0,4},{4,8},{8,12},{12,14},{14,10},{10,6},{6,2},{2,0},{1,5},{5,9},... | collective-permute-start | bytes 786440 | tf_op jit(solution)/shard_map/ppermute | solution.py:137
  46.8 0.4 collective-permute-start.21
  47.2 5.5 %collective-permute-done.18 = f32[128,512]{1,0:T(8,128)S(1)} collective-permute-done((f32[128,512]{1,0:T(8,128)S(1)}, f32[128,512]{1,0:T(8,128)S(1)}, u32[]{:S(2)}, u32[]{:S(2)}) %collective-permute-start.18) | collective-permute-done | bytes 262176 | tf_op jit(solution)/shard_map/ppermute | solution.py:137
  52.6 1.4 %collective-permute-done.21 = f32[128,512]{1,0:T(8,128)S(1)} collective-permute-done((f32[128,512]{1,0:T(8,128)S(1)}, f32[128,512]{1,0:T(8,128)S(1)}, u32[]{:S(2)}, u32[]{:S(2)}) %collective-permute-start.21) | collective-permute-done | bytes 262176 | tf_op jit(solution)/shard_map/ppermute | solution.py:142
  54.0 0.1 slice_add_fusion.3
  54.1 1.6 %collective-permute-start.19 = (f32[128,512]{1,0:T(8,128)S(1)}, f32[128,512]{1,0:T(8,128)S(1)}, u32[]{:S(2)}, u32[]{:S(2)}) collective-permute-start(f32[128,512]{1,0:T(8,128)S(1)} %get-tuple-element.9), channel_id=1, source_target_pairs={{0,4},{4,8},{8,12},{12,14},{14,10},{10,6},{6,2},{2,0},{1,5},{5,9},... | collective-permute-start | bytes 786440 | tf_op jit(solution)/shard_map/ppermute | solution.py:137
  55.8 0.4 collective-permute-start.22
  56.2 4.3 %collective-permute-done.19 = f32[128,512]{1,0:T(8,128)S(1)} collective-permute-done((f32[128,512]{1,0:T(8,128)S(1)}, f32[128,512]{1,0:T(8,128)S(1)}, u32[]{:S(2)}, u32[]{:S(2)}) %collective-permute-start.19) | collective-permute-done | bytes 262176 | tf_op jit(solution)/shard_map/ppermute | solution.py:137
  60.5 1.6 %collective-permute-done.22 = f32[128,512]{1,0:T(8,128)S(1)} collective-permute-done((f32[128,512]{1,0:T(8,128)S(1)}, f32[128,512]{1,0:T(8,128)S(1)}, u32[]{:S(2)}, u32[]{:S(2)}) %collective-permute-start.22) | collective-permute-done | bytes 262176 | tf_op jit(solution)/shard_map/ppermute | solution.py:142
  62.1 0.1 slice_add_fusion.2
  62.2 1.6 %collective-permute-start.20 = (f32[128,512]{1,0:T(8,128)S(1)}, f32[128,512]{1,0:T(8,128)S(1)}, u32[]{:S(2)}, u32[]{:S(2)}) collective-permute-start(f32[128,512]{1,0:T(8,128)S(1)} %get-tuple-element.7), channel_id=1, source_target_pairs={{0,4},{4,8},{8,12},{12,14},{14,10},{10,6},{6,2},{2,0},{1,5},{5,9},... | collective-permute-start | bytes 786440 | tf_op jit(solution)/shard_map/ppermute | solution.py:138
  63.9 0.4 collective-permute-start.23
  64.3 4.3 %collective-permute-done.20 = f32[128,512]{1,0:T(8,128)S(1)} collective-permute-done((f32[128,512]{1,0:T(8,128)S(1)}, f32[128,512]{1,0:T(8,128)S(1)}, u32[]{:S(2)}, u32[]{:S(2)}) %collective-permute-start.20) | collective-permute-done | bytes 262176 | tf_op jit(solution)/shard_map/ppermute | solution.py:138
  68.6 1.6 %collective-permute-done.23 = f32[128,512]{1,0:T(8,128)S(1)} collective-permute-done((f32[128,512]{1,0:T(8,128)S(1)}, f32[128,512]{1,0:T(8,128)S(1)}, u32[]{:S(2)}, u32[]{:S(2)}) %collective-permute-start.23) | collective-permute-done | bytes 262176 | tf_op jit(solution)/shard_map/ppermute | solution.py:143
  70.2 0.8 %fusion.38 = f32[128,512]{1,0:T(8,128)} fusion(f32[128,512]{1,0:T(8,128)S(1)} %collective-permute-done.23, f32[128,512]{1,0:T(8,128)S(1)} %collective-permute-done.20, f32[1024,512]{1,0:T(8,128)S(1)} %convolution_bitcast_fusion), kind=kLoop, calls=%fused_computation.46 | loop fusion | flops 131072 | bytes 1048576 | tf_op jit(solution)/shard_map/add | solution.py:143
  (38 shorter events, 0.6 us)
Async XLA Ops:
  0.0 35.9 %copy-start = (bf16[2,256,512]{2,1,0:T(8,128)(2,1)S(1)}, bf16[2,256,512]{2,1,0:T(8,128)(2,1)}, u32[]{:S(2)}) copy-start(bf16[2,256,512]{2,1,0:T(8,128)(2,1)} %param.10) | copy-start | bytes 1572868
  0.0 7.9 %collective-permute-start = (bf16[64,1024]{1,0:T(8,128)(2,1)}, bf16[64,1024]{1,0:T(8,128)(2,1)S(1)}, u32[]{:S(2)}, u32[]{:S(2)}) collective-permute-start(bf16[64,1024]{1,0:T(8,128)(2,1)} %param.8), channel_id=1, source_target_pairs={{0,4},{4,8},{8,12},{12,14},{14,10},{10,6},{6,2},{2,0},{1,5},{5,9},... | collective-permute-start | bytes 393224 | tf_op jit(solution)/shard_map/ppermute | solution.py:46
  3.1 8.5 %collective-permute-start.8 = (bf16[64,1024]{1,0:T(8,128)(2,1)}, bf16[64,1024]{1,0:T(8,128)(2,1)S(1)}, u32[]{:S(2)}, u32[]{:S(2)}) collective-permute-start(bf16[64,1024]{1,0:T(8,128)(2,1)} %param.8), channel_id=1, source_target_pairs={{0,2},{4,0},{8,4},{12,8},{14,12},{10,14},{6,10},{2,6},{1,3},{5,1},... | collective-permute-start | bytes 393224 | tf_op jit(solution)/shard_map/ppermute | solution.py:50
  3.1 8.9 %collective-permute-start.14 = (bf16[64,1024]{1,0:T(8,128)(2,1)}, bf16[64,1024]{1,0:T(8,128)(2,1)S(1)}, u32[]{:S(2)}, u32[]{:S(2)}) collective-permute-start(bf16[64,1024]{1,0:T(8,128)(2,1)} %param.8), channel_id=1, source_target_pairs={{0,1},{1,0},{2,3},{3,2},{4,5},{5,4},{6,7},{7,6},{8,9},{9,8},{10,11... | collective-permute-start | bytes 393224 | tf_op jit(solution)/shard_map/ppermute | solution.py:53
  7.9 6.2 %collective-permute-start.2 = (bf16[64,1024]{1,0:T(8,128)(2,1)S(1)}, bf16[64,1024]{1,0:T(8,128)(2,1)S(1)}, u32[]{:S(2)}, u32[]{:S(2)}) collective-permute-start(bf16[64,1024]{1,0:T(8,128)(2,1)S(1)} %collective-permute-done), channel_id=1, source_target_pairs={{0,4},{4,8},{8,12},{12,14},{14,10},{10,6},{6,2},{2,0},{1,5},{5,9},... | collective-permute-start | bytes 393224 | tf_op jit(solution)/shard_map/ppermute | solution.py:46
  10.0 5.9 %collective-permute-start.1 = (bf16[64,1024]{1,0:T(8,128)(2,1)S(1)}, bf16[64,1024]{1,0:T(8,128)(2,1)S(1)}, u32[]{:S(2)}, u32[]{:S(2)}) collective-permute-start(bf16[64,1024]{1,0:T(8,128)(2,1)S(1)} %collective-permute-done), channel_id=1, source_target_pairs={{0,1},{1,0},{2,3},{3,2},{4,5},{5,4},{6,7},{7,6},{8,9},{9,8},{10,11... | collective-permute-start | bytes 393224 | tf_op jit(solution)/shard_map/ppermute | solution.py:53
  11.6 5.7 %collective-permute-start.9 = (bf16[64,1024]{1,0:T(8,128)(2,1)S(1)}, bf16[64,1024]{1,0:T(8,128)(2,1)S(1)}, u32[]{:S(2)}, u32[]{:S(2)}) collective-permute-start(bf16[64,1024]{1,0:T(8,128)(2,1)S(1)} %collective-permute-done.8), channel_id=1, source_target_pairs={{0,2},{4,0},{8,4},{12,8},{14,12},{10,14},{6,10},{2,6},{1,3},{5,1},... | collective-permute-start | bytes 393224 | tf_op jit(solution)/shard_map/ppermute | solution.py:50
  11.9 5.7 %collective-permute-start.13 = (bf16[64,1024]{1,0:T(8,128)(2,1)S(1)}, bf16[64,1024]{1,0:T(8,128)(2,1)S(1)}, u32[]{:S(2)}, u32[]{:S(2)}) collective-permute-start(bf16[64,1024]{1,0:T(8,128)(2,1)S(1)} %collective-permute-done.8), channel_id=1, source_target_pairs={{0,1},{1,0},{2,3},{3,2},{4,5},{5,4},{6,7},{7,6},{8,9},{9,8},{10,11... | collective-permute-start | bytes 393224 | tf_op jit(solution)/shard_map/ppermute | solution.py:53
  14.1 5.2 %collective-permute-start.4 = (bf16[64,1024]{1,0:T(8,128)(2,1)S(1)}, bf16[64,1024]{1,0:T(8,128)(2,1)S(1)}, u32[]{:S(2)}, u32[]{:S(2)}) collective-permute-start(bf16[64,1024]{1,0:T(8,128)(2,1)S(1)} %collective-permute-done.2), channel_id=1, source_target_pairs={{0,4},{4,8},{8,12},{12,14},{14,10},{10,6},{6,2},{2,0},{1,5},{5,9},... | collective-permute-start | bytes 393224 | tf_op jit(solution)/shard_map/ppermute | solution.py:46
  15.9 5.1 %collective-permute-start.3 = (bf16[64,1024]{1,0:T(8,128)(2,1)S(1)}, bf16[64,1024]{1,0:T(8,128)(2,1)S(1)}, u32[]{:S(2)}, u32[]{:S(2)}) collective-permute-start(bf16[64,1024]{1,0:T(8,128)(2,1)S(1)} %collective-permute-done.2), channel_id=1, source_target_pairs={{0,1},{1,0},{2,3},{3,2},{4,5},{5,4},{6,7},{7,6},{8,9},{9,8},{10,11... | collective-permute-start | bytes 393224 | tf_op jit(solution)/shard_map/ppermute | solution.py:53
  17.3 5.0 %collective-permute-start.10 = (bf16[64,1024]{1,0:T(8,128)(2,1)S(1)}, bf16[64,1024]{1,0:T(8,128)(2,1)S(1)}, u32[]{:S(2)}, u32[]{:S(2)}) collective-permute-start(bf16[64,1024]{1,0:T(8,128)(2,1)S(1)} %collective-permute-done.9), channel_id=1, source_target_pairs={{0,2},{4,0},{8,4},{12,8},{14,12},{10,14},{6,10},{2,6},{1,3},{5,1},... | collective-permute-start | bytes 393224 | tf_op jit(solution)/shard_map/ppermute | solution.py:50
  17.6 4.7 %collective-permute-start.12 = (bf16[64,1024]{1,0:T(8,128)(2,1)S(1)}, bf16[64,1024]{1,0:T(8,128)(2,1)S(1)}, u32[]{:S(2)}, u32[]{:S(2)}) collective-permute-start(bf16[64,1024]{1,0:T(8,128)(2,1)S(1)} %collective-permute-done.9), channel_id=1, source_target_pairs={{0,1},{1,0},{2,3},{3,2},{4,5},{5,4},{6,7},{7,6},{8,9},{9,8},{10,11... | collective-permute-start | bytes 393224 | tf_op jit(solution)/shard_map/ppermute | solution.py:53
  19.3 5.0 %collective-permute-start.6 = (bf16[64,1024]{1,0:T(8,128)(2,1)S(1)}, bf16[64,1024]{1,0:T(8,128)(2,1)S(1)}, u32[]{:S(2)}, u32[]{:S(2)}) collective-permute-start(bf16[64,1024]{1,0:T(8,128)(2,1)S(1)} %collective-permute-done.4), channel_id=1, source_target_pairs={{0,4},{4,8},{8,12},{12,14},{14,10},{10,6},{6,2},{2,0},{1,5},{5,9},... | collective-permute-start | bytes 393224 | tf_op jit(solution)/shard_map/ppermute | solution.py:46
  21.0 3.3 %collective-permute-start.5 = (bf16[64,1024]{1,0:T(8,128)(2,1)S(1)}, bf16[64,1024]{1,0:T(8,128)(2,1)S(1)}, u32[]{:S(2)}, u32[]{:S(2)}) collective-permute-start(bf16[64,1024]{1,0:T(8,128)(2,1)S(1)} %collective-permute-done.4), channel_id=1, source_target_pairs={{0,1},{1,0},{2,3},{3,2},{4,5},{5,4},{6,7},{7,6},{8,9},{9,8},{10,11... | collective-permute-start | bytes 393224 | tf_op jit(solution)/shard_map/ppermute | solution.py:53
  22.2 2.1 %collective-permute-start.11 = (bf16[64,1024]{1,0:T(8,128)(2,1)S(1)}, bf16[64,1024]{1,0:T(8,128)(2,1)S(1)}, u32[]{:S(2)}, u32[]{:S(2)}) collective-permute-start(bf16[64,1024]{1,0:T(8,128)(2,1)S(1)} %collective-permute-done.10), channel_id=1, source_target_pairs={{0,1},{1,0},{2,3},{3,2},{4,5},{5,4},{6,7},{7,6},{8,9},{9,8},{10,11... | collective-permute-start | bytes 393224 | tf_op jit(solution)/shard_map/ppermute | solution.py:53
  24.3 1.3 %collective-permute-start.7 = (bf16[64,1024]{1,0:T(8,128)(2,1)S(1)}, bf16[64,1024]{1,0:T(8,128)(2,1)S(1)}, u32[]{:S(2)}, u32[]{:S(2)}) collective-permute-start(bf16[64,1024]{1,0:T(8,128)(2,1)S(1)} %collective-permute-done.6), channel_id=1, source_target_pairs={{0,1},{1,0},{2,3},{3,2},{4,5},{5,4},{6,7},{7,6},{8,9},{9,8},{10,11... | collective-permute-start | bytes 393224 | tf_op jit(solution)/shard_map/ppermute | solution.py:53
  25.7 1.6 %copy-start.1 = (bf16[2,1024,512]{2,1,0:T(8,128)(2,1)S(1)}, bf16[2,1024,512]{2,1,0:T(8,128)(2,1)}, u32[]{:S(2)}) copy-start(bf16[2,1024,512]{2,1,0:T(8,128)(2,1)} %param.7) | copy-start | bytes 6291460
  29.9 4.5 %collective-permute-start.15 = (bf16[1024,512]{1,0:T(8,128)(2,1)S(1)}, bf16[1024,512]{1,0:T(8,128)(2,1)S(1)}, u32[]{:S(2)}, u32[]{:S(2)}) collective-permute-start(bf16[1024,512]{1,0:T(8,128)(2,1)S(1)} %convolution_convert_fusion.1), channel_id=1, source_target_pairs={{0,1},{1,0},{2,3},{3,2},{4,5},{5,4},{6,7},{7,6},{8,9},{9,8},{10,11... | collective-permute-start | bytes 3145736 | tf_op jit(solution)/shard_map/ppermute | solution.py:80
  30.1 4.3 %collective-permute-start.16 = (bf16[1024,512]{1,0:T(8,128)(2,1)S(1)}, bf16[1024,512]{1,0:T(8,128)(2,1)S(1)}, u32[]{:S(2)}, u32[]{:S(2)}) collective-permute-start(bf16[1024,512]{1,0:T(8,128)(2,1)S(1)} %convolution_convert_fusion), channel_id=1, source_target_pairs={{0,1},{1,0},{2,3},{3,2},{4,5},{5,4},{6,7},{7,6},{8,9},{9,8},{10,11... | collective-permute-start | bytes 3145736 | tf_op jit(solution)/shard_map/ppermute | solution.py:80
  36.6 8.4 %collective-permute-start.17 = (f32[128,512]{1,0:T(8,128)S(1)}, f32[128,512]{1,0:T(8,128)S(1)}, u32[]{:S(2)}, u32[]{:S(2)}) collective-permute-start(f32[128,512]{1,0:T(8,128)S(1)} %slice.53), channel_id=1, source_target_pairs={{0,4},{4,8},{8,12},{12,14},{14,10},{10,6},{6,2},{2,0},{1,5},{5,9},... | collective-permute-start | bytes 786440 | tf_op jit(solution)/shard_map/ppermute | solution.py:137
  45.1 7.6 %collective-permute-start.18 = (f32[128,512]{1,0:T(8,128)S(1)}, f32[128,512]{1,0:T(8,128)S(1)}, u32[]{:S(2)}, u32[]{:S(2)}) collective-permute-start(f32[128,512]{1,0:T(8,128)S(1)} %get-tuple-element.11), channel_id=1, source_target_pairs={{0,4},{4,8},{8,12},{12,14},{14,10},{10,6},{6,2},{2,0},{1,5},{5,9},... | collective-permute-start | bytes 786440 | tf_op jit(solution)/shard_map/ppermute | solution.py:137
  46.8 7.2 %collective-permute-start.21 = (f32[128,512]{1,0:T(8,128)S(1)}, f32[128,512]{1,0:T(8,128)S(1)}, u32[]{:S(2)}, u32[]{:S(2)}) collective-permute-start(f32[128,512]{1,0:T(8,128)S(1)} %get-tuple-element.12), channel_id=1, source_target_pairs={{0,2},{4,0},{8,4},{12,8},{14,12},{10,14},{6,10},{2,6},{1,3},{5,1},... | collective-permute-start | bytes 786440 | tf_op jit(solution)/shard_map/ppermute | solution.py:142
  54.1 6.4 %collective-permute-start.19 = (f32[128,512]{1,0:T(8,128)S(1)}, f32[128,512]{1,0:T(8,128)S(1)}, u32[]{:S(2)}, u32[]{:S(2)}) collective-permute-start(f32[128,512]{1,0:T(8,128)S(1)} %get-tuple-element.9), channel_id=1, source_target_pairs={{0,4},{4,8},{8,12},{12,14},{14,10},{10,6},{6,2},{2,0},{1,5},{5,9},... | collective-permute-start | bytes 786440 | tf_op jit(solution)/shard_map/ppermute | solution.py:137
  55.8 6.4 %collective-permute-start.22 = (f32[128,512]{1,0:T(8,128)S(1)}, f32[128,512]{1,0:T(8,128)S(1)}, u32[]{:S(2)}, u32[]{:S(2)}) collective-permute-start(f32[128,512]{1,0:T(8,128)S(1)} %get-tuple-element.10), channel_id=1, source_target_pairs={{0,2},{4,0},{8,4},{12,8},{14,12},{10,14},{6,10},{2,6},{1,3},{5,1},... | collective-permute-start | bytes 786440 | tf_op jit(solution)/shard_map/ppermute | solution.py:142
  62.2 6.4 %collective-permute-start.20 = (f32[128,512]{1,0:T(8,128)S(1)}, f32[128,512]{1,0:T(8,128)S(1)}, u32[]{:S(2)}, u32[]{:S(2)}) collective-permute-start(f32[128,512]{1,0:T(8,128)S(1)} %get-tuple-element.7), channel_id=1, source_target_pairs={{0,4},{4,8},{8,12},{12,14},{14,10},{10,6},{6,2},{2,0},{1,5},{5,9},... | collective-permute-start | bytes 786440 | tf_op jit(solution)/shard_map/ppermute | solution.py:138
  63.9 6.4 %collective-permute-start.23 = (f32[128,512]{1,0:T(8,128)S(1)}, f32[128,512]{1,0:T(8,128)S(1)}, u32[]{:S(2)}, u32[]{:S(2)}) collective-permute-start(f32[128,512]{1,0:T(8,128)S(1)} %get-tuple-element.8), channel_id=1, source_target_pairs={{0,2},{4,0},{8,4},{12,8},{14,12},{10,14},{6,10},{2,6},{1,3},{5,1},... | collective-permute-start | bytes 786440 | tf_op jit(solution)/shard_map/ppermute | solution.py:143

commit v8 on v7

--- a/solution.py
+++ b/solution.py
@@ -116,6 +116,7 @@
         reach = n // 2
         back = n - 1 - reach
         shifts = list(range(reach, 0, -1)) + list(range(-back, 0)) + [0]
+        even = n % 2 == 0
         table = np.array([[ring[(p + d) % n] for d in shifts] for p in range(n)], np.int32)
         pos_of = np.argsort(np.array(ring))
         by_vec = jnp.asarray(table[pos_of])
@@ -131,17 +132,30 @@
         ).reshape(n, per, -1)
         right = [(ring[i], ring[(i + 1) % n]) for i in range(n)]
         left = [(ring[i], ring[(i - 1) % n]) for i in range(n)]
-        total = part[n - 1]
-        acc = part[0]
+        if even:
+            cut = part.shape[2] // 2
+            got_r = lax.ppermute(part[0][:, :cut], "vec", right)
+            got_l = lax.ppermute(part[0][:, cut:], "vec", left)
+            if reach == 1:
+                return part[n - 1] + jnp.concatenate([got_r, got_l], axis=1)
+            acc_r = jnp.concatenate([got_r + part[1][:, :cut], part[1][:, cut:]], axis=1)
+            acc_l = jnp.concatenate([part[reach][:, :cut], got_l + part[reach][:, cut:]], axis=1)
+            for k in range(2, reach):
+                acc_r = lax.ppermute(acc_r, "vec", right) + part[k]
+                acc_l = lax.ppermute(acc_l, "vec", left) + part[reach + k - 1]
+            return (
+                part[n - 1]
+                + lax.ppermute(acc_r, "vec", right)
+                + lax.ppermute(acc_l, "vec", left)
+            )
+        acc_r = part[0]
+        acc_l = part[reach]
         for k in range(1, reach):
-            acc = lax.ppermute(acc, "vec", right) + part[k]
-        total = total + lax.ppermute(acc, "vec", right)
-        if back:
-            acc = part[reach]
-            for k in range(1, back):
-                acc = lax.ppermute(acc, "vec", left) + part[reach + k]
-            total = total + lax.ppermute(acc, "vec", left)
-        return total
+            acc_r = lax.ppermute(acc_r, "vec", right) + part[k]
+            if k < back:
+                acc_l = lax.ppermute(acc_l, "vec", left) + part[reach + k]
+        total = part[n - 1] + lax.ppermute(acc_r, "vec", right)
+        return total + lax.ppermute(acc_l, "vec", left) if back else total
 
     return per_device
 

time: 71.2 us -> 68.6 us (0.963)
  waiting for transfers between devices: 34.2 us -> 30.9 us
  local copies, waits for them, and re-layouts: 3.99 us -> 4.84 us
    ppermute x7 -> x8, waiting for transfers between devices: 25.4 us -> 22.1 us  [the longest x2 6.7 us: per_device(): acc_l = lax.ppermute(acc_l, 'vec', left) + part[reach + k - 1]]
    add x0 -> x1, local copies, waits for them, and re-layouts: none -> 0.84 us  [per_device(): part[n - 1] + lax.ppermute(acc_r, 'vec', right)]
    add x4, other arithmetic: 1 us -> 0.28 us  [the longest x2 0.16 us: per_device(): acc_r = lax.ppermute(acc_r, 'vec', right) + part[k]]
    ppermute x7 -> x8, starting transfers between devices: 7.95 us -> 8.36 us  [the longest x2 3.33 us: per_device(): acc_r = lax.ppermute(acc_r, 'vec', right) + part[k]]
  transfers between devices with their start and end apart: 24 -> 25, of which waited for: 13 -> 14; matrix products, arithmetic and copies ran while one was open for 16% -> 17% of each run, Pallas kernels for 0% -> 0%
where the time goes in v8:
time: 68.6 us; the launch traced here: 68.4 us
  waiting for transfers between devices  30.9 us (45%)
  starting transfers between devices  18.4 us (27%)
  other arithmetic  7.91 us (12%)
  matrix products  6.11 us (9%)
  local copies, waits for them, and re-layouts  4.84 us (7%)
    ppermute x4, starting transfers between devices, ring_all_gather(): cur = lax.ppermute(cur, 'vec', right)  8.58 us
    ppermute x2, waiting for transfers between devices, per_device(): acc_l = lax.ppermute(acc_l, 'vec', left) + part[reach + k - 1]  6.7 us
    ppermute x4, waiting for transfers between devices, ring_all_gather(): cur = lax.ppermute(cur, 'vec', right)  4.9 us
    ppermute x2, waiting for transfers between devices, per_device(): acc_r = lax.ppermute(acc_r, 'vec', right) + part[k]  4.59 us
    ppermute x1, waiting for transfers between devices, per_device(): lax.ppermute(acc_r, 'vec', right)  4.35 us
    ppermute x1, waiting for transfers between devices, per_device(): got_r = lax.ppermute(part[0][:, :cut], 'vec', right)  3.52 us
    ppermute x2, starting transfers between devices, per_device(): acc_r = lax.ppermute(acc_r, 'vec', right) + part[k]  3.33 us
    select_n x2, other arithmetic, ring_all_gather(): out = jnp.where(offset == d, pair[None], out)  2.75 us
  transfers between devices with their start and end apart: 25, of which 14 were waited for; matrix products, arithmetic and copies ran while one was open for 17% of the time, Pallas kernels for 0%

profile of v8, /device:TPU:0, one launch (start us, length us, event | category | flops | bytes accessed | tf_op | source)
XLA Modules:
  0.0 68.4 jit_solution(6279617265430553632)
XLA Ops:
  0.0 3.1 %collective-permute-start = (bf16[64,1024]{1,0:T(8,128)(2,1)}, bf16[64,1024]{1,0:T(8,128)(2,1)S(1)}, u32[]{:S(2)}, u32[]{:S(2)}) collective-permute-start(bf16[64,1024]{1,0:T(8,128)(2,1)} %param.8), channel_id=1, source_target_pairs={{0,4},{4,8},{8,12},{12,14},{14,10},{10,6},{6,2},{2,0},{1,5},{5,9},... | collective-permute-start | bytes 393224 | tf_op jit(solution)/shard_map/ppermute | solution.py:46
  3.1 1.2 %dynamic_slice.3 = s32[1]{0:T(128)} dynamic-slice(s32[8]{0:T(128)} %constant.46.clone, s32[]{:T(128)S(6)} %select_n.245), dynamic_slice_sizes={1} | dynamic-slice | bytes 12 | tf_op jit(solution)/shard_map/dynamic_slice | solution.py:55
  4.3 1.3 %broadcast_compare_fusion.6 = (pred[8]{0:T(512)(128)(4,1)S(1)}, s32[8]{0:T(128)S(1)}) fusion(s32[8]{0:T(128)} %constant.46.clone, s32[]{:T(128)} %bitcast), kind=kLoop, calls=%fused_computation.77 | loop fusion | flops 104 | bytes 76 | tf_op jit(solution)/shard_map/eq | solution.py:61
  5.6 0.7 %broadcast_multiply_fusion = s32[2,2]{1,0:T(2,128)S(1)} fusion(s32[2,2]{1,0:T(2,128)} %param.9), kind=kLoop, calls=%fused_computation.70 | loop fusion | flops 4 | bytes 32 | tf_op jit(solution)/shard_map/mul | solution.py:83
  6.3 0.8 %select_reduce_fusion.1 = s32[8]{0:T(128)S(1)} fusion(s32[8,8]{1,0:T(8,128)} %constant.47.clone, pred[8]{0:T(512)(128)(4,1)S(1)} %iota_compare_fusion.7), kind=kLoop, calls=%fused_computation.61 | loop fusion | flops 120 | bytes 296 | tf_op jit(solution)/shard_map/reduce_sum | solution.py:124
  7.1 0.8 %select_reduce_fusion = s32[8]{0:T(128)S(1)} fusion(s32[8]{0:T(128)} %param.11, s32[8]{0:T(128)S(1)} %select_reduce_fusion.1), kind=kLoop, calls=%fused_computation.59 | loop fusion | flops 184 | bytes 96 | tf_op jit(solution)/shard_map/reduce_sum | solution.py:125
  7.9 2.1 %collective-permute-start.2 = (bf16[64,1024]{1,0:T(8,128)(2,1)S(1)}, bf16[64,1024]{1,0:T(8,128)(2,1)S(1)}, u32[]{:S(2)}, u32[]{:S(2)}) collective-permute-start(bf16[64,1024]{1,0:T(8,128)(2,1)S(1)} %collective-permute-done), channel_id=1, source_target_pairs={{0,4},{4,8},{8,12},{12,14},{14,10},{10,6},{6,2},{2,0},{1,5},{5,9},... | collective-permute-start | bytes 393224 | tf_op jit(solution)/shard_map/ppermute | solution.py:46
  10.0 0.2 collective-permute-start.1
  10.2 0.1 broadcast_in_dim.217
  10.3 0.1 broadcast_in_dim.218
  10.4 0.1 broadcast_in_dim.221
  10.5 0.1 broadcast_in_dim.222
  10.6 0.1 broadcast_in_dim.225
  10.6 0.1 broadcast_in_dim.226
  10.8 0.1 broadcast_in_dim.230
  10.9 0.1 broadcast_in_dim.233
  11.0 0.1 broadcast_in_dim.234
  11.1 0.1 broadcast_in_dim.237
  11.1 0.1 broadcast_in_dim.238
  11.3 0.1 broadcast_in_dim.242
  11.4 0.1 broadcast_in_dim.213
  11.5 0.1 broadcast_in_dim.214
  11.6 0.3 collective-permute-start.9
  11.9 1.0 %maximum_select_fusion.7 = bf16[2,64,1024]{2,1,0:T(8,128)(2,1)S(1)} fusion(bf16[1,64,1024]{2,1,0:T(8,128)(2,1)S(1)} %bitcast.91, bf16[1,64,1024]{2,1,0:T(8,128)(2,1)} %bitcast.87, pred[]{:T(512)S(6)} %eq.83), kind=kLoop, calls=%fused_computation.53 | loop fusion | flops 393216 | bytes 524289 | tf_op jit(solution)/shard_map/jit(_where)/select_n | solution.py:60
  13.0 1.1 %collective-permute-done.2 = bf16[64,1024]{1,0:T(8,128)(2,1)S(1)} collective-permute-done((bf16[64,1024]{1,0:T(8,128)(2,1)S(1)}, bf16[64,1024]{1,0:T(8,128)(2,1)S(1)}, u32[]{:S(2)}, u32[]{:S(2)}) %collective-permute-start.2) | collective-permute-done | bytes 131104 | tf_op jit(solution)/shard_map/ppermute | solution.py:46
  14.1 1.8 %collective-permute-start.4 = (bf16[64,1024]{1,0:T(8,128)(2,1)S(1)}, bf16[64,1024]{1,0:T(8,128)(2,1)S(1)}, u32[]{:S(2)}, u32[]{:S(2)}) collective-permute-start(bf16[64,1024]{1,0:T(8,128)(2,1)S(1)} %collective-permute-done.2), channel_id=1, source_target_pairs={{0,4},{4,8},{8,12},{12,14},{14,10},{10,6},{6,2},{2,0},{1,5},{5,9},... | collective-permute-start | bytes 393224 | tf_op jit(solution)/shard_map/ppermute | solution.py:46
  16.0 1.3 %collective-permute-done.9 = bf16[64,1024]{1,0:T(8,128)(2,1)S(1)} collective-permute-done((bf16[64,1024]{1,0:T(8,128)(2,1)S(1)}, bf16[64,1024]{1,0:T(8,128)(2,1)S(1)}, u32[]{:S(2)}, u32[]{:S(2)}) %collective-permute-start.9) | collective-permute-done | bytes 131104 | tf_op jit(solution)/shard_map/ppermute | solution.py:50
  17.3 0.3 collective-permute-start.10
  17.6 1.7 %collective-permute-done.4 = bf16[64,1024]{1,0:T(8,128)(2,1)S(1)} collective-permute-done((bf16[64,1024]{1,0:T(8,128)(2,1)S(1)}, bf16[64,1024]{1,0:T(8,128)(2,1)S(1)}, u32[]{:S(2)}, u32[]{:S(2)}) %collective-permute-start.4) | collective-permute-done | bytes 131104 | tf_op jit(solution)/shard_map/ppermute | solution.py:46
  19.3 1.6 %collective-permute-start.6 = (bf16[64,1024]{1,0:T(8,128)(2,1)S(1)}, bf16[64,1024]{1,0:T(8,128)(2,1)S(1)}, u32[]{:S(2)}, u32[]{:S(2)}) collective-permute-start(bf16[64,1024]{1,0:T(8,128)(2,1)S(1)} %collective-permute-done.4), channel_id=1, source_target_pairs={{0,4},{4,8},{8,12},{12,14},{14,10},{10,6},{6,2},{2,0},{1,5},{5,9},... | collective-permute-start | bytes 393224 | tf_op jit(solution)/shard_map/ppermute | solution.py:46
  21.0 1.2 %collective-permute-done.10 = bf16[64,1024]{1,0:T(8,128)(2,1)S(1)} collective-permute-done((bf16[64,1024]{1,0:T(8,128)(2,1)S(1)}, bf16[64,1024]{1,0:T(8,128)(2,1)S(1)}, u32[]{:S(2)}, u32[]{:S(2)}) %collective-permute-start.10) | collective-permute-done | bytes 131104 | tf_op jit(solution)/shard_map/ppermute | solution.py:50
  22.3 2.0 %collective-permute-done.6 = bf16[64,1024]{1,0:T(8,128)(2,1)S(1)} collective-permute-done((bf16[64,1024]{1,0:T(8,128)(2,1)S(1)}, bf16[64,1024]{1,0:T(8,128)(2,1)S(1)}, u32[]{:S(2)}, u32[]{:S(2)}) %collective-permute-start.6) | collective-permute-done | bytes 131104 | tf_op jit(solution)/shard_map/ppermute | solution.py:46
  24.4 1.3 %collective-permute-done.7 = bf16[64,1024]{1,0:T(8,128)(2,1)S(1)} collective-permute-done((bf16[64,1024]{1,0:T(8,128)(2,1)S(1)}, bf16[64,1024]{1,0:T(8,128)(2,1)S(1)}, u32[]{:S(2)}, u32[]{:S(2)}) %collective-permute-start.7) | collective-permute-done | bytes 131104 | tf_op jit(solution)/shard_map/ppermute | solution.py:53
  25.7 0.9 %select_select_fusion = bf16[8,2,64,1024]{3,2,1,0:T(8,128)(2,1)S(1)} fusion(pred[8]{0:T(512)(128)(4,1)S(1)} %get-tuple-element.23, pred[8]{0:T(512)(128)(4,1)S(1)} %get-tuple-element.18, pred[8]{0:T(512)(128)(4,1)S(1)} %get-tuple-element.19, pred[8]{0:T(512)(128)(4,1)S(1)} %get-tuple-element.20, pred[8]{0:T(512)(128)(4,1)S(1)} %get-tuple-element.21, ...), kind=kLoop, calls=%fused_computation.21 | loop fusion | flops 8388608 | bytes 4194368 | tf_op jit(solution)/shard_map/jit(_where)/select_n | solution.py:61
  26.6 0.6 copy-done.1
  27.3 1.3 %convolution_convert_fusion.1 = bf16[1024,512]{1,0:T(8,128)(2,1)S(1)} fusion(bf16[1024,1024]{1,0:T(8,128)(2,1)S(1)} %bitcast.84, bf16[2,1024,512]{2,1,0:T(8,128)(2,1)S(1)} %copy-done.1), kind=kOutput, calls=%fused_computation.25 | convolution fusion | flops 1074266112 | bytes 4194304 | tf_op jit(solution)/shard_map/sp,sr->pr/dot_general | solution.py:77
  28.6 1.3 %convolution_convert_fusion = bf16[1024,512]{1,0:T(8,128)(2,1)S(1)} fusion(bf16[1024,1024]{1,0:T(8,128)(2,1)S(1)} %bitcast.85, bf16[2,1024,512]{2,1,0:T(8,128)(2,1)S(1)} %copy-done.1), kind=kOutput, calls=%fused_computation.24 | convolution fusion | flops 1074266112 | bytes 4194304 | tf_op jit(solution)/shard_map/sp,sr->pr/dot_general | solution.py:77
  29.9 0.2 collective-permute-start.15
  30.1 0.4 collective-permute-start.16
  30.5 1.8 %fusion.16 = bf16[1024,1024]{1,0:T(8,128)(2,1)S(1)} fusion(pred[1024]{0:T(1024)(128)(4,1)S(1)} %broadcast_in_dim.242, pred[1024]{0:T(1024)(128)(4,1)S(1)} %broadcast_in_dim.238, pred[1024]{0:T(1024)(128)(4,1)S(1)} %broadcast_in_dim.234, pred[1024]{0:T(1024)(128)(4,1)S(1)} %broadcast_in_dim.230, pred[1024]{0:T(1024)(128)(4,1)S(1)} %broadcast_in_dim.226, ...), kind=kLoop, calls=%fused_computation.18 | loop fusion | flops 8388608 | bytes 4202496 | tf_op jit(solution)/shard_map/jit(_where)/select_n | solution.py:61
  32.3 1.3 %fusion.22 = bf16[2,1024,256]{1,2,0:T(8,128)(2,1)S(1)} fusion(bf16[1024,1024]{1,0:T(8,128)(2,1)S(1)} %fusion.16, s32[2,256]{1,0:T(2,128)S(1)} %bitcast_add_fusion), kind=kOutput, calls=%fused_computation.26 | convolution fusion | flops 1074790400 | bytes 3147776 | tf_op jit(solution)/shard_map/rc,gcj->grj/dot_general | solution.py:89
  33.6 0.7 %fusion = f32[2,1024,256]{2,1,0:T(8,128)S(1)} fusion(bf16[1,1024,512]{2,1,0:T(8,128)(2,1)S(1)} %bitcast.104, bf16[1,1024,512]{2,1,0:T(8,128)(2,1)S(1)} %bitcast.106, pred[]{:T(512)S(6)} %eq.83, bf16[2,1024,256]{1,2,0:T(8,128)(2,1)S(1)} %fusion.22), kind=kOutput, calls=%fused_computation.1 | convolution fusion | flops 538181632 | bytes 5242881 | tf_op jit(solution)/shard_map/gpr,grj->gpj/dot_general | solution.py:98
  34.4 0.8 %add_convert_fusion = bf16[2,1024,256]{2,1,0:T(8,128)(2,1)S(1)} fusion(f32[2,1024,256]{2,1,0:T(8,128)S(1)} %fusion, bf16[1,1024,512]{2,1,0:T(8,128)(2,1)S(1)} %bitcast.105, bf16[1,1024,512]{2,1,0:T(8,128)(2,1)S(1)} %bitcast.103, pred[]{:T(512)S(6)} %eq.83, bf16[2,1024,256]{1,2,0:T(8,128)(2,1)S(1)} %fusion.22), kind=kOutput, calls=%fused_computation.19 | convolution fusion | flops 539230208 | bytes 6291457 | tf_op jit(solution)/shard_map/gpr,grj->gpj/dot_general | solution.py:99
  35.2 0.6 gather_fusion
  35.9 0.8 %convolution_bitcast_fusion = f32[1024,512]{0,1:T(8,128)S(1)} fusion(bf16[2,1024,256]{2,1,0:T(8,128)(2,1)S(1)} %bitcast.82, bf16[2,256,512]{2,1,0:T(8,128)(2,1)S(1)} %copy-done), kind=kOutput, calls=%fused_computation.22 | convolution fusion | flops 536870912 | bytes 3670016 | tf_op jit(solution)/shard_map/gpj,gjq->pq/dot_general | solution.py:130
  36.7 1.7 %collective-permute-start.17 = (f32[128,256]{0,1:T(8,128)S(1)}, f32[128,256]{0,1:T(8,128)S(1)}, u32[]{:S(2)}, u32[]{:S(2)}) collective-permute-start(f32[128,256]{0,1:T(8,128)S(1)} %get-tuple-element.15), channel_id=1, source_target_pairs={{0,4},{4,8},{8,12},{12,14},{14,10},{10,6},{6,2},{2,0},{1,5},{5,9},... | collective-permute-start | bytes 393224 | tf_op jit(solution)/shard_map/ppermute | solution.py:137
  38.4 0.4 collective-permute-start.21
  38.8 3.5 %collective-permute-done.17 = f32[128,256]{0,1:T(8,128)S(1)} collective-permute-done((f32[128,256]{0,1:T(8,128)S(1)}, f32[128,256]{0,1:T(8,128)S(1)}, u32[]{:S(2)}, u32[]{:S(2)}) %collective-permute-start.17) | collective-permute-done | bytes 131104 | tf_op jit(solution)/shard_map/ppermute | solution.py:137
  42.3 1.4 %collective-permute-done.21 = f32[128,256]{0,1:T(8,128)S(1)} collective-permute-done((f32[128,256]{0,1:T(8,128)S(1)}, f32[128,256]{0,1:T(8,128)S(1)}, u32[]{:S(2)}, u32[]{:S(2)}) %collective-permute-start.21) | collective-permute-done | bytes 131104 | tf_op jit(solution)/shard_map/ppermute | solution.py:138
  43.7 0.4 collective-permute-start.22
  44.2 1.7 %collective-permute-start.18 = (f32[128,512]{0,1:T(8,128)S(1)}, f32[128,512]{0,1:T(8,128)S(1)}, u32[]{:S(2)}, u32[]{:S(2)}) collective-permute-start(f32[128,512]{0,1:T(8,128)S(1)} %pad_maximum_fusion), channel_id=1, source_target_pairs={{0,4},{4,8},{8,12},{12,14},{14,10},{10,6},{6,2},{2,0},{1,5},{5,9},... | collective-permute-start | bytes 786440 | tf_op jit(solution)/shard_map/ppermute | solution.py:144
  45.9 5.1 %collective-permute-done.22 = f32[128,512]{0,1:T(8,128)S(1)} collective-permute-done((f32[128,512]{0,1:T(8,128)S(1)}, f32[128,512]{0,1:T(8,128)S(1)}, u32[]{:S(2)}, u32[]{:S(2)}) %collective-permute-start.22) | collective-permute-done | bytes 262176 | tf_op jit(solution)/shard_map/ppermute | solution.py:145
  51.0 0.2 collective-permute-done.18
  51.3 0.1 slice_add_fusion.3
  51.3 1.6 %collective-permute-start.19 = (f32[128,512]{0,1:T(8,128)S(1)}, f32[128,512]{0,1:T(8,128)S(1)}, u32[]{:S(2)}, u32[]{:S(2)}) collective-permute-start(f32[128,512]{0,1:T(8,128)S(1)} %get-tuple-element.9), channel_id=1, source_target_pairs={{0,4},{4,8},{8,12},{12,14},{14,10},{10,6},{6,2},{2,0},{1,5},{5,9},... | collective-permute-start | bytes 786440 | tf_op jit(solution)/shard_map/ppermute | solution.py:144
  53.0 0.5 collective-permute-start.23
  53.4 4.3 %collective-permute-done.19 = f32[128,512]{0,1:T(8,128)S(1)} collective-permute-done((f32[128,512]{0,1:T(8,128)S(1)}, f32[128,512]{0,1:T(8,128)S(1)}, u32[]{:S(2)}, u32[]{:S(2)}) %collective-permute-start.19) | collective-permute-done | bytes 262176 | tf_op jit(solution)/shard_map/ppermute | solution.py:144
  57.8 1.6 %collective-permute-done.23 = f32[128,512]{0,1:T(8,128)S(1)} collective-permute-done((f32[128,512]{0,1:T(8,128)S(1)}, f32[128,512]{0,1:T(8,128)S(1)}, u32[]{:S(2)}, u32[]{:S(2)}) %collective-permute-start.23) | collective-permute-done | bytes 262176 | tf_op jit(solution)/shard_map/ppermute | solution.py:145
  59.3 0.1 slice_add_fusion.2
  59.4 1.6 %collective-permute-start.20 = (f32[128,512]{0,1:T(8,128)S(1)}, f32[128,512]{0,1:T(8,128)S(1)}, u32[]{:S(2)}, u32[]{:S(2)}) collective-permute-start(f32[128,512]{0,1:T(8,128)S(1)} %get-tuple-element.7), channel_id=1, source_target_pairs={{0,4},{4,8},{8,12},{12,14},{14,10},{10,6},{6,2},{2,0},{1,5},{5,9},... | collective-permute-start | bytes 786440 | tf_op jit(solution)/shard_map/ppermute | solution.py:148
  61.1 0.4 collective-permute-start.24
  61.5 4.3 %collective-permute-done.20 = f32[128,512]{0,1:T(8,128)S(1)} collective-permute-done((f32[128,512]{0,1:T(8,128)S(1)}, f32[128,512]{0,1:T(8,128)S(1)}, u32[]{:S(2)}, u32[]{:S(2)}) %collective-permute-start.20) | collective-permute-done | bytes 262176 | tf_op jit(solution)/shard_map/ppermute | solution.py:148
  65.8 1.6 %collective-permute-done.24 = f32[128,512]{0,1:T(8,128)S(1)} collective-permute-done((f32[128,512]{0,1:T(8,128)S(1)}, f32[128,512]{0,1:T(8,128)S(1)}, u32[]{:S(2)}, u32[]{:S(2)}) %collective-permute-start.24) | collective-permute-done | bytes 262176 | tf_op jit(solution)/shard_map/ppermute | solution.py:149
  67.5 0.8 %copy.22 = f32[128,512]{1,0:T(8,128)} copy(f32[128,512]{0,1:T(8,128)S(1)} %fusion.38) | data formatting | bytes 524288 | tf_op jit(solution)/shard_map/add | solution.py:147
  (43 shorter events, 0.8 us)
Async XLA Ops:
  0.0 35.9 %copy-start = (bf16[2,256,512]{2,1,0:T(8,128)(2,1)S(1)}, bf16[2,256,512]{2,1,0:T(8,128)(2,1)}, u32[]{:S(2)}) copy-start(bf16[2,256,512]{2,1,0:T(8,128)(2,1)} %param.10) | copy-start | bytes 1572868
  0.0 7.9 %collective-permute-start = (bf16[64,1024]{1,0:T(8,128)(2,1)}, bf16[64,1024]{1,0:T(8,128)(2,1)S(1)}, u32[]{:S(2)}, u32[]{:S(2)}) collective-permute-start(bf16[64,1024]{1,0:T(8,128)(2,1)} %param.8), channel_id=1, source_target_pairs={{0,4},{4,8},{8,12},{12,14},{14,10},{10,6},{6,2},{2,0},{1,5},{5,9},... | collective-permute-start | bytes 393224 | tf_op jit(solution)/shard_map/ppermute | solution.py:46
  3.1 8.5 %collective-permute-start.8 = (bf16[64,1024]{1,0:T(8,128)(2,1)}, bf16[64,1024]{1,0:T(8,128)(2,1)S(1)}, u32[]{:S(2)}, u32[]{:S(2)}) collective-permute-start(bf16[64,1024]{1,0:T(8,128)(2,1)} %param.8), channel_id=1, source_target_pairs={{0,2},{4,0},{8,4},{12,8},{14,12},{10,14},{6,10},{2,6},{1,3},{5,1},... | collective-permute-start | bytes 393224 | tf_op jit(solution)/shard_map/ppermute | solution.py:50
  3.1 8.9 %collective-permute-start.14 = (bf16[64,1024]{1,0:T(8,128)(2,1)}, bf16[64,1024]{1,0:T(8,128)(2,1)S(1)}, u32[]{:S(2)}, u32[]{:S(2)}) collective-permute-start(bf16[64,1024]{1,0:T(8,128)(2,1)} %param.8), channel_id=1, source_target_pairs={{0,1},{1,0},{2,3},{3,2},{4,5},{5,4},{6,7},{7,6},{8,9},{9,8},{10,11... | collective-permute-start | bytes 393224 | tf_op jit(solution)/shard_map/ppermute | solution.py:53
  7.9 6.2 %collective-permute-start.2 = (bf16[64,1024]{1,0:T(8,128)(2,1)S(1)}, bf16[64,1024]{1,0:T(8,128)(2,1)S(1)}, u32[]{:S(2)}, u32[]{:S(2)}) collective-permute-start(bf16[64,1024]{1,0:T(8,128)(2,1)S(1)} %collective-permute-done), channel_id=1, source_target_pairs={{0,4},{4,8},{8,12},{12,14},{14,10},{10,6},{6,2},{2,0},{1,5},{5,9},... | collective-permute-start | bytes 393224 | tf_op jit(solution)/shard_map/ppermute | solution.py:46
  10.0 5.9 %collective-permute-start.1 = (bf16[64,1024]{1,0:T(8,128)(2,1)S(1)}, bf16[64,1024]{1,0:T(8,128)(2,1)S(1)}, u32[]{:S(2)}, u32[]{:S(2)}) collective-permute-start(bf16[64,1024]{1,0:T(8,128)(2,1)S(1)} %collective-permute-done), channel_id=1, source_target_pairs={{0,1},{1,0},{2,3},{3,2},{4,5},{5,4},{6,7},{7,6},{8,9},{9,8},{10,11... | collective-permute-start | bytes 393224 | tf_op jit(solution)/shard_map/ppermute | solution.py:53
  11.6 5.7 %collective-permute-start.9 = (bf16[64,1024]{1,0:T(8,128)(2,1)S(1)}, bf16[64,1024]{1,0:T(8,128)(2,1)S(1)}, u32[]{:S(2)}, u32[]{:S(2)}) collective-permute-start(bf16[64,1024]{1,0:T(8,128)(2,1)S(1)} %collective-permute-done.8), channel_id=1, source_target_pairs={{0,2},{4,0},{8,4},{12,8},{14,12},{10,14},{6,10},{2,6},{1,3},{5,1},... | collective-permute-start | bytes 393224 | tf_op jit(solution)/shard_map/ppermute | solution.py:50
  11.9 5.7 %collective-permute-start.13 = (bf16[64,1024]{1,0:T(8,128)(2,1)S(1)}, bf16[64,1024]{1,0:T(8,128)(2,1)S(1)}, u32[]{:S(2)}, u32[]{:S(2)}) collective-permute-start(bf16[64,1024]{1,0:T(8,128)(2,1)S(1)} %collective-permute-done.8), channel_id=1, source_target_pairs={{0,1},{1,0},{2,3},{3,2},{4,5},{5,4},{6,7},{7,6},{8,9},{9,8},{10,11... | collective-permute-start | bytes 393224 | tf_op jit(solution)/shard_map/ppermute | solution.py:53
  14.1 5.2 %collective-permute-start.4 = (bf16[64,1024]{1,0:T(8,128)(2,1)S(1)}, bf16[64,1024]{1,0:T(8,128)(2,1)S(1)}, u32[]{:S(2)}, u32[]{:S(2)}) collective-permute-start(bf16[64,1024]{1,0:T(8,128)(2,1)S(1)} %collective-permute-done.2), channel_id=1, source_target_pairs={{0,4},{4,8},{8,12},{12,14},{14,10},{10,6},{6,2},{2,0},{1,5},{5,9},... | collective-permute-start | bytes 393224 | tf_op jit(solution)/shard_map/ppermute | solution.py:46
  15.9 5.1 %collective-permute-start.3 = (bf16[64,1024]{1,0:T(8,128)(2,1)S(1)}, bf16[64,1024]{1,0:T(8,128)(2,1)S(1)}, u32[]{:S(2)}, u32[]{:S(2)}) collective-permute-start(bf16[64,1024]{1,0:T(8,128)(2,1)S(1)} %collective-permute-done.2), channel_id=1, source_target_pairs={{0,1},{1,0},{2,3},{3,2},{4,5},{5,4},{6,7},{7,6},{8,9},{9,8},{10,11... | collective-permute-start | bytes 393224 | tf_op jit(solution)/shard_map/ppermute | solution.py:53
  17.3 5.0 %collective-permute-start.10 = (bf16[64,1024]{1,0:T(8,128)(2,1)S(1)}, bf16[64,1024]{1,0:T(8,128)(2,1)S(1)}, u32[]{:S(2)}, u32[]{:S(2)}) collective-permute-start(bf16[64,1024]{1,0:T(8,128)(2,1)S(1)} %collective-permute-done.9), channel_id=1, source_target_pairs={{0,2},{4,0},{8,4},{12,8},{14,12},{10,14},{6,10},{2,6},{1,3},{5,1},... | collective-permute-start | bytes 393224 | tf_op jit(solution)/shard_map/ppermute | solution.py:50
  17.6 4.7 %collective-permute-start.12 = (bf16[64,1024]{1,0:T(8,128)(2,1)S(1)}, bf16[64,1024]{1,0:T(8,128)(2,1)S(1)}, u32[]{:S(2)}, u32[]{:S(2)}) collective-permute-start(bf16[64,1024]{1,0:T(8,128)(2,1)S(1)} %collective-permute-done.9), channel_id=1, source_target_pairs={{0,1},{1,0},{2,3},{3,2},{4,5},{5,4},{6,7},{7,6},{8,9},{9,8},{10,11... | collective-permute-start | bytes 393224 | tf_op jit(solution)/shard_map/ppermute | solution.py:53
  19.3 5.0 %collective-permute-start.6 = (bf16[64,1024]{1,0:T(8,128)(2,1)S(1)}, bf16[64,1024]{1,0:T(8,128)(2,1)S(1)}, u32[]{:S(2)}, u32[]{:S(2)}) collective-permute-start(bf16[64,1024]{1,0:T(8,128)(2,1)S(1)} %collective-permute-done.4), channel_id=1, source_target_pairs={{0,4},{4,8},{8,12},{12,14},{14,10},{10,6},{6,2},{2,0},{1,5},{5,9},... | collective-permute-start | bytes 393224 | tf_op jit(solution)/shard_map/ppermute | solution.py:46
  21.0 3.3 %collective-permute-start.5 = (bf16[64,1024]{1,0:T(8,128)(2,1)S(1)}, bf16[64,1024]{1,0:T(8,128)(2,1)S(1)}, u32[]{:S(2)}, u32[]{:S(2)}) collective-permute-start(bf16[64,1024]{1,0:T(8,128)(2,1)S(1)} %collective-permute-done.4), channel_id=1, source_target_pairs={{0,1},{1,0},{2,3},{3,2},{4,5},{5,4},{6,7},{7,6},{8,9},{9,8},{10,11... | collective-permute-start | bytes 393224 | tf_op jit(solution)/shard_map/ppermute | solution.py:53
  22.2 2.1 %collective-permute-start.11 = (bf16[64,1024]{1,0:T(8,128)(2,1)S(1)}, bf16[64,1024]{1,0:T(8,128)(2,1)S(1)}, u32[]{:S(2)}, u32[]{:S(2)}) collective-permute-start(bf16[64,1024]{1,0:T(8,128)(2,1)S(1)} %collective-permute-done.10), channel_id=1, source_target_pairs={{0,1},{1,0},{2,3},{3,2},{4,5},{5,4},{6,7},{7,6},{8,9},{9,8},{10,11... | collective-permute-start | bytes 393224 | tf_op jit(solution)/shard_map/ppermute | solution.py:53
  24.3 1.3 %collective-permute-start.7 = (bf16[64,1024]{1,0:T(8,128)(2,1)S(1)}, bf16[64,1024]{1,0:T(8,128)(2,1)S(1)}, u32[]{:S(2)}, u32[]{:S(2)}) collective-permute-start(bf16[64,1024]{1,0:T(8,128)(2,1)S(1)} %collective-permute-done.6), channel_id=1, source_target_pairs={{0,1},{1,0},{2,3},{3,2},{4,5},{5,4},{6,7},{7,6},{8,9},{9,8},{10,11... | collective-permute-start | bytes 393224 | tf_op jit(solution)/shard_map/ppermute | solution.py:53
  25.7 1.6 %copy-start.1 = (bf16[2,1024,512]{2,1,0:T(8,128)(2,1)S(1)}, bf16[2,1024,512]{2,1,0:T(8,128)(2,1)}, u32[]{:S(2)}) copy-start(bf16[2,1024,512]{2,1,0:T(8,128)(2,1)} %param.7) | copy-start | bytes 6291460
  29.9 4.5 %collective-permute-start.15 = (bf16[1024,512]{1,0:T(8,128)(2,1)S(1)}, bf16[1024,512]{1,0:T(8,128)(2,1)S(1)}, u32[]{:S(2)}, u32[]{:S(2)}) collective-permute-start(bf16[1024,512]{1,0:T(8,128)(2,1)S(1)} %convolution_convert_fusion.1), channel_id=1, source_target_pairs={{0,1},{1,0},{2,3},{3,2},{4,5},{5,4},{6,7},{7,6},{8,9},{9,8},{10,11... | collective-permute-start | bytes 3145736 | tf_op jit(solution)/shard_map/ppermute | solution.py:80
  30.1 4.3 %collective-permute-start.16 = (bf16[1024,512]{1,0:T(8,128)(2,1)S(1)}, bf16[1024,512]{1,0:T(8,128)(2,1)S(1)}, u32[]{:S(2)}, u32[]{:S(2)}) collective-permute-start(bf16[1024,512]{1,0:T(8,128)(2,1)S(1)} %convolution_convert_fusion), channel_id=1, source_target_pairs={{0,1},{1,0},{2,3},{3,2},{4,5},{5,4},{6,7},{7,6},{8,9},{9,8},{10,11... | collective-permute-start | bytes 3145736 | tf_op jit(solution)/shard_map/ppermute | solution.py:80
  36.7 5.6 %collective-permute-start.17 = (f32[128,256]{0,1:T(8,128)S(1)}, f32[128,256]{0,1:T(8,128)S(1)}, u32[]{:S(2)}, u32[]{:S(2)}) collective-permute-start(f32[128,256]{0,1:T(8,128)S(1)} %get-tuple-element.15), channel_id=1, source_target_pairs={{0,4},{4,8},{8,12},{12,14},{14,10},{10,6},{6,2},{2,0},{1,5},{5,9},... | collective-permute-start | bytes 393224 | tf_op jit(solution)/shard_map/ppermute | solution.py:137
  38.4 5.3 %collective-permute-start.21 = (f32[128,256]{0,1:T(8,128)S(1)}, f32[128,256]{0,1:T(8,128)S(1)}, u32[]{:S(2)}, u32[]{:S(2)}) collective-permute-start(f32[128,256]{0,1:T(8,128)S(1)} %get-tuple-element.16), channel_id=1, source_target_pairs={{0,2},{4,0},{8,4},{12,8},{14,12},{10,14},{6,10},{2,6},{1,3},{5,1},... | collective-permute-start | bytes 393224 | tf_op jit(solution)/shard_map/ppermute | solution.py:138
  43.7 7.3 %collective-permute-start.22 = (f32[128,512]{0,1:T(8,128)S(1)}, f32[128,512]{0,1:T(8,128)S(1)}, u32[]{:S(2)}, u32[]{:S(2)}) collective-permute-start(f32[128,512]{0,1:T(8,128)S(1)} %pad_maximum_fusion.1), channel_id=1, source_target_pairs={{0,2},{4,0},{8,4},{12,8},{14,12},{10,14},{6,10},{2,6},{1,3},{5,1},... | collective-permute-start | bytes 786440 | tf_op jit(solution)/shard_map/ppermute | solution.py:145
  44.2 7.1 %collective-permute-start.18 = (f32[128,512]{0,1:T(8,128)S(1)}, f32[128,512]{0,1:T(8,128)S(1)}, u32[]{:S(2)}, u32[]{:S(2)}) collective-permute-start(f32[128,512]{0,1:T(8,128)S(1)} %pad_maximum_fusion), channel_id=1, source_target_pairs={{0,4},{4,8},{8,12},{12,14},{14,10},{10,6},{6,2},{2,0},{1,5},{5,9},... | collective-permute-start | bytes 786440 | tf_op jit(solution)/shard_map/ppermute | solution.py:144
  51.3 6.4 %collective-permute-start.19 = (f32[128,512]{0,1:T(8,128)S(1)}, f32[128,512]{0,1:T(8,128)S(1)}, u32[]{:S(2)}, u32[]{:S(2)}) collective-permute-start(f32[128,512]{0,1:T(8,128)S(1)} %get-tuple-element.9), channel_id=1, source_target_pairs={{0,4},{4,8},{8,12},{12,14},{14,10},{10,6},{6,2},{2,0},{1,5},{5,9},... | collective-permute-start | bytes 786440 | tf_op jit(solution)/shard_map/ppermute | solution.py:144
  53.0 6.4 %collective-permute-start.23 = (f32[128,512]{0,1:T(8,128)S(1)}, f32[128,512]{0,1:T(8,128)S(1)}, u32[]{:S(2)}, u32[]{:S(2)}) collective-permute-start(f32[128,512]{0,1:T(8,128)S(1)} %get-tuple-element.10), channel_id=1, source_target_pairs={{0,2},{4,0},{8,4},{12,8},{14,12},{10,14},{6,10},{2,6},{1,3},{5,1},... | collective-permute-start | bytes 786440 | tf_op jit(solution)/shard_map/ppermute | solution.py:145
  59.4 6.4 %collective-permute-start.20 = (f32[128,512]{0,1:T(8,128)S(1)}, f32[128,512]{0,1:T(8,128)S(1)}, u32[]{:S(2)}, u32[]{:S(2)}) collective-permute-start(f32[128,512]{0,1:T(8,128)S(1)} %get-tuple-element.7), channel_id=1, source_target_pairs={{0,4},{4,8},{8,12},{12,14},{14,10},{10,6},{6,2},{2,0},{1,5},{5,9},... | collective-permute-start | bytes 786440 | tf_op jit(solution)/shard_map/ppermute | solution.py:148
  61.1 6.4 %collective-permute-start.24 = (f32[128,512]{0,1:T(8,128)S(1)}, f32[128,512]{0,1:T(8,128)S(1)}, u32[]{:S(2)}, u32[]{:S(2)}) collective-permute-start(f32[128,512]{0,1:T(8,128)S(1)} %get-tuple-element.8), channel_id=1, source_target_pairs={{0,2},{4,0},{8,4},{12,8},{14,12},{10,14},{6,10},{2,6},{1,3},{5,1},... | collective-permute-start | bytes 786440 | tf_op jit(solution)/shard_map/ppermute | solution.py:149

commit v9 on v8

--- a/solution.py
+++ b/solution.py
@@ -51,9 +51,10 @@
         lb.append(cur)
     got = [x] + lb + rb[::-1]
     theirs = lax.ppermute(tuple(got), "orb", [(0, 1), (1, 0)])
-    pos_of = jnp.asarray(np.argsort(np.array(ring)).astype(np.int32))
-    pos = pos_of[lax.axis_index("vec")]
-    offset = ((pos_of - pos) % n)[:, None, None, None]
+    pos_of = np.argsort(np.array(ring))
+    table = jnp.asarray(((pos_of[None, :] - pos_of[:, None]) % n).astype(np.int32))
+    hits = (jnp.arange(n, dtype=jnp.int32) == lax.axis_index("vec"))[:, None]
+    offset = jnp.sum(jnp.where(hits, table, 0), axis=0)[:, None, None, None]
     first = lax.axis_index("orb") == 0
     out = jnp.zeros((n, 2) + x.shape, x.dtype)
     for d in range(n):
@@ -127,9 +128,18 @@
             axis=1,
         ).reshape(-1)
         ordered = jnp.take(by_group, order, axis=1, mode="clip").reshape(active_rotated.shape)
-        part = jnp.einsum(
-            "gpj,gjq->pq", ordered, factors, preferred_element_type=jnp.float32
-        ).reshape(n, per, -1)
+        first_block = jnp.einsum(
+            "gpj,gjq->pq", ordered[:, :per], factors, preferred_element_type=jnp.float32
+        )
+        later = ordered[:, per:]
+        part = jnp.concatenate(
+            [
+                first_block[None],
+                jnp.einsum(
+                    "gpj,gjq->pq", later, factors, preferred_element_type=jnp.float32
+                ).reshape(n - 1, per, -1),
+            ]
+        )
         right = [(ring[i], ring[(i + 1) % n]) for i in range(n)]
         left = [(ring[i], ring[(i - 1) % n]) for i in range(n)]
         if even:

time: 68.6 us -> 66 us (0.962)
  other arithmetic: 7.91 us -> 6.55 us
  local copies, waits for them, and re-layouts: 4.84 us -> 3.6 us
    ppermute x3, waiting for transfers between devices: 2.56 us -> 4.16 us  [ring_all_gather(): cur = lax.ppermute(cur, 'vec', left)]
    eq x2 -> x1, other arithmetic: 1.32 us -> 0.01 us  [ring_all_gather(): out = jnp.where(offset == d, pair[None], out)]
    ppermute x4, waiting for transfers between devices: 4.9 us -> 3.63 us  [ring_all_gather(): cur = lax.ppermute(cur, 'vec', right)]
    dynamic_slice x1 -> x0, local copies, waits for them, and re-layouts: 1.24 us -> none  [ring_all_gather(): pos = pos_of[lax.axis_index('vec')]]
    ppermute x1, waiting for transfers between devices: 3.52 us -> 2.77 us  [per_device(): got_r = lax.ppermute(part[0][:, :cut], 'vec', right)]
  transfers between devices with their start and end apart: 25 -> 25, of which waited for: 14 -> 16; matrix products, arithmetic and copies ran while one was open for 17% -> 14% of each run, Pallas kernels for 0% -> 0%
where the time goes in v9:
time: 66 us; the launch traced here: 65.7 us
  waiting for transfers between devices  30.6 us (46%)
  starting transfers between devices  18.4 us (28%)
  other arithmetic  6.55 us (10%)
  matrix products  6.44 us (10%)
  local copies, waits for them, and re-layouts  3.6 us (5%)
    ppermute x4, starting transfers between devices, ring_all_gather(): cur = lax.ppermute(cur, 'vec', right)  8.53 us
    ppermute x2, waiting for transfers between devices, per_device(): acc_l = lax.ppermute(acc_l, 'vec', left) + part[reach + k - 1]  6.69 us
    ppermute x2, waiting for transfers between devices, per_device(): acc_r = lax.ppermute(acc_r, 'vec', right) + part[k]  4.59 us
    ppermute x1, waiting for transfers between devices, per_device(): lax.ppermute(acc_r, 'vec', right)  4.35 us
    ppermute x3, waiting for transfers between devices, ring_all_gather(): cur = lax.ppermute(cur, 'vec', left)  4.16 us
    ppermute x4, waiting for transfers between devices, ring_all_gather(): cur = lax.ppermute(cur, 'vec', right)  3.63 us
    ppermute x2, starting transfers between devices, per_device(): acc_r = lax.ppermute(acc_r, 'vec', right) + part[k]  3.42 us
    ppermute x1, waiting for transfers between devices, per_device(): got_r = lax.ppermute(part[0][:, :cut], 'vec', right)  2.77 us
  transfers between devices with their start and end apart: 25, of which 16 were waited for; matrix products, arithmetic and copies ran while one was open for 14% of the time, Pallas kernels for 0%

profile of v9, /device:TPU:0, one launch (start us, length us, event | category | flops | bytes accessed | tf_op | source)
XLA Modules:
  0.0 65.7 jit_solution(6521654338137222668)
XLA Ops:
  0.0 3.1 %collective-permute-start = (bf16[64,1024]{1,0:T(8,128)(2,1)}, bf16[64,1024]{1,0:T(8,128)(2,1)S(1)}, u32[]{:S(2)}, u32[]{:S(2)}) collective-permute-start(bf16[64,1024]{1,0:T(8,128)(2,1)} %param.8), channel_id=1, source_target_pairs={{0,4},{4,8},{8,12},{12,14},{14,10},{10,6},{6,2},{2,0},{1,5},{5,9},... | collective-permute-start | bytes 393224 | tf_op jit(solution)/shard_map/ppermute | solution.py:46
  3.1 0.8 %select_reduce_fusion.1 = (s32[8]{0:T(128)S(1)}, s32[8]{0:T(128)S(1)}) fusion(s32[8,8]{1,0:T(8,128)} %constant.34.clone, pred[8]{0:T(512)(128)(4,1)S(1)} %iota_compare_fusion.7, s32[8,8]{1,0:T(8,128)} %constant.33.clone), kind=kLoop, calls=%fused_computation.64 | loop fusion | flops 240 | bytes 584 | tf_op jit(solution)/shard_map/reduce_sum | solution.py:125
  3.9 0.7 %broadcast_multiply_fusion = s32[2,2]{1,0:T(2,128)S(1)} fusion(s32[2,2]{1,0:T(2,128)} %param.9), kind=kLoop, calls=%fused_computation.69 | loop fusion | flops 4 | bytes 32 | tf_op jit(solution)/shard_map/mul | solution.py:84
  4.6 0.8 %select_reduce_fusion = s32[8]{0:T(128)S(1)} fusion(s32[8]{0:T(128)} %param.11, s32[8]{0:T(128)S(1)} %get-tuple-element.5), kind=kLoop, calls=%fused_computation.62 | loop fusion | flops 184 | bytes 96 | tf_op jit(solution)/shard_map/reduce_sum | solution.py:126
  5.4 1.3 %collective-permute-done = bf16[64,1024]{1,0:T(8,128)(2,1)S(1)} collective-permute-done((bf16[64,1024]{1,0:T(8,128)(2,1)}, bf16[64,1024]{1,0:T(8,128)(2,1)S(1)}, u32[]{:S(2)}, u32[]{:S(2)}) %collective-permute-start) | collective-permute-done | bytes 131104 | tf_op jit(solution)/shard_map/ppermute | solution.py:46
  6.7 1.8 %collective-permute-start.2 = (bf16[64,1024]{1,0:T(8,128)(2,1)S(1)}, bf16[64,1024]{1,0:T(8,128)(2,1)S(1)}, u32[]{:S(2)}, u32[]{:S(2)}) collective-permute-start(bf16[64,1024]{1,0:T(8,128)(2,1)S(1)} %collective-permute-done), channel_id=1, source_target_pairs={{0,4},{4,8},{8,12},{12,14},{14,10},{10,6},{6,2},{2,0},{1,5},{5,9},... | collective-permute-start | bytes 393224 | tf_op jit(solution)/shard_map/ppermute | solution.py:46
  8.5 0.1 broadcast_in_dim.220
  8.6 0.1 broadcast_in_dim.221
  8.7 0.1 broadcast_in_dim.224
  8.7 0.1 broadcast_in_dim.225
  8.8 0.1 broadcast_in_dim.228
  8.9 0.1 broadcast_in_dim.229
  9.0 0.1 broadcast_in_dim.232
  9.1 0.1 broadcast_in_dim.233
  9.2 0.1 broadcast_in_dim.236
  9.2 0.1 broadcast_in_dim.237
  9.3 0.1 broadcast_in_dim.240
  9.4 0.1 broadcast_in_dim.241
  9.6 0.1 broadcast_in_dim.245
  9.7 0.1 broadcast_in_dim.248
  9.8 0.1 broadcast_in_dim.249
  9.8 0.2 collective-permute-start.9
  10.1 0.4 collective-permute-start.13
  10.4 1.0 %maximum_select_fusion.7 = bf16[2,64,1024]{2,1,0:T(8,128)(2,1)S(1)} fusion(bf16[1,64,1024]{2,1,0:T(8,128)(2,1)S(1)} %bitcast.95, bf16[1,64,1024]{2,1,0:T(8,128)(2,1)} %bitcast.91, pred[]{:T(512)S(6)} %eq.117), kind=kLoop, calls=%fused_computation.55 | loop fusion | flops 393216 | bytes 524289 | tf_op jit(solution)/shard_map/jit(_where)/select_n | solution.py:61
  11.5 0.2 collective-permute-done.2
  11.6 1.8 %collective-permute-start.4 = (bf16[64,1024]{1,0:T(8,128)(2,1)S(1)}, bf16[64,1024]{1,0:T(8,128)(2,1)S(1)}, u32[]{:S(2)}, u32[]{:S(2)}) collective-permute-start(bf16[64,1024]{1,0:T(8,128)(2,1)S(1)} %collective-permute-done.2), channel_id=1, source_target_pairs={{0,4},{4,8},{8,12},{12,14},{14,10},{10,6},{6,2},{2,0},{1,5},{5,9},... | collective-permute-start | bytes 393224 | tf_op jit(solution)/shard_map/ppermute | solution.py:46
  13.5 2.3 %collective-permute-done.9 = bf16[64,1024]{1,0:T(8,128)(2,1)S(1)} collective-permute-done((bf16[64,1024]{1,0:T(8,128)(2,1)S(1)}, bf16[64,1024]{1,0:T(8,128)(2,1)S(1)}, u32[]{:S(2)}, u32[]{:S(2)}) %collective-permute-start.9) | collective-permute-done | bytes 131104 | tf_op jit(solution)/shard_map/ppermute | solution.py:50
  15.8 0.3 collective-permute-start.10
  16.1 1.0 %collective-permute-done.4 = bf16[64,1024]{1,0:T(8,128)(2,1)S(1)} collective-permute-done((bf16[64,1024]{1,0:T(8,128)(2,1)S(1)}, bf16[64,1024]{1,0:T(8,128)(2,1)S(1)}, u32[]{:S(2)}, u32[]{:S(2)}) %collective-permute-start.4) | collective-permute-done | bytes 131104 | tf_op jit(solution)/shard_map/ppermute | solution.py:46
  17.1 1.8 %collective-permute-start.6 = (bf16[64,1024]{1,0:T(8,128)(2,1)S(1)}, bf16[64,1024]{1,0:T(8,128)(2,1)S(1)}, u32[]{:S(2)}, u32[]{:S(2)}) collective-permute-start(bf16[64,1024]{1,0:T(8,128)(2,1)S(1)} %collective-permute-done.4), channel_id=1, source_target_pairs={{0,4},{4,8},{8,12},{12,14},{14,10},{10,6},{6,2},{2,0},{1,5},{5,9},... | collective-permute-start | bytes 393224 | tf_op jit(solution)/shard_map/ppermute | solution.py:46
  18.9 1.9 %collective-permute-done.10 = bf16[64,1024]{1,0:T(8,128)(2,1)S(1)} collective-permute-done((bf16[64,1024]{1,0:T(8,128)(2,1)S(1)}, bf16[64,1024]{1,0:T(8,128)(2,1)S(1)}, u32[]{:S(2)}, u32[]{:S(2)}) %collective-permute-start.10) | collective-permute-done | bytes 131104 | tf_op jit(solution)/shard_map/ppermute | solution.py:50
  20.9 1.2 %collective-permute-done.6 = bf16[64,1024]{1,0:T(8,128)(2,1)S(1)} collective-permute-done((bf16[64,1024]{1,0:T(8,128)(2,1)S(1)}, bf16[64,1024]{1,0:T(8,128)(2,1)S(1)}, u32[]{:S(2)}, u32[]{:S(2)}) %collective-permute-start.6) | collective-permute-done | bytes 131104 | tf_op jit(solution)/shard_map/ppermute | solution.py:46
  22.2 1.2 %collective-permute-done.7 = bf16[64,1024]{1,0:T(8,128)(2,1)S(1)} collective-permute-done((bf16[64,1024]{1,0:T(8,128)(2,1)S(1)}, bf16[64,1024]{1,0:T(8,128)(2,1)S(1)}, u32[]{:S(2)}, u32[]{:S(2)}) %collective-permute-start.7) | collective-permute-done | bytes 131104 | tf_op jit(solution)/shard_map/ppermute | solution.py:53
  23.5 0.9 %select_select_fusion = bf16[8,2,64,1024]{3,2,1,0:T(8,128)(2,1)S(1)} fusion(pred[8]{0:T(512)(128)(4,1)S(1)} %get-tuple-element.18, pred[8]{0:T(512)(128)(4,1)S(1)} %get-tuple-element.19, pred[8]{0:T(512)(128)(4,1)S(1)} %get-tuple-element.20, pred[8]{0:T(512)(128)(4,1)S(1)} %get-tuple-element.21, pred[8]{0:T(512)(128)(4,1)S(1)} %get-tuple-element.22, ...), kind=kLoop, calls=%fused_computation.21 | loop fusion | flops 8388608 | bytes 4194368 | tf_op jit(solution)/shard_map/jit(_where)/select_n | solution.py:62
  24.4 0.6 copy-done.1
  25.0 1.3 %convolution_convert_fusion.1 = bf16[1024,512]{1,0:T(8,128)(2,1)S(1)} fusion(bf16[1024,1024]{1,0:T(8,128)(2,1)S(1)} %bitcast.88, bf16[2,1024,512]{2,1,0:T(8,128)(2,1)S(1)} %copy-done.1), kind=kOutput, calls=%fused_computation.25 | convolution fusion | flops 1074266112 | bytes 4194304 | tf_op jit(solution)/shard_map/sp,sr->pr/dot_general | solution.py:78
  26.3 1.3 %convolution_convert_fusion = bf16[1024,512]{1,0:T(8,128)(2,1)S(1)} fusion(bf16[1024,1024]{1,0:T(8,128)(2,1)S(1)} %bitcast.89, bf16[2,1024,512]{2,1,0:T(8,128)(2,1)S(1)} %copy-done.1), kind=kOutput, calls=%fused_computation.24 | convolution fusion | flops 1074266112 | bytes 4194304 | tf_op jit(solution)/shard_map/sp,sr->pr/dot_general | solution.py:78
  27.6 0.2 collective-permute-start.15
  27.8 0.4 collective-permute-start.16
  28.3 1.8 %fusion.16 = bf16[1024,1024]{1,0:T(8,128)(2,1)S(1)} fusion(pred[1024]{0:T(1024)(128)(4,1)S(1)} %broadcast_in_dim.249, pred[1024]{0:T(1024)(128)(4,1)S(1)} %broadcast_in_dim.245, pred[1024]{0:T(1024)(128)(4,1)S(1)} %broadcast_in_dim.241, pred[1024]{0:T(1024)(128)(4,1)S(1)} %broadcast_in_dim.237, pred[1024]{0:T(1024)(128)(4,1)S(1)} %broadcast_in_dim.233, ...), kind=kLoop, calls=%fused_computation.18 | loop fusion | flops 8388608 | bytes 4202496 | tf_op jit(solution)/shard_map/jit(_where)/select_n | solution.py:62
  30.1 1.3 %fusion.22 = bf16[2,1024,256]{1,2,0:T(8,128)(2,1)S(1)} fusion(bf16[1024,1024]{1,0:T(8,128)(2,1)S(1)} %fusion.16, s32[2,256]{1,0:T(2,128)S(1)} %bitcast_add_fusion), kind=kOutput, calls=%fused_computation.26 | convolution fusion | flops 1074790400 | bytes 3147776 | tf_op jit(solution)/shard_map/rc,gcj->grj/dot_general | solution.py:90
  31.4 0.7 %fusion = f32[2,1024,256]{2,1,0:T(8,128)S(1)} fusion(bf16[1,1024,512]{2,1,0:T(8,128)(2,1)S(1)} %bitcast.108, bf16[1,1024,512]{2,1,0:T(8,128)(2,1)S(1)} %bitcast.110, pred[]{:T(512)S(6)} %eq.117, bf16[2,1024,256]{1,2,0:T(8,128)(2,1)S(1)} %fusion.22), kind=kOutput, calls=%fused_computation.1 | convolution fusion | flops 538181632 | bytes 5242881 | tf_op jit(solution)/shard_map/gpr,grj->gpj/dot_general | solution.py:99
  32.1 0.8 %add_convert_fusion = bf16[2,1024,256]{2,1,0:T(8,128)(2,1)S(1)} fusion(f32[2,1024,256]{2,1,0:T(8,128)S(1)} %fusion, bf16[1,1024,512]{2,1,0:T(8,128)(2,1)S(1)} %bitcast.109, bf16[1,1024,512]{2,1,0:T(8,128)(2,1)S(1)} %bitcast.107, pred[]{:T(512)S(6)} %eq.117, bf16[2,1024,256]{1,2,0:T(8,128)(2,1)S(1)} %fusion.22), kind=kOutput, calls=%fused_computation.19 | convolution fusion | flops 539230208 | bytes 6291457 | tf_op jit(solution)/shard_map/gpr,grj->gpj/dot_general | solution.py:100
  32.9 0.6 gather_fusion
  33.5 0.1 copy.24
  33.6 0.3 convolution_bitcast_fusion.1
  34.0 1.9 %collective-permute-start.17 = (f32[128,256]{0,1:T(8,128)S(1)}, f32[128,256]{0,1:T(8,128)S(1)}, u32[]{:S(2)}, u32[]{:S(2)}) collective-permute-start(f32[128,256]{0,1:T(8,128)S(1)} %get-tuple-element.15), channel_id=1, source_target_pairs={{0,4},{4,8},{8,12},{12,14},{14,10},{10,6},{6,2},{2,0},{1,5},{5,9},... | collective-permute-start | bytes 393224 | tf_op jit(solution)/shard_map/ppermute | solution.py:147
  35.9 0.2 collective-permute-start.21
  36.1 0.7 %convolution_bitcast_fusion = f32[896,512]{0,1:T(8,128)S(1)} fusion(bf16[2,256,512]{2,1,0:T(8,128)(2,1)S(1)} %copy-done, bf16[2,1024,256]{2,1,0:T(8,128)(2,1)S(1)} %bitcast.87), kind=kOutput, calls=%fused_computation.22 | convolution fusion | flops 469762048 | bytes 3276800 | tf_op jit(solution)/shard_map/gpj,gjq->pq/dot_general | solution.py:138
  36.8 2.8 %collective-permute-done.17 = f32[128,256]{0,1:T(8,128)S(1)} collective-permute-done((f32[128,256]{0,1:T(8,128)S(1)}, f32[128,256]{0,1:T(8,128)S(1)}, u32[]{:S(2)}, u32[]{:S(2)}) %collective-permute-start.17) | collective-permute-done | bytes 131104 | tf_op jit(solution)/shard_map/ppermute | solution.py:147
  39.6 1.6 %collective-permute-done.21 = f32[128,256]{0,1:T(8,128)S(1)} collective-permute-done((f32[128,256]{0,1:T(8,128)S(1)}, f32[128,256]{0,1:T(8,128)S(1)}, u32[]{:S(2)}, u32[]{:S(2)}) %collective-permute-start.21) | collective-permute-done | bytes 131104 | tf_op jit(solution)/shard_map/ppermute | solution.py:148
  41.2 0.3 collective-permute-start.22
  41.6 1.8 %collective-permute-start.18 = (f32[128,512]{0,1:T(8,128)S(1)}, f32[128,512]{0,1:T(8,128)S(1)}, u32[]{:S(2)}, u32[]{:S(2)}) collective-permute-start(f32[128,512]{0,1:T(8,128)S(1)} %pad_maximum_fusion), channel_id=1, source_target_pairs={{0,4},{4,8},{8,12},{12,14},{14,10},{10,6},{6,2},{2,0},{1,5},{5,9},... | collective-permute-start | bytes 786440 | tf_op jit(solution)/shard_map/ppermute | solution.py:154
  43.4 5.1 %collective-permute-done.22 = f32[128,512]{0,1:T(8,128)S(1)} collective-permute-done((f32[128,512]{0,1:T(8,128)S(1)}, f32[128,512]{0,1:T(8,128)S(1)}, u32[]{:S(2)}, u32[]{:S(2)}) %collective-permute-start.22) | collective-permute-done | bytes 262176 | tf_op jit(solution)/shard_map/ppermute | solution.py:155
  48.5 0.2 collective-permute-done.18
  48.8 1.6 %collective-permute-start.19 = (f32[128,512]{0,1:T(8,128)S(1)}, f32[128,512]{0,1:T(8,128)S(1)}, u32[]{:S(2)}, u32[]{:S(2)}) collective-permute-start(f32[128,512]{0,1:T(8,128)S(1)} %get-tuple-element.9), channel_id=1, source_target_pairs={{0,4},{4,8},{8,12},{12,14},{14,10},{10,6},{6,2},{2,0},{1,5},{5,9},... | collective-permute-start | bytes 786440 | tf_op jit(solution)/shard_map/ppermute | solution.py:154
  50.5 0.5 collective-permute-start.23
  50.9 4.3 %collective-permute-done.19 = f32[128,512]{0,1:T(8,128)S(1)} collective-permute-done((f32[128,512]{0,1:T(8,128)S(1)}, f32[128,512]{0,1:T(8,128)S(1)}, u32[]{:S(2)}, u32[]{:S(2)}) %collective-permute-start.19) | collective-permute-done | bytes 262176 | tf_op jit(solution)/shard_map/ppermute | solution.py:154
  55.3 1.6 %collective-permute-done.23 = f32[128,512]{0,1:T(8,128)S(1)} collective-permute-done((f32[128,512]{0,1:T(8,128)S(1)}, f32[128,512]{0,1:T(8,128)S(1)}, u32[]{:S(2)}, u32[]{:S(2)}) %collective-permute-start.23) | collective-permute-done | bytes 262176 | tf_op jit(solution)/shard_map/ppermute | solution.py:155
  56.9 1.6 %collective-permute-start.20 = (f32[128,512]{0,1:T(8,128)S(1)}, f32[128,512]{0,1:T(8,128)S(1)}, u32[]{:S(2)}, u32[]{:S(2)}) collective-permute-start(f32[128,512]{0,1:T(8,128)S(1)} %get-tuple-element.7), channel_id=1, source_target_pairs={{0,4},{4,8},{8,12},{12,14},{14,10},{10,6},{6,2},{2,0},{1,5},{5,9},... | collective-permute-start | bytes 786440 | tf_op jit(solution)/shard_map/ppermute | solution.py:158
  58.5 0.5 collective-permute-start.24
  59.0 4.3 %collective-permute-done.20 = f32[128,512]{0,1:T(8,128)S(1)} collective-permute-done((f32[128,512]{0,1:T(8,128)S(1)}, f32[128,512]{0,1:T(8,128)S(1)}, u32[]{:S(2)}, u32[]{:S(2)}) %collective-permute-start.20) | collective-permute-done | bytes 262176 | tf_op jit(solution)/shard_map/ppermute | solution.py:158
  63.3 1.5 %collective-permute-done.24 = f32[128,512]{0,1:T(8,128)S(1)} collective-permute-done((f32[128,512]{0,1:T(8,128)S(1)}, f32[128,512]{0,1:T(8,128)S(1)}, u32[]{:S(2)}, u32[]{:S(2)}) %collective-permute-start.24) | collective-permute-done | bytes 262176 | tf_op jit(solution)/shard_map/ppermute | solution.py:159
  64.9 0.8 %copy.28 = f32[128,512]{1,0:T(8,128)} copy(f32[128,512]{0,1:T(8,128)S(1)} %fusion.39) | data formatting | bytes 524288 | tf_op jit(solution)/shard_map/add | solution.py:157
  (42 shorter events, 0.8 us)
Async XLA Ops:
  0.0 33.6 %copy-start = (bf16[2,256,512]{2,1,0:T(8,128)(2,1)S(1)}, bf16[2,256,512]{2,1,0:T(8,128)(2,1)}, u32[]{:S(2)}) copy-start(bf16[2,256,512]{2,1,0:T(8,128)(2,1)} %param.10) | copy-start | bytes 1572868
  0.0 6.7 %collective-permute-start = (bf16[64,1024]{1,0:T(8,128)(2,1)}, bf16[64,1024]{1,0:T(8,128)(2,1)S(1)}, u32[]{:S(2)}, u32[]{:S(2)}) collective-permute-start(bf16[64,1024]{1,0:T(8,128)(2,1)} %param.8), channel_id=1, source_target_pairs={{0,4},{4,8},{8,12},{12,14},{14,10},{10,6},{6,2},{2,0},{1,5},{5,9},... | collective-permute-start | bytes 393224 | tf_op jit(solution)/shard_map/ppermute | solution.py:46
  3.1 6.8 %collective-permute-start.8 = (bf16[64,1024]{1,0:T(8,128)(2,1)}, bf16[64,1024]{1,0:T(8,128)(2,1)S(1)}, u32[]{:S(2)}, u32[]{:S(2)}) collective-permute-start(bf16[64,1024]{1,0:T(8,128)(2,1)} %param.8), channel_id=1, source_target_pairs={{0,2},{4,0},{8,4},{12,8},{14,12},{10,14},{6,10},{2,6},{1,3},{5,1},... | collective-permute-start | bytes 393224 | tf_op jit(solution)/shard_map/ppermute | solution.py:50
  3.1 7.4 %collective-permute-start.14 = (bf16[64,1024]{1,0:T(8,128)(2,1)}, bf16[64,1024]{1,0:T(8,128)(2,1)S(1)}, u32[]{:S(2)}, u32[]{:S(2)}) collective-permute-start(bf16[64,1024]{1,0:T(8,128)(2,1)} %param.8), channel_id=1, source_target_pairs={{0,1},{1,0},{2,3},{3,2},{4,5},{5,4},{6,7},{7,6},{8,9},{9,8},{10,11... | collective-permute-start | bytes 393224 | tf_op jit(solution)/shard_map/ppermute | solution.py:53
  6.7 5.0 %collective-permute-start.2 = (bf16[64,1024]{1,0:T(8,128)(2,1)S(1)}, bf16[64,1024]{1,0:T(8,128)(2,1)S(1)}, u32[]{:S(2)}, u32[]{:S(2)}) collective-permute-start(bf16[64,1024]{1,0:T(8,128)(2,1)S(1)} %collective-permute-done), channel_id=1, source_target_pairs={{0,4},{4,8},{8,12},{12,14},{14,10},{10,6},{6,2},{2,0},{1,5},{5,9},... | collective-permute-start | bytes 393224 | tf_op jit(solution)/shard_map/ppermute | solution.py:46
  8.5 5.0 %collective-permute-start.1 = (bf16[64,1024]{1,0:T(8,128)(2,1)S(1)}, bf16[64,1024]{1,0:T(8,128)(2,1)S(1)}, u32[]{:S(2)}, u32[]{:S(2)}) collective-permute-start(bf16[64,1024]{1,0:T(8,128)(2,1)S(1)} %collective-permute-done), channel_id=1, source_target_pairs={{0,1},{1,0},{2,3},{3,2},{4,5},{5,4},{6,7},{7,6},{8,9},{9,8},{10,11... | collective-permute-start | bytes 393224 | tf_op jit(solution)/shard_map/ppermute | solution.py:53
  9.8 5.9 %collective-permute-start.9 = (bf16[64,1024]{1,0:T(8,128)(2,1)S(1)}, bf16[64,1024]{1,0:T(8,128)(2,1)S(1)}, u32[]{:S(2)}, u32[]{:S(2)}) collective-permute-start(bf16[64,1024]{1,0:T(8,128)(2,1)S(1)} %collective-permute-done.8), channel_id=1, source_target_pairs={{0,2},{4,0},{8,4},{12,8},{14,12},{10,14},{6,10},{2,6},{1,3},{5,1},... | collective-permute-start | bytes 393224 | tf_op jit(solution)/shard_map/ppermute | solution.py:50
  10.1 6.0 %collective-permute-start.13 = (bf16[64,1024]{1,0:T(8,128)(2,1)S(1)}, bf16[64,1024]{1,0:T(8,128)(2,1)S(1)}, u32[]{:S(2)}, u32[]{:S(2)}) collective-permute-start(bf16[64,1024]{1,0:T(8,128)(2,1)S(1)} %collective-permute-done.8), channel_id=1, source_target_pairs={{0,1},{1,0},{2,3},{3,2},{4,5},{5,4},{6,7},{7,6},{8,9},{9,8},{10,11... | collective-permute-start | bytes 393224 | tf_op jit(solution)/shard_map/ppermute | solution.py:53
  11.6 5.4 %collective-permute-start.4 = (bf16[64,1024]{1,0:T(8,128)(2,1)S(1)}, bf16[64,1024]{1,0:T(8,128)(2,1)S(1)}, u32[]{:S(2)}, u32[]{:S(2)}) collective-permute-start(bf16[64,1024]{1,0:T(8,128)(2,1)S(1)} %collective-permute-done.2), channel_id=1, source_target_pairs={{0,4},{4,8},{8,12},{12,14},{14,10},{10,6},{6,2},{2,0},{1,5},{5,9},... | collective-permute-start | bytes 393224 | tf_op jit(solution)/shard_map/ppermute | solution.py:46
  13.5 5.4 %collective-permute-start.3 = (bf16[64,1024]{1,0:T(8,128)(2,1)S(1)}, bf16[64,1024]{1,0:T(8,128)(2,1)S(1)}, u32[]{:S(2)}, u32[]{:S(2)}) collective-permute-start(bf16[64,1024]{1,0:T(8,128)(2,1)S(1)} %collective-permute-done.2), channel_id=1, source_target_pairs={{0,1},{1,0},{2,3},{3,2},{4,5},{5,4},{6,7},{7,6},{8,9},{9,8},{10,11... | collective-permute-start | bytes 393224 | tf_op jit(solution)/shard_map/ppermute | solution.py:53
  15.8 5.1 %collective-permute-start.10 = (bf16[64,1024]{1,0:T(8,128)(2,1)S(1)}, bf16[64,1024]{1,0:T(8,128)(2,1)S(1)}, u32[]{:S(2)}, u32[]{:S(2)}) collective-permute-start(bf16[64,1024]{1,0:T(8,128)(2,1)S(1)} %collective-permute-done.9), channel_id=1, source_target_pairs={{0,2},{4,0},{8,4},{12,8},{14,12},{10,14},{6,10},{2,6},{1,3},{5,1},... | collective-permute-start | bytes 393224 | tf_op jit(solution)/shard_map/ppermute | solution.py:50
  16.1 4.8 %collective-permute-start.12 = (bf16[64,1024]{1,0:T(8,128)(2,1)S(1)}, bf16[64,1024]{1,0:T(8,128)(2,1)S(1)}, u32[]{:S(2)}, u32[]{:S(2)}) collective-permute-start(bf16[64,1024]{1,0:T(8,128)(2,1)S(1)} %collective-permute-done.9), channel_id=1, source_target_pairs={{0,1},{1,0},{2,3},{3,2},{4,5},{5,4},{6,7},{7,6},{8,9},{9,8},{10,11... | collective-permute-start | bytes 393224 | tf_op jit(solution)/shard_map/ppermute | solution.py:53
  17.1 5.0 %collective-permute-start.6 = (bf16[64,1024]{1,0:T(8,128)(2,1)S(1)}, bf16[64,1024]{1,0:T(8,128)(2,1)S(1)}, u32[]{:S(2)}, u32[]{:S(2)}) collective-permute-start(bf16[64,1024]{1,0:T(8,128)(2,1)S(1)} %collective-permute-done.4), channel_id=1, source_target_pairs={{0,4},{4,8},{8,12},{12,14},{14,10},{10,6},{6,2},{2,0},{1,5},{5,9},... | collective-permute-start | bytes 393224 | tf_op jit(solution)/shard_map/ppermute | solution.py:46
  18.9 3.2 %collective-permute-start.5 = (bf16[64,1024]{1,0:T(8,128)(2,1)S(1)}, bf16[64,1024]{1,0:T(8,128)(2,1)S(1)}, u32[]{:S(2)}, u32[]{:S(2)}) collective-permute-start(bf16[64,1024]{1,0:T(8,128)(2,1)S(1)} %collective-permute-done.4), channel_id=1, source_target_pairs={{0,1},{1,0},{2,3},{3,2},{4,5},{5,4},{6,7},{7,6},{8,9},{9,8},{10,11... | collective-permute-start | bytes 393224 | tf_op jit(solution)/shard_map/ppermute | solution.py:53
  20.8 1.3 %collective-permute-start.11 = (bf16[64,1024]{1,0:T(8,128)(2,1)S(1)}, bf16[64,1024]{1,0:T(8,128)(2,1)S(1)}, u32[]{:S(2)}, u32[]{:S(2)}) collective-permute-start(bf16[64,1024]{1,0:T(8,128)(2,1)S(1)} %collective-permute-done.10), channel_id=1, source_target_pairs={{0,1},{1,0},{2,3},{3,2},{4,5},{5,4},{6,7},{7,6},{8,9},{9,8},{10,11... | collective-permute-start | bytes 393224 | tf_op jit(solution)/shard_map/ppermute | solution.py:53
  22.1 1.3 %collective-permute-start.7 = (bf16[64,1024]{1,0:T(8,128)(2,1)S(1)}, bf16[64,1024]{1,0:T(8,128)(2,1)S(1)}, u32[]{:S(2)}, u32[]{:S(2)}) collective-permute-start(bf16[64,1024]{1,0:T(8,128)(2,1)S(1)} %collective-permute-done.6), channel_id=1, source_target_pairs={{0,1},{1,0},{2,3},{3,2},{4,5},{5,4},{6,7},{7,6},{8,9},{9,8},{10,11... | collective-permute-start | bytes 393224 | tf_op jit(solution)/shard_map/ppermute | solution.py:53
  23.4 1.6 %copy-start.1 = (bf16[2,1024,512]{2,1,0:T(8,128)(2,1)S(1)}, bf16[2,1024,512]{2,1,0:T(8,128)(2,1)}, u32[]{:S(2)}) copy-start(bf16[2,1024,512]{2,1,0:T(8,128)(2,1)} %param.7) | copy-start | bytes 6291460
  27.6 4.5 %collective-permute-start.15 = (bf16[1024,512]{1,0:T(8,128)(2,1)S(1)}, bf16[1024,512]{1,0:T(8,128)(2,1)S(1)}, u32[]{:S(2)}, u32[]{:S(2)}) collective-permute-start(bf16[1024,512]{1,0:T(8,128)(2,1)S(1)} %convolution_convert_fusion.1), channel_id=1, source_target_pairs={{0,1},{1,0},{2,3},{3,2},{4,5},{5,4},{6,7},{7,6},{8,9},{9,8},{10,11... | collective-permute-start | bytes 3145736 | tf_op jit(solution)/shard_map/ppermute | solution.py:81
  27.8 4.3 %collective-permute-start.16 = (bf16[1024,512]{1,0:T(8,128)(2,1)S(1)}, bf16[1024,512]{1,0:T(8,128)(2,1)S(1)}, u32[]{:S(2)}, u32[]{:S(2)}) collective-permute-start(bf16[1024,512]{1,0:T(8,128)(2,1)S(1)} %convolution_convert_fusion), channel_id=1, source_target_pairs={{0,1},{1,0},{2,3},{3,2},{4,5},{5,4},{6,7},{7,6},{8,9},{9,8},{10,11... | collective-permute-start | bytes 3145736 | tf_op jit(solution)/shard_map/ppermute | solution.py:81
  34.0 5.6 %collective-permute-start.17 = (f32[128,256]{0,1:T(8,128)S(1)}, f32[128,256]{0,1:T(8,128)S(1)}, u32[]{:S(2)}, u32[]{:S(2)}) collective-permute-start(f32[128,256]{0,1:T(8,128)S(1)} %get-tuple-element.15), channel_id=1, source_target_pairs={{0,4},{4,8},{8,12},{12,14},{14,10},{10,6},{6,2},{2,0},{1,5},{5,9},... | collective-permute-start | bytes 393224 | tf_op jit(solution)/shard_map/ppermute | solution.py:147
  35.9 5.3 %collective-permute-start.21 = (f32[128,256]{0,1:T(8,128)S(1)}, f32[128,256]{0,1:T(8,128)S(1)}, u32[]{:S(2)}, u32[]{:S(2)}) collective-permute-start(f32[128,256]{0,1:T(8,128)S(1)} %get-tuple-element.16), channel_id=1, source_target_pairs={{0,2},{4,0},{8,4},{12,8},{14,12},{10,14},{6,10},{2,6},{1,3},{5,1},... | collective-permute-start | bytes 393224 | tf_op jit(solution)/shard_map/ppermute | solution.py:148
  41.2 7.3 %collective-permute-start.22 = (f32[128,512]{0,1:T(8,128)S(1)}, f32[128,512]{0,1:T(8,128)S(1)}, u32[]{:S(2)}, u32[]{:S(2)}) collective-permute-start(f32[128,512]{0,1:T(8,128)S(1)} %pad_maximum_fusion.1), channel_id=1, source_target_pairs={{0,2},{4,0},{8,4},{12,8},{14,12},{10,14},{6,10},{2,6},{1,3},{5,1},... | collective-permute-start | bytes 786440 | tf_op jit(solution)/shard_map/ppermute | solution.py:155
  41.6 7.2 %collective-permute-start.18 = (f32[128,512]{0,1:T(8,128)S(1)}, f32[128,512]{0,1:T(8,128)S(1)}, u32[]{:S(2)}, u32[]{:S(2)}) collective-permute-start(f32[128,512]{0,1:T(8,128)S(1)} %pad_maximum_fusion), channel_id=1, source_target_pairs={{0,4},{4,8},{8,12},{12,14},{14,10},{10,6},{6,2},{2,0},{1,5},{5,9},... | collective-permute-start | bytes 786440 | tf_op jit(solution)/shard_map/ppermute | solution.py:154
  48.8 6.4 %collective-permute-start.19 = (f32[128,512]{0,1:T(8,128)S(1)}, f32[128,512]{0,1:T(8,128)S(1)}, u32[]{:S(2)}, u32[]{:S(2)}) collective-permute-start(f32[128,512]{0,1:T(8,128)S(1)} %get-tuple-element.9), channel_id=1, source_target_pairs={{0,4},{4,8},{8,12},{12,14},{14,10},{10,6},{6,2},{2,0},{1,5},{5,9},... | collective-permute-start | bytes 786440 | tf_op jit(solution)/shard_map/ppermute | solution.py:154
  50.5 6.4 %collective-permute-start.23 = (f32[128,512]{0,1:T(8,128)S(1)}, f32[128,512]{0,1:T(8,128)S(1)}, u32[]{:S(2)}, u32[]{:S(2)}) collective-permute-start(f32[128,512]{0,1:T(8,128)S(1)} %get-tuple-element.10), channel_id=1, source_target_pairs={{0,2},{4,0},{8,4},{12,8},{14,12},{10,14},{6,10},{2,6},{1,3},{5,1},... | collective-permute-start | bytes 786440 | tf_op jit(solution)/shard_map/ppermute | solution.py:155
  56.9 6.4 %collective-permute-start.20 = (f32[128,512]{0,1:T(8,128)S(1)}, f32[128,512]{0,1:T(8,128)S(1)}, u32[]{:S(2)}, u32[]{:S(2)}) collective-permute-start(f32[128,512]{0,1:T(8,128)S(1)} %get-tuple-element.7), channel_id=1, source_target_pairs={{0,4},{4,8},{8,12},{12,14},{14,10},{10,6},{6,2},{2,0},{1,5},{5,9},... | collective-permute-start | bytes 786440 | tf_op jit(solution)/shard_map/ppermute | solution.py:158
  58.5 6.4 %collective-permute-start.24 = (f32[128,512]{0,1:T(8,128)S(1)}, f32[128,512]{0,1:T(8,128)S(1)}, u32[]{:S(2)}, u32[]{:S(2)}) collective-permute-start(f32[128,512]{0,1:T(8,128)S(1)} %get-tuple-element.8), channel_id=1, source_target_pairs={{0,2},{4,0},{8,4},{12,8},{14,12},{10,14},{6,10},{2,6},{1,3},{5,1},... | collective-permute-start | bytes 786440 | tf_op jit(solution)/shard_map/ppermute | solution.py:159
